TPU v7x, 512 devices: a whole 4x8x8 slice. The times are simulated.
512 devices in a mesh: gx: 32 (over x, y), gy: 16 (over z, core).
Axes of the slice: x: 4, y: 8, z: 8, core: 2. Of those that a mesh axis runs over, the one named last changes fastest.
Arguments:
- test_block: float32 [32, 8, 512, 2048], P(None, None, 'gx', 'gy'), may hold values from -1500 to 1500, as said below
- kappa_sq: float32 [8, 512, 2048], P(None, 'gx', 'gy'), may hold values from 0.05 to 2
Outputs:
- basis: float32 [32, 8, 512, 2048], P(None, None, 'gx', 'gy')
Inputs may be any that keep to these rules, and one draw needn't show every extreme that they name: `test_block`: real-valued entries.
All inputs are finite; a program needn't handle non-finite values.
Results may differ from a plain program's by a relative error of at most 0.0003.
Values sent between devices are 32-bit elements; how exact they have to be, the bound alone decides.
No kernel may reach another device: no remote copies, remote signals or barrier semaphores. Data moves between devices by JAX's collectives and lax.ppermute only.
A program may use at most 64 MiB of HBM per device.

v0:
```python
import math

import jax
import jax.numpy as jnp
from jax import lax
from jax.sharding import PartitionSpec as P


def extended(block, sides, width):
    for axis, dim in sides:
        count = lax.axis_size(axis)
        forward = [(i, i + 1) for i in range(count - 1)]
        backward = [(target, source) for source, target in forward]
        low = lax.ppermute(
            lax.slice_in_dim(block, block.shape[dim] - width, None, axis=dim), axis, forward
        )
        high = lax.ppermute(lax.slice_in_dim(block, 0, width, axis=dim), axis, backward)
        block = jnp.concatenate([low, block, high], axis=dim)
    return block


def stencil(padded, coefficient):
    center = padded[:, :, 1:-1, 1:-1]
    neighbours = padded[:, :, 2:, 1:-1] + padded[:, :, :-2, 1:-1]
    neighbours = neighbours + padded[:, :, 1:-1, 2:] + padded[:, :, 1:-1, :-2]
    z_padded = jnp.pad(center, ((0, 0), (1, 1), (0, 0), (0, 0)))
    neighbours = neighbours + z_padded[:, 2:] + z_padded[:, :-2]
    return (6.0 + coefficient) * center - neighbours


def lower_solve(factor, block):
    return lax.linalg.triangular_solve(factor, block, left_side=True, lower=True)


def apply_once(field_in, kappa_sq):
    padded = extended(field_in, (("gx", 2), ("gy", 3)), 1)
    return stencil(padded, kappa_sq)


def merge_factors(stacked):
    summed = jnp.einsum("nij,nkj->ik", stacked, stacked, precision=lax.Precision.HIGHEST)
    return jnp.linalg.cholesky(summed)


def merged_factor(gram_matrix):
    stacked = lax.all_gather(gram_matrix[None], "gx", axis=0, tiled=True)
    column_factor = jnp.linalg.cholesky(jnp.sum(stacked, axis=0))
    stacked_columns = lax.all_gather(column_factor[None], "gy", axis=0, tiled=True)
    return merge_factors(stacked_columns)


def body(test_block, kappa_sq):
    cols_here, depth_here, x_cells, y_cells = test_block.shape
    sample = apply_once(apply_once(test_block, kappa_sq), kappa_sq)
    flattened = sample.reshape(cols_here, -1)
    gram_one = jnp.dot(flattened, flattened.T, precision=lax.Precision.HIGHEST)
    factor_one = merged_factor(gram_one)
    partial_value = lower_solve(factor_one, flattened)
    gram_two = jnp.dot(partial_value, partial_value.T, precision=lax.Precision.HIGHEST)
    factor_two = merged_factor(gram_two)
    scale_factor = math.sqrt(flattened.shape[1] * lax.axis_size("gx") * lax.axis_size("gy"))
    result = lower_solve(factor_two, partial_value) * scale_factor
    return result.reshape(cols_here, depth_here, x_cells, y_cells)


def solution(mesh):
    in_specs = (P(None, None, "gx", "gy"), P(None, "gx", "gy"))
    out_specs = P(None, None, "gx", "gy")
    return jax.shard_map(body, mesh=mesh, in_specs=in_specs, out_specs=out_specs, check_vma=False)
```

profile of v0, /device:TPU:1, one launch (start us, length us, event | category | flops | bytes accessed | tf_op | source)
XLA Modules:
  0.0 260.5 jit_solution(14732550015322631781)
XLA Ops:
  0.0 2.6 %copy.82 = f32[32,8,16,128]{3,1,2,0:T(8,128)S(1)} copy(f32[32,8,16,128]{3,2,1,0:T(8,128)} %param.5) | data formatting | bytes 4194304 | tf_op args[0]
  2.6 1.3 copy-done.1
  4.0 4.0 %collective-permute-start.1 = (f32[32,8,1,128]{3,1,2,0:T(8,128)S(1)}, f32[32,8,1,128]{3,1,2,0:T(8,128)S(1)}, u32[]{:S(2)}, u32[]{:S(2)}) collective-permute-start(f32[32,8,1,128]{3,1,2,0:T(8,128)S(1)} %get-tuple-element.13), channel_id=1, source_target_pairs={{0,16},{16,32},{32,48},{48,64},{64,80},{80,96},{96,112},{112,128},... | collective-permute-start | bytes 393224 | tf_op jit(solution)/shard_map/ppermute | solution.py:14
  8.0 1.3 collective-permute-start
  9.3 4.5 %copy.88 = f32[32,8,16,128]{0,1,3,2:T(8,128)} copy(f32[32,8,16,128]{3,2,1,0:T(8,128)S(1)} %copy-done.2) | data formatting | bytes 4194304 | tf_op args[0]
  14.4 3.9 %pad_maximum_fusion = f32[32,8,18,128]{0,1,3,2:T(8,128)S(1)} fusion(f32[32,8,1,128]{0,1,3,2:T(8,128)S(1)} %copy.89, f32[32,8,16,128]{0,1,3,2:T(8,128)} %copy.88, f32[32,8,1,128]{0,1,3,2:T(8,128)S(1)} %copy.87), kind=kLoop, calls=%fused_computation.1 | loop fusion | flops 1179648 | bytes 4718592 | tf_op jit(solution)/shard_map/concatenate | solution.py:18
  18.4 3.6 %copy-done = f32[32,8,18,128]{0,1,3,2:T(8,128)} copy-done((f32[32,8,18,128]{0,1,3,2:T(8,128)}, f32[32,8,18,128]{0,1,3,2:T(8,128)S(1)}, u32[]{:S(2)}) %copy-start) | copy-done | bytes 2359320
  22.0 6.8 %collective-permute-start.2 = (f32[32,8,18,1]{0,1,3,2:T(8,128)S(1)}, f32[32,8,18,1]{0,1,3,2:T(8,128)S(1)}, u32[]{:S(2)}, u32[]{:S(2)}) collective-permute-start(f32[32,8,18,1]{0,1,3,2:T(8,128)S(1)} %get-tuple-element.6), channel_id=1, source_target_pairs={{1,0},{2,1},{3,2},{4,3},{5,4},{6,5},{7,6},{8,7},{9,8},{10,9},{11,1... | collective-permute-start | bytes 55304 | tf_op jit(solution)/shard_map/ppermute | solution.py:17
  28.7 1.9 collective-permute-start.3
  30.7 7.9 %copy.90 = f32[32,8,18,128]{3,1,2,0:T(8,128)} copy(f32[32,8,18,128]{0,1,3,2:T(8,128)} %copy-done) | data formatting | bytes 4718592 | tf_op jit(solution)/shard_map/concatenate | solution.py:18
  38.7 2.3 copy.91
  41.0 2.3 copy.92
  43.3 8.0 %fusion.2 = f32[32,8,16,128]{3,1,2,0:T(8,128)S(1)} fusion(f32[32,8,16,128]{3,1,2,0:T(8,128)} %copy-done.1, f32[32,8,18,128]{3,1,2,0:T(8,128)} %copy.90, f32[32,8,18,1]{3,1,2,0:T(8,128)} %copy.92, f32[32,8,18,1]{3,1,2,0:T(8,128)} %copy.91, f32[32,8,1,128]{3,1,2,0:T(8,128)S(1)} %collective-permute-done.1, f32[32,8,1,128]{3,1,2,0:T(8,128)S(1)} %collective-permute-done, ...), kind=kLoop, calls=%fused_computation.9 | loop fusion | flops 5767168 | bytes 6918144 | tf_op jit(solution)/shard_map/sub | solution.py:28
  51.4 1.3 collective-permute-start.4
  52.7 4.2 %collective-permute-start.5 = (f32[32,8,1,128]{3,1,2,0:T(8,128)S(1)}, f32[32,8,1,128]{3,1,2,0:T(8,128)S(1)}, u32[]{:S(2)}, u32[]{:S(2)}) collective-permute-start(f32[32,8,1,128]{3,1,2,0:T(8,128)S(1)} %get-tuple-element.11), channel_id=1, source_target_pairs={{0,16},{16,32},{32,48},{48,64},{64,80},{80,96},{96,112},{112,128},... | collective-permute-start | bytes 393224 | tf_op jit(solution)/shard_map/ppermute | solution.py:14
  56.8 1.3 collective-permute-done.4
  58.2 0.9 collective-permute-done.5
  59.2 2.9 %fusion.38 = (f32[32,8,18,1]{3,1,2,0:T(8,128)}, f32[32,8,18,1]{3,1,2,0:T(8,128)}) fusion(f32[32,8,18,128]{3,1,2,0:T(8,128)S(1)} %pad_maximum_fusion.1), kind=kLoop, calls=%fused_computation.71 | loop fusion | bytes 73728 | tf_op jit(solution)/shard_map/slice | solution.py:17
  62.1 2.6 copy.107
  64.7 3.4 %collective-permute-start.6 = (f32[32,8,18,1]{0,1,3,2:T(8,128)S(1)}, f32[32,8,18,1]{0,1,3,2:T(8,128)S(1)}, u32[]{:S(2)}, u32[]{:S(2)}) collective-permute-start(f32[32,8,18,1]{0,1,3,2:T(8,128)S(1)} %copy.107), channel_id=1, source_target_pairs={{1,0},{2,1},{3,2},{4,3},{5,4},{6,5},{7,6},{8,7},{9,8},{10,9},{11,1... | collective-permute-start | bytes 55304 | tf_op jit(solution)/shard_map/ppermute | solution.py:17
  68.1 2.6 copy.108
  70.7 2.4 collective-permute-start.7
  73.0 2.3 copy.96
  75.4 2.3 copy.98
  77.7 4.0 %fusion.5 = f32[32,8,16,128]{3,1,2,0:T(8,128)S(1)} fusion(f32[32,8,16,128]{3,1,2,0:T(8,128)S(1)} %fusion.2, f32[32,8,18,1]{3,1,2,0:T(8,128)} %copy.98, f32[32,8,1,128]{3,1,2,0:T(8,128)S(1)} %collective-permute-done.4, f32[32,8,1,128]{3,1,2,0:T(8,128)S(1)} %collective-permute-done.5, f32[32,8,18,1]{3,1,2,0:T(8,128)} %copy.96, f32[8,16,128]{2,0,1:T(8,128)S(1)} %copy.81), kind=kLoop, calls=%fused_computation.12 | loop fusion | flops 7864320 | bytes 4558848 | tf_op jit(solution)/shard_map/sub | solution.py:28
  81.8 2.8 %fusion.18 = f32[32,32]{1,0:T(8,128)S(1)} fusion(f32[32,8,16,128]{3,1,2,0:T(8,128)S(1)} %fusion.5), kind=kOutput, calls=%fused_computation.37 | convolution fusion | flops 201326592 | bytes 2101248 | tf_op jit(solution)/shard_map/dot_general | solution.py:56
  84.6 1.7 copy.103
  86.3 43.5 %all-gather = f32[1024,32]{1,0:T(8,128)S(1)} all-gather(f32[32,32]{1,0:T(8,128)S(1)} %fusion.18), channel_id=2, replica_groups=mesh['gx'=32,'gy'=16] {'gx'}, dimensions={0}, use_global_device_ids=true | all-gather | bytes 135168 | tf_op jit(solution)/shard_map/all_gather | solution.py:46
  130.0 2.9 %cholesky.74 = f32[32,32]{1,0:T(8,128)S(1)} custom-call(f32[32,32]{1,0:T(8,128)S(1)} %fusion.28), custom_call_target="Cholesky" | custom-call | tf_op jit(solution)/shard_map/jit(cholesky)/cholesky | solution.py:47
  132.9 0.7 compare_reduce_fusion.3
  133.6 0.7 fusion.30
  134.3 35.5 %all-gather.1 = f32[512,32]{1,0:T(8,128)S(1)} all-gather(f32[32,32]{1,0:T(8,128)S(1)} %fusion.30), channel_id=3, replica_groups=mesh['gx'=32,'gy'=16] {'gy'}, dimensions={0}, use_global_device_ids=true | all-gather | bytes 69632 | tf_op jit(solution)/shard_map/all_gather | solution.py:48
  170.2 2.9 %cholesky.85 = f32[32,32]{1,0:T(8,128)S(1)} custom-call(f32[32,32]{1,0:T(8,128)S(1)} %fusion.27), custom_call_target="Cholesky" | custom-call | tf_op jit(solution)/shard_map/jit(cholesky)/cholesky | solution.py:42
  173.2 0.7 compare_reduce_fusion.2
  173.9 0.7 fusion.21
  174.6 2.4 custom-call.6
  177.0 4.6 %fusion.6 = f32[32,16384]{1,0:T(8,128)S(1)} fusion(f32[4,8,128,128]{3,2,1,0:T(8,128)} %bitcast.54, f32[1,32,32]{1,2,0:T(8,128)S(1)} %custom-call.6), kind=kOutput, calls=%fused_computation.13 | convolution fusion | flops 201326592 | bytes 4198400 | tf_op jit(solution)/shard_map/triangular_solve/dot.1 | solution.py:32
  181.6 1.8 fusion.41
  183.4 35.5 %all-gather.2 = f32[1024,32]{1,0:T(8,128)S(1)} all-gather(f32[32,32]{1,0:T(8,128)S(1)} %fusion.41), channel_id=4, replica_groups=mesh['gx'=32,'gy'=16] {'gx'}, dimensions={0}, use_global_device_ids=true | all-gather | bytes 135168 | tf_op jit(solution)/shard_map/all_gather | solution.py:46
  219.1 2.9 %cholesky.96 = f32[32,32]{1,0:T(8,128)S(1)} custom-call(f32[32,32]{1,0:T(8,128)S(1)} %fusion.25), custom_call_target="Cholesky" | custom-call | tf_op jit(solution)/shard_map/jit(cholesky)/cholesky | solution.py:47
  222.7 0.6 fusion.29
  223.3 26.4 %all-gather.3 = f32[512,32]{1,0:T(8,128)S(1)} all-gather(f32[32,32]{1,0:T(8,128)S(1)} %fusion.29), channel_id=5, replica_groups=mesh['gx'=32,'gy'=16] {'gy'}, dimensions={0}, use_global_device_ids=true | all-gather | bytes 69632 | tf_op jit(solution)/shard_map/all_gather | solution.py:48
  250.2 2.9 %cholesky.107 = f32[32,32]{1,0:T(8,128)S(1)} custom-call(f32[32,32]{1,0:T(8,128)S(1)} %fusion.24), custom_call_target="Cholesky" | custom-call | tf_op jit(solution)/shard_map/jit(cholesky)/cholesky | solution.py:42
  253.1 0.6 compare_reduce_fusion
  253.8 0.7 fusion.22
  254.4 2.4 custom-call.7
  256.9 2.0 fusion.17
  258.8 1.7 copy.110
  (37 shorter events, 2.7 us)
Async XLA Ops:
  0.0 9.3 %copy-start.2 = (f32[32,8,16,128]{3,2,1,0:T(8,128)S(1)}, f32[32,8,16,128]{3,2,1,0:T(8,128)}, u32[]{:S(2)}) copy-start(f32[32,8,16,128]{3,2,1,0:T(8,128)} %param.5) | copy-start | bytes 6291460
  2.6 1.3 copy-start.1
  4.0 9.9 %collective-permute-start.1 = (f32[32,8,1,128]{3,1,2,0:T(8,128)S(1)}, f32[32,8,1,128]{3,1,2,0:T(8,128)S(1)}, u32[]{:S(2)}, u32[]{:S(2)}) collective-permute-start(f32[32,8,1,128]{3,1,2,0:T(8,128)S(1)} %get-tuple-element.13), channel_id=1, source_target_pairs={{0,16},{16,32},{32,48},{48,64},{64,80},{80,96},{96,112},{112,128},... | collective-permute-start | bytes 393224 | tf_op jit(solution)/shard_map/ppermute | solution.py:14
  8.0 6.1 %collective-permute-start = (f32[32,8,1,128]{3,1,2,0:T(8,128)S(1)}, f32[32,8,1,128]{3,1,2,0:T(8,128)S(1)}, u32[]{:S(2)}, u32[]{:S(2)}) collective-permute-start(f32[32,8,1,128]{3,1,2,0:T(8,128)S(1)} %get-tuple-element.14), channel_id=1, source_target_pairs={{16,0},{32,16},{48,32},{64,48},{80,64},{96,80},{112,96},{128,112},... | collective-permute-start | bytes 393224 | tf_op jit(solution)/shard_map/ppermute | solution.py:17
  14.4 16.3 %copy-start.3 = (f32[8,16,128]{2,1,0:T(8,128)S(1)}, f32[8,16,128]{2,1,0:T(8,128)}, u32[]{:S(2)}) copy-start(f32[8,16,128]{2,1,0:T(8,128)} %param.6) | copy-start | bytes 196612
  18.3 3.6 %copy-start = (f32[32,8,18,128]{0,1,3,2:T(8,128)}, f32[32,8,18,128]{0,1,3,2:T(8,128)S(1)}, u32[]{:S(2)}) copy-start(f32[32,8,18,128]{0,1,3,2:T(8,128)S(1)} %pad_maximum_fusion) | copy-start | bytes 7077892
  22.0 16.7 %collective-permute-start.2 = (f32[32,8,18,1]{0,1,3,2:T(8,128)S(1)}, f32[32,8,18,1]{0,1,3,2:T(8,128)S(1)}, u32[]{:S(2)}, u32[]{:S(2)}) collective-permute-start(f32[32,8,18,1]{0,1,3,2:T(8,128)S(1)} %get-tuple-element.6), channel_id=1, source_target_pairs={{1,0},{2,1},{3,2},{4,3},{5,4},{6,5},{7,6},{8,7},{9,8},{10,9},{11,1... | collective-permute-start | bytes 55304 | tf_op jit(solution)/shard_map/ppermute | solution.py:17
  28.7 12.3 %collective-permute-start.3 = (f32[32,8,18,1]{0,1,3,2:T(8,128)S(1)}, f32[32,8,18,1]{0,1,3,2:T(8,128)S(1)}, u32[]{:S(2)}, u32[]{:S(2)}) collective-permute-start(f32[32,8,18,1]{0,1,3,2:T(8,128)S(1)} %get-tuple-element.8), channel_id=1, source_target_pairs={{0,1},{1,2},{2,3},{3,4},{4,5},{5,6},{6,7},{7,8},{8,9},{9,10},{10,1... | collective-permute-start | bytes 55304 | tf_op jit(solution)/shard_map/ppermute | solution.py:14
  51.4 6.8 %collective-permute-start.4 = (f32[32,8,1,128]{3,1,2,0:T(8,128)S(1)}, f32[32,8,1,128]{3,1,2,0:T(8,128)S(1)}, u32[]{:S(2)}, u32[]{:S(2)}) collective-permute-start(f32[32,8,1,128]{3,1,2,0:T(8,128)S(1)} %get-tuple-element.12), channel_id=1, source_target_pairs={{16,0},{32,16},{48,32},{64,48},{80,64},{96,80},{112,96},{128,112},... | collective-permute-start | bytes 393224 | tf_op jit(solution)/shard_map/ppermute | solution.py:17
  52.7 6.4 %collective-permute-start.5 = (f32[32,8,1,128]{3,1,2,0:T(8,128)S(1)}, f32[32,8,1,128]{3,1,2,0:T(8,128)S(1)}, u32[]{:S(2)}, u32[]{:S(2)}) collective-permute-start(f32[32,8,1,128]{3,1,2,0:T(8,128)S(1)} %get-tuple-element.11), channel_id=1, source_target_pairs={{0,16},{16,32},{32,48},{48,64},{64,80},{80,96},{96,112},{112,128},... | collective-permute-start | bytes 393224 | tf_op jit(solution)/shard_map/ppermute | solution.py:14
  64.7 8.3 %collective-permute-start.6 = (f32[32,8,18,1]{0,1,3,2:T(8,128)S(1)}, f32[32,8,18,1]{0,1,3,2:T(8,128)S(1)}, u32[]{:S(2)}, u32[]{:S(2)}) collective-permute-start(f32[32,8,18,1]{0,1,3,2:T(8,128)S(1)} %copy.107), channel_id=1, source_target_pairs={{1,0},{2,1},{3,2},{4,3},{5,4},{6,5},{7,6},{8,7},{9,8},{10,9},{11,1... | collective-permute-start | bytes 55304 | tf_op jit(solution)/shard_map/ppermute | solution.py:17
  70.7 4.7 %collective-permute-start.7 = (f32[32,8,18,1]{0,1,3,2:T(8,128)S(1)}, f32[32,8,18,1]{0,1,3,2:T(8,128)S(1)}, u32[]{:S(2)}, u32[]{:S(2)}) collective-permute-start(f32[32,8,18,1]{0,1,3,2:T(8,128)S(1)} %copy.108), channel_id=1, source_target_pairs={{0,1},{1,2},{2,3},{3,4},{4,5},{5,6},{6,7},{7,8},{8,9},{9,10},{10,1... | collective-permute-start | bytes 55304 | tf_op jit(solution)/shard_map/ppermute | solution.py:14
where the time goes:
time: 261 us
  blocking collectives  141 us (54%)
  local copies, waits for them, and re-layouts  41.7 us (16%)
  other arithmetic  38.4 us (15%)
  starting transfers between devices  25.2 us (10%)
  matrix products  11.8 us (5%)
    all_gather x2, blocking collectives, merged_factor(): stacked = lax.all_gather(gram_matrix[None], 'gx', axis=0, tiled=True)  79 us
    all_gather x2, blocking collectives, merged_factor(): lax.all_gather(column_factor[None], 'gy', axis=0, tiled=True)  61.9 us
    unnamed x13, local copies, waits for them, and re-layouts  19 us
    ppermute x4, starting transfers between devices, extended(): lax.ppermute(lax.slice_in_dim(block, 0, width, axis=dim), axis, backward)  12.7 us
    ppermute x4, starting transfers between devices, extended(): lax.ppermute(lax.slice_in_dim(block, block.shape[dim] - width, None, axis...  12.5 us
    sub x2, other arithmetic, stencil(): return (6.0 + coefficient) * center - neighbours  12 us
    concatenate x1, local copies, waits for them, and re-layouts, extended(): block = jnp.concatenate([low, block, high], axis=dim)  7.95 us
    another operation x6, other arithmetic, merged_factor(): column_factor = jnp.linalg.cholesky(jnp.sum(stacked, axis=0))  7.27 us
  transfers between devices with their start and end apart: 8, of which 2 were waited for; matrix products, arithmetic and copies ran while one was open for 8% of the time, Pallas kernels for 0%

commit v1 on v0

v1 whole, which is shorter than its diff:
```python
import math

import jax
import jax.numpy as jnp
from jax import lax
from jax.sharding import PartitionSpec as P

HIGHEST = lax.Precision.HIGHEST


def shifted_in(lower_part, upper_part, axis):
    count = lax.axis_size(axis)
    forward = [(i, i + 1) for i in range(count - 1)]
    backward = [(i + 1, i) for i in range(count - 1)]
    from_below = lax.ppermute(lower_part, axis, forward)
    from_above = lax.ppermute(upper_part, axis, backward)
    return from_below, from_above


def extend(block, width):
    below, above = shifted_in(block[:, :, -width:, :], block[:, :, :width, :], "gx")
    block = jnp.concatenate([below, block, above], axis=2)
    left, right = shifted_in(block[..., -width:], block[..., :width], "gy")
    return jnp.concatenate([left, block, right], axis=3)


def stencil(padded, coefficient):
    center = padded[:, :, 1:-1, 1:-1]
    neighbours = padded[:, :, 2:, 1:-1] + padded[:, :, :-2, 1:-1]
    neighbours = neighbours + padded[:, :, 1:-1, 2:] + padded[:, :, 1:-1, :-2]
    z_padded = jnp.pad(center, ((0, 0), (1, 1), (0, 0), (0, 0)))
    neighbours = neighbours + z_padded[:, 2:] + z_padded[:, :-2]
    return (6.0 + coefficient) * center - neighbours


def inside_mask(x_cells, y_cells):
    ix, iy = lax.axis_index("gx"), lax.axis_index("gy")
    nx, ny = lax.axis_size("gx"), lax.axis_size("gy")
    rows = lax.broadcasted_iota(jnp.int32, (x_cells + 2, y_cells + 2), 0)
    cols = lax.broadcasted_iota(jnp.int32, (x_cells + 2, y_cells + 2), 1)
    row_ok = ((rows > 0) | (ix > 0)) & ((rows < x_cells + 1) | (ix < nx - 1))
    col_ok = ((cols > 0) | (iy > 0)) & ((cols < y_cells + 1) | (iy < ny - 1))
    return row_ok & col_ok


def butterfly_sum(value):
    for axis in ("gy", "gx"):
        count = lax.axis_size(axis)
        step = 1
        while step < count:
            pairs = [(i, i ^ step) for i in range(count)]
            value = value + lax.ppermute(value, axis, pairs)
            step *= 2
    return value


def gram(block):
    return jnp.einsum("czxy,dzxy->cd", block, block, precision=HIGHEST)


def inverse_factor(gram_matrix):
    factor = jnp.linalg.cholesky(gram_matrix)
    eye = jnp.eye(factor.shape[0], dtype=factor.dtype)
    return lax.linalg.triangular_solve(factor, eye, left_side=True, lower=True)


def body(test_block, kappa_sq):
    cols_here, depth_here, x_cells, y_cells = test_block.shape
    joined = jnp.concatenate([test_block, kappa_sq[None]], axis=0)
    padded = extend(joined, 2)
    field_ext, kappa_ext = padded[:cols_here], padded[cols_here]
    once = stencil(field_ext, kappa_ext[None, :, 1:-1, 1:-1])
    once = jnp.where(inside_mask(x_cells, y_cells), once, 0.0)
    sample = stencil(once, kappa_sq)
    inverse_one = inverse_factor(butterfly_sum(gram(sample)))
    partial_value = jnp.einsum("cd,dzxy->czxy", inverse_one, sample, precision=HIGHEST)
    inverse_two = inverse_factor(butterfly_sum(gram(partial_value)))
    cells = depth_here * x_cells * y_cells * lax.axis_size("gx") * lax.axis_size("gy")
    result = jnp.einsum("cd,dzxy->czxy", inverse_two, partial_value, precision=HIGHEST)
    return result * math.sqrt(cells)


def solution(mesh):
    in_specs = (P(None, None, "gx", "gy"), P(None, "gx", "gy"))
    out_specs = P(None, None, "gx", "gy")
    return jax.shard_map(body, mesh=mesh, in_specs=in_specs, out_specs=out_specs, check_vma=False)
```

time: 261 us -> 215 us (0.82)
  the two profiles are of different devices: /device:TPU:1 before, /device:TPU:24 now
where the time goes in v1:
time: 215 us; the launch traced here: 214 us
  starting transfers between devices  83.9 us (39%)
  waiting for transfers between devices  60.9 us (28%)
  other arithmetic  29.8 us (14%)
  local copies, waits for them, and re-layouts  27.4 us (13%)
  matrix products  11.5 us (5%)
    ppermute x18, starting transfers between devices, butterfly_sum(): value = value + lax.ppermute(value, axis, pairs)  74.7 us
    ppermute x18, waiting for transfers between devices, butterfly_sum(): value = value + lax.ppermute(value, axis, pairs)  51.3 us
    slice x3, local copies, waits for them, and re-layouts, extend(): left, right = shifted_in(block[..., -width:], block[..., :width], 'gy')  10 us
    another operation x6, other arithmetic, inverse_factor(): factor = jnp.linalg.cholesky(gram_matrix)  7.21 us
    select_n x1, other arithmetic, body(): once = jnp.where(inside_mask(x_cells, y_cells), once, 0.0)  7.04 us
    concatenate x1, other arithmetic, extend(): return jnp.concatenate([left, block, right], axis=3)  6.97 us
    another operation x4, other arithmetic, inverse_factor(): return lax.linalg.triangular_solve(factor, eye, left_side=True, lower=True)  6.16 us
    ppermute x2, starting transfers between devices, shifted_in(): from_below = lax.ppermute(lower_part, axis, forward)  5.99 us
  transfers between devices with their start and end apart: 22, of which 21 were waited for; matrix products, arithmetic and copies ran while one was open for 3% of the time, Pallas kernels for 0%

profile of v1, /device:TPU:24, one launch (start us, length us, event | category | flops | bytes accessed | tf_op | source)
XLA Modules:
  0.0 213.9 jit_solution(3777513770414002428)
XLA Ops:
  0.0 2.5 %copy.17 = f32[32,8,16,128]{3,1,2,0:T(8,128)S(1)} copy(f32[32,8,16,128]{3,2,1,0:T(8,128)} %param.5) | data formatting | bytes 4194304 | tf_op args[0]
  2.6 4.7 %collective-permute-start = (f32[33,8,2,128]{3,1,2,0:T(8,128)S(1)}, f32[33,8,2,128]{3,1,2,0:T(8,128)S(1)}, u32[]{:S(2)}, u32[]{:S(2)}) collective-permute-start(f32[33,8,2,128]{3,1,2,0:T(8,128)S(1)} %get-tuple-element.9), channel_id=1, source_target_pairs={{0,16},{16,32},{32,48},{48,64},{64,80},{80,96},{96,112},{112,128},... | collective-permute-start | bytes 811016 | tf_op jit(solution)/shard_map/ppermute | solution.py:15
  7.3 1.9 collective-permute-start.1
  9.3 3.7 %collective-permute-done = f32[33,8,2,128]{3,1,2,0:T(8,128)S(1)} collective-permute-done((f32[33,8,2,128]{3,1,2,0:T(8,128)S(1)}, f32[33,8,2,128]{3,1,2,0:T(8,128)S(1)}, u32[]{:S(2)}, u32[]{:S(2)}) %collective-permute-start) | collective-permute-done | bytes 270368 | tf_op jit(solution)/shard_map/ppermute | solution.py:15
  13.0 5.3 %collective-permute-done.1 = f32[33,8,2,128]{3,1,2,0:T(8,128)S(1)} collective-permute-done((f32[33,8,2,128]{3,1,2,0:T(8,128)S(1)}, f32[33,8,2,128]{3,1,2,0:T(8,128)S(1)}, u32[]{:S(2)}, u32[]{:S(2)}) %collective-permute-start.1) | collective-permute-done | bytes 270368 | tf_op jit(solution)/shard_map/ppermute | solution.py:16
  18.6 3.4 %fusion.31 = (f32[33,8,20,2]{3,1,2,0:T(8,128)}, f32[33,8,20,2]{3,1,2,0:T(8,128)}) fusion(f32[33,8,20,128]{3,1,2,0:T(8,128)S(1)} %pad_maximum_fusion.9), kind=kLoop, calls=%fused_computation.66 | loop fusion | bytes 168960 | tf_op jit(solution)/shard_map/slice | solution.py:23
  22.0 3.3 %copy.18 = f32[33,8,20,2]{0,1,3,2:T(8,128)S(1)} copy(f32[33,8,20,2]{3,1,2,0:T(8,128)} %get-tuple-element.6) | data formatting | bytes 84480 | tf_op jit(solution)/shard_map/slice | solution.py:23
  26.6 3.3 %copy.19 = f32[33,8,20,2]{0,1,3,2:T(8,128)S(1)} copy(f32[33,8,20,2]{3,1,2,0:T(8,128)} %get-tuple-element.8) | data formatting | bytes 84480 | tf_op jit(solution)/shard_map/slice | solution.py:23
  31.3 3.9 %copy.20 = f32[33,8,20,2]{3,1,2,0:T(8,128)} copy(f32[33,8,20,2]{0,1,3,2:T(8,128)S(1)} %collective-permute-done.2) | data formatting | bytes 84480 | tf_op jit(solution)/shard_map/ppermute | solution.py:15
  35.8 3.8 %copy.21 = f32[33,8,20,2]{3,1,2,0:T(8,128)} copy(f32[33,8,20,2]{0,1,3,2:T(8,128)S(1)} %collective-permute-done.3) | data formatting | bytes 84480 | tf_op jit(solution)/shard_map/ppermute | solution.py:16
  39.6 7.0 %pad_maximum_fusion = f32[33,8,20,132]{3,1,2,0:T(8,128)S(1)} fusion(f32[33,8,20,2]{3,1,2,0:T(8,128)} %copy.21, f32[33,8,2,128]{3,1,2,0:T(8,128)S(1)} %collective-permute-done.1, f32[1,8,16,128]{3,1,2,0:T(8,128)S(1)} %bitcast.44, f32[32,8,16,128]{3,1,2,0:T(8,128)S(1)} %copy.17, f32[33,8,2,128]{3,1,2,0:T(8,128)S(1)} %collective-permute-done, ...), kind=kLoop, calls=%fused_computation.2 | loop fusion | flops 3484800 | bytes 5575680 | tf_op jit(solution)/shard_map/concatenate | solution.py:24
  49.4 7.0 %fusion.3 = f32[32,8,18,130]{3,1,2,0:T(8,128)S(1)} fusion(f32[32,8,18,130]{3,1,2,0:T(8,128)S(1)} %slice.97, f32[33,8,20,2]{3,1,2,0:T(8,128)S(1)} %copy-done, f32[33,8,2,128]{3,1,2,0:T(8,128)S(1)} %collective-permute-done.1, f32[33,8,2,128]{3,1,2,0:T(8,128)S(1)} %collective-permute-done, f32[1,8,16,128]{3,1,2,0:T(8,128)S(1)} %bitcast.46, ...), kind=kLoop, calls=%fused_computation.8 | loop fusion | flops 9584640 | bytes 12449700 | tf_op jit(solution)/shard_map/jit(_where)/select_n | solution.py:73
  60.1 2.8 %fusion.15 = f32[32,32]{0,1:T(8,128)S(1)} fusion(f32[32,8,16,128]{3,1,2,0:T(8,128)S(1)} %fusion.8), kind=kOutput, calls=%fused_computation.34 | convolution fusion | flops 201326592 | bytes 2101248 | tf_op jit(solution)/shard_map/czxy,dzxy->cd/dot_general | solution.py:58
  62.9 5.8 %collective-permute-start.4 = (f32[32,32]{0,1:T(8,128)S(1)}, f32[32,32]{0,1:T(8,128)S(1)}, u32[]{:S(2)}, u32[]{:S(2)}) collective-permute-start(f32[32,32]{0,1:T(8,128)S(1)} %fusion.15), channel_id=1, source_target_pairs={{0,1},{1,0},{2,3},{3,2},{4,5},{5,4},{6,7},{7,6},{8,9},{9,8},{10,11... | collective-permute-start | bytes 12296 | tf_op jit(solution)/shard_map/ppermute | solution.py:52
  69.5 4.3 %collective-permute-start.5 = (f32[32,32]{0,1:T(8,128)S(1)}, f32[32,32]{0,1:T(8,128)S(1)}, u32[]{:S(2)}, u32[]{:S(2)}) collective-permute-start(f32[32,32]{0,1:T(8,128)S(1)} %add.123), channel_id=1, source_target_pairs={{0,2},{1,3},{2,0},{3,1},{4,6},{5,7},{6,4},{7,5},{8,10},{9,11},{10,... | collective-permute-start | bytes 12296 | tf_op jit(solution)/shard_map/ppermute | solution.py:52
  75.5 8.5 %collective-permute-start.6 = (f32[32,32]{0,1:T(8,128)S(1)}, f32[32,32]{0,1:T(8,128)S(1)}, u32[]{:S(2)}, u32[]{:S(2)}) collective-permute-start(f32[32,32]{0,1:T(8,128)S(1)} %add.124), channel_id=1, source_target_pairs={{0,4},{1,5},{2,6},{3,7},{4,0},{5,1},{6,2},{7,3},{8,12},{9,13},{10,... | collective-permute-start | bytes 12296 | tf_op jit(solution)/shard_map/ppermute | solution.py:52
  85.8 6.9 %collective-permute-start.7 = (f32[32,32]{0,1:T(8,128)S(1)}, f32[32,32]{0,1:T(8,128)S(1)}, u32[]{:S(2)}, u32[]{:S(2)}) collective-permute-start(f32[32,32]{0,1:T(8,128)S(1)} %add.125), channel_id=1, source_target_pairs={{0,8},{1,9},{2,10},{3,11},{4,12},{5,13},{6,14},{7,15},{8,0},{9,1},... | collective-permute-start | bytes 12296 | tf_op jit(solution)/shard_map/ppermute | solution.py:52
  92.8 2.6 %collective-permute-done.7 = f32[32,32]{0,1:T(8,128)S(1)} collective-permute-done((f32[32,32]{0,1:T(8,128)S(1)}, f32[32,32]{0,1:T(8,128)S(1)}, u32[]{:S(2)}, u32[]{:S(2)}) %collective-permute-start.7) | collective-permute-done | bytes 4128 | tf_op jit(solution)/shard_map/ppermute | solution.py:52
  95.4 1.9 collective-permute-start.8
  97.3 3.7 %collective-permute-done.8 = f32[32,32]{0,1:T(8,128)S(1)} collective-permute-done((f32[32,32]{0,1:T(8,128)S(1)}, f32[32,32]{0,1:T(8,128)S(1)}, u32[]{:S(2)}, u32[]{:S(2)}) %collective-permute-start.8) | collective-permute-done | bytes 4128 | tf_op jit(solution)/shard_map/ppermute | solution.py:52
  102.9 4.7 %collective-permute-done.9 = f32[32,32]{0,1:T(8,128)S(1)} collective-permute-done((f32[32,32]{0,1:T(8,128)S(1)}, f32[32,32]{0,1:T(8,128)S(1)}, u32[]{:S(2)}, u32[]{:S(2)}) %collective-permute-start.9) | collective-permute-done | bytes 4128 | tf_op jit(solution)/shard_map/ppermute | solution.py:52
  107.6 3.8 %collective-permute-start.10 = (f32[32,32]{0,1:T(8,128)S(1)}, f32[32,32]{0,1:T(8,128)S(1)}, u32[]{:S(2)}, u32[]{:S(2)}) collective-permute-start(f32[32,32]{0,1:T(8,128)S(1)} %add.128), channel_id=1, source_target_pairs={{0,64},{16,80},{32,96},{48,112},{64,0},{80,16},{96,32},{112,48},{1... | collective-permute-start | bytes 12296 | tf_op jit(solution)/shard_map/ppermute | solution.py:52
  111.4 5.7 %collective-permute-done.10 = f32[32,32]{0,1:T(8,128)S(1)} collective-permute-done((f32[32,32]{0,1:T(8,128)S(1)}, f32[32,32]{0,1:T(8,128)S(1)}, u32[]{:S(2)}, u32[]{:S(2)}) %collective-permute-start.10) | collective-permute-done | bytes 4128 | tf_op jit(solution)/shard_map/ppermute | solution.py:52
  117.1 3.4 %collective-permute-start.11 = (f32[32,32]{0,1:T(8,128)S(1)}, f32[32,32]{0,1:T(8,128)S(1)}, u32[]{:S(2)}, u32[]{:S(2)}) collective-permute-start(f32[32,32]{0,1:T(8,128)S(1)} %add.129), channel_id=1, source_target_pairs={{0,128},{16,144},{32,160},{48,176},{64,192},{80,208},{96,224},{112... | collective-permute-start | bytes 12296 | tf_op jit(solution)/shard_map/ppermute | solution.py:52
  120.5 2.2 %collective-permute-done.11 = f32[32,32]{0,1:T(8,128)S(1)} collective-permute-done((f32[32,32]{0,1:T(8,128)S(1)}, f32[32,32]{0,1:T(8,128)S(1)}, u32[]{:S(2)}, u32[]{:S(2)}) %collective-permute-start.11) | collective-permute-done | bytes 4128 | tf_op jit(solution)/shard_map/ppermute | solution.py:52
  122.7 5.1 %collective-permute-start.12 = (f32[32,32]{0,1:T(8,128)S(1)}, f32[32,32]{0,1:T(8,128)S(1)}, u32[]{:S(2)}, u32[]{:S(2)}) collective-permute-start(f32[32,32]{0,1:T(8,128)S(1)} %add.130), channel_id=1, source_target_pairs={{0,256},{16,272},{32,288},{48,304},{64,320},{80,336},{96,352},{112... | collective-permute-start | bytes 12296 | tf_op jit(solution)/shard_map/ppermute | solution.py:52
  127.8 2.0 collective-permute-done.12
  129.9 2.9 %cholesky.44 = f32[32,32]{1,0:T(8,128)S(1)} custom-call(f32[32,32]{1,0:T(8,128)S(1)} %fusion.28), custom_call_target="Cholesky" | custom-call | tf_op jit(solution)/shard_map/jit(cholesky)/cholesky | solution.py:62
  134.2 2.4 %custom-call.6 = f32[1,32,32]{1,2,0:T(8,128)S(1)} custom-call(f32[1,32,32]{2,1,0:T(8,128)S(1)} %fusion.23), custom_call_target="InvertDiagBlocksLowerTriangular" | custom-call | tf_op jit(solution)/shard_map/triangular_solve/custom-call.0 | solution.py:64
  136.9 4.5 %fusion.11 = f32[32,8,16,128]{3,0,2,1:T(8,128)S(1)} fusion(f32[32,32,1,1]{1,0,3,2:T(8,128)S(1)} %convolution_bitcast_fusion.1, f32[32,8,16,128]{3,1,2,0:T(8,128)} %copy-done.2), kind=kOutput, calls=%fused_computation.29 | convolution fusion | flops 201326592 | bytes 4198400 | tf_op jit(solution)/shard_map/cd,dzxy->czxy/dot_general | solution.py:76
  143.2 1.9 collective-permute-start.13
  146.3 3.7 %collective-permute-start.14 = (f32[32,32]{0,1:T(8,128)S(1)}, f32[32,32]{0,1:T(8,128)S(1)}, u32[]{:S(2)}, u32[]{:S(2)}) collective-permute-start(f32[32,32]{0,1:T(8,128)S(1)} %add.132), channel_id=1, source_target_pairs={{0,2},{1,3},{2,0},{3,1},{4,6},{5,7},{6,4},{7,5},{8,10},{9,11},{10,... | collective-permute-start | bytes 12296 | tf_op jit(solution)/shard_map/ppermute | solution.py:52
  151.9 4.8 %collective-permute-start.15 = (f32[32,32]{0,1:T(8,128)S(1)}, f32[32,32]{0,1:T(8,128)S(1)}, u32[]{:S(2)}, u32[]{:S(2)}) collective-permute-start(f32[32,32]{0,1:T(8,128)S(1)} %add.133), channel_id=1, source_target_pairs={{0,4},{1,5},{2,6},{3,7},{4,0},{5,1},{6,2},{7,3},{8,12},{9,13},{10,... | collective-permute-start | bytes 12296 | tf_op jit(solution)/shard_map/ppermute | solution.py:52
  158.4 6.9 %collective-permute-start.16 = (f32[32,32]{0,1:T(8,128)S(1)}, f32[32,32]{0,1:T(8,128)S(1)}, u32[]{:S(2)}, u32[]{:S(2)}) collective-permute-start(f32[32,32]{0,1:T(8,128)S(1)} %add.134), channel_id=1, source_target_pairs={{0,8},{1,9},{2,10},{3,11},{4,12},{5,13},{6,14},{7,15},{8,0},{9,1},... | collective-permute-start | bytes 12296 | tf_op jit(solution)/shard_map/ppermute | solution.py:52
  165.3 2.6 %collective-permute-done.16 = f32[32,32]{0,1:T(8,128)S(1)} collective-permute-done((f32[32,32]{0,1:T(8,128)S(1)}, f32[32,32]{0,1:T(8,128)S(1)}, u32[]{:S(2)}, u32[]{:S(2)}) %collective-permute-start.16) | collective-permute-done | bytes 4128 | tf_op jit(solution)/shard_map/ppermute | solution.py:52
  168.0 1.9 collective-permute-start.17
  169.9 3.7 %collective-permute-done.17 = f32[32,32]{0,1:T(8,128)S(1)} collective-permute-done((f32[32,32]{0,1:T(8,128)S(1)}, f32[32,32]{0,1:T(8,128)S(1)}, u32[]{:S(2)}, u32[]{:S(2)}) %collective-permute-start.17) | collective-permute-done | bytes 4128 | tf_op jit(solution)/shard_map/ppermute | solution.py:52
  175.5 4.6 %collective-permute-done.18 = f32[32,32]{0,1:T(8,128)S(1)} collective-permute-done((f32[32,32]{0,1:T(8,128)S(1)}, f32[32,32]{0,1:T(8,128)S(1)}, u32[]{:S(2)}, u32[]{:S(2)}) %collective-permute-start.18) | collective-permute-done | bytes 4128 | tf_op jit(solution)/shard_map/ppermute | solution.py:52
  180.1 3.8 %collective-permute-start.19 = (f32[32,32]{0,1:T(8,128)S(1)}, f32[32,32]{0,1:T(8,128)S(1)}, u32[]{:S(2)}, u32[]{:S(2)}) collective-permute-start(f32[32,32]{0,1:T(8,128)S(1)} %add.137), channel_id=1, source_target_pairs={{0,64},{16,80},{32,96},{48,112},{64,0},{80,16},{96,32},{112,48},{1... | collective-permute-start | bytes 12296 | tf_op jit(solution)/shard_map/ppermute | solution.py:52
  183.9 5.7 %collective-permute-done.19 = f32[32,32]{0,1:T(8,128)S(1)} collective-permute-done((f32[32,32]{0,1:T(8,128)S(1)}, f32[32,32]{0,1:T(8,128)S(1)}, u32[]{:S(2)}, u32[]{:S(2)}) %collective-permute-start.19) | collective-permute-done | bytes 4128 | tf_op jit(solution)/shard_map/ppermute | solution.py:52
  189.7 3.4 %collective-permute-start.20 = (f32[32,32]{0,1:T(8,128)S(1)}, f32[32,32]{0,1:T(8,128)S(1)}, u32[]{:S(2)}, u32[]{:S(2)}) collective-permute-start(f32[32,32]{0,1:T(8,128)S(1)} %add.138), channel_id=1, source_target_pairs={{0,128},{16,144},{32,160},{48,176},{64,192},{80,208},{96,224},{112... | collective-permute-start | bytes 12296 | tf_op jit(solution)/shard_map/ppermute | solution.py:52
  193.1 2.2 %collective-permute-done.20 = f32[32,32]{0,1:T(8,128)S(1)} collective-permute-done((f32[32,32]{0,1:T(8,128)S(1)}, f32[32,32]{0,1:T(8,128)S(1)}, u32[]{:S(2)}, u32[]{:S(2)}) %collective-permute-start.20) | collective-permute-done | bytes 4128 | tf_op jit(solution)/shard_map/ppermute | solution.py:52
  195.3 4.9 %collective-permute-start.21 = (f32[32,32]{0,1:T(8,128)S(1)}, f32[32,32]{0,1:T(8,128)S(1)}, u32[]{:S(2)}, u32[]{:S(2)}) collective-permute-start(f32[32,32]{0,1:T(8,128)S(1)} %add.139), channel_id=1, source_target_pairs={{0,256},{16,272},{32,288},{48,304},{64,320},{80,336},{96,352},{112... | collective-permute-start | bytes 12296 | tf_op jit(solution)/shard_map/ppermute | solution.py:52
  200.2 2.3 %collective-permute-done.21 = f32[32,32]{0,1:T(8,128)S(1)} collective-permute-done((f32[32,32]{0,1:T(8,128)S(1)}, f32[32,32]{0,1:T(8,128)S(1)}, u32[]{:S(2)}, u32[]{:S(2)}) %collective-permute-start.21) | collective-permute-done | bytes 4128 | tf_op jit(solution)/shard_map/ppermute | solution.py:52
  202.5 2.9 %cholesky.55 = f32[32,32]{1,0:T(8,128)S(1)} custom-call(f32[32,32]{1,0:T(8,128)S(1)} %fusion.26), custom_call_target="Cholesky" | custom-call | tf_op jit(solution)/shard_map/jit(cholesky)/cholesky | solution.py:62
  206.8 2.4 %custom-call.7 = f32[1,32,32]{1,2,0:T(8,128)S(1)} custom-call(f32[1,32,32]{2,1,0:T(8,128)S(1)} %fusion.24), custom_call_target="InvertDiagBlocksLowerTriangular" | custom-call | tf_op jit(solution)/shard_map/triangular_solve/custom-call.0 | solution.py:64
  209.4 1.9 convolution_multiply_fusion
  211.4 2.5 %copy.35 = f32[32,8,16,128]{3,2,1,0:T(8,128)} copy(f32[32,8,16,128]{3,0,2,1:T(8,128)S(1)} %convolution_multiply_fusion) | data formatting | bytes 4194304 | tf_op jit(solution)/shard_map/mul | solution.py:80
  (64 shorter events, 28.1 us)
Async XLA Ops:
  0.0 2.5 %copy-start.3 = (f32[8,16,128]{2,1,0:T(8,128)S(1)}, f32[8,16,128]{2,1,0:T(8,128)}, u32[]{:S(2)}) copy-start(f32[8,16,128]{2,1,0:T(8,128)} %param.6) | copy-start | bytes 196612
  2.6 10.4 %collective-permute-start = (f32[33,8,2,128]{3,1,2,0:T(8,128)S(1)}, f32[33,8,2,128]{3,1,2,0:T(8,128)S(1)}, u32[]{:S(2)}, u32[]{:S(2)}) collective-permute-start(f32[33,8,2,128]{3,1,2,0:T(8,128)S(1)} %get-tuple-element.9), channel_id=1, source_target_pairs={{0,16},{16,32},{32,48},{48,64},{64,80},{80,96},{96,112},{112,128},... | collective-permute-start | bytes 811016 | tf_op jit(solution)/shard_map/ppermute | solution.py:15
  7.3 11.0 %collective-permute-start.1 = (f32[33,8,2,128]{3,1,2,0:T(8,128)S(1)}, f32[33,8,2,128]{3,1,2,0:T(8,128)S(1)}, u32[]{:S(2)}, u32[]{:S(2)}) collective-permute-start(f32[33,8,2,128]{3,1,2,0:T(8,128)S(1)} %get-tuple-element.10), channel_id=1, source_target_pairs={{16,0},{32,16},{48,32},{64,48},{80,64},{96,80},{112,96},{128,112},... | collective-permute-start | bytes 811016 | tf_op jit(solution)/shard_map/ppermute | solution.py:16
  25.3 6.0 %collective-permute-start.2 = (f32[33,8,20,2]{0,1,3,2:T(8,128)S(1)}, f32[33,8,20,2]{0,1,3,2:T(8,128)S(1)}, u32[]{:S(2)}, u32[]{:S(2)}) collective-permute-start(f32[33,8,20,2]{0,1,3,2:T(8,128)S(1)} %copy.18), channel_id=1, source_target_pairs={{0,1},{1,2},{2,3},{3,4},{4,5},{5,6},{6,7},{7,8},{8,9},{9,10},{10,1... | collective-permute-start | bytes 126728 | tf_op jit(solution)/shard_map/ppermute | solution.py:15
  29.9 5.9 %collective-permute-start.3 = (f32[33,8,20,2]{0,1,3,2:T(8,128)S(1)}, f32[33,8,20,2]{0,1,3,2:T(8,128)S(1)}, u32[]{:S(2)}, u32[]{:S(2)}) collective-permute-start(f32[33,8,20,2]{0,1,3,2:T(8,128)S(1)} %copy.19), channel_id=1, source_target_pairs={{1,0},{2,1},{3,2},{4,3},{5,4},{6,5},{7,6},{8,7},{9,8},{10,9},{11,1... | collective-permute-start | bytes 126728 | tf_op jit(solution)/shard_map/ppermute | solution.py:16
  46.6 1.8 copy-start
  46.6 2.6 %copy-start.1 = (f32[33,8,20,2]{3,1,2,0:T(8,128)S(1)}, f32[33,8,20,2]{3,1,2,0:T(8,128)}, u32[]{:S(2)}) copy-start(f32[33,8,20,2]{3,1,2,0:T(8,128)} %copy.21) | copy-start | bytes 126724
  58.7 1.3 copy-start.2
  62.9 6.6 %collective-permute-start.4 = (f32[32,32]{0,1:T(8,128)S(1)}, f32[32,32]{0,1:T(8,128)S(1)}, u32[]{:S(2)}, u32[]{:S(2)}) collective-permute-start(f32[32,32]{0,1:T(8,128)S(1)} %fusion.15), channel_id=1, source_target_pairs={{0,1},{1,0},{2,3},{3,2},{4,5},{5,4},{6,7},{7,6},{8,9},{9,8},{10,11... | collective-permute-start | bytes 12296 | tf_op jit(solution)/shard_map/ppermute | solution.py:52
  69.5 6.0 %collective-permute-start.5 = (f32[32,32]{0,1:T(8,128)S(1)}, f32[32,32]{0,1:T(8,128)S(1)}, u32[]{:S(2)}, u32[]{:S(2)}) collective-permute-start(f32[32,32]{0,1:T(8,128)S(1)} %add.123), channel_id=1, source_target_pairs={{0,2},{1,3},{2,0},{3,1},{4,6},{5,7},{6,4},{7,5},{8,10},{9,11},{10,... | collective-permute-start | bytes 12296 | tf_op jit(solution)/shard_map/ppermute | solution.py:52
  75.5 10.3 %collective-permute-start.6 = (f32[32,32]{0,1:T(8,128)S(1)}, f32[32,32]{0,1:T(8,128)S(1)}, u32[]{:S(2)}, u32[]{:S(2)}) collective-permute-start(f32[32,32]{0,1:T(8,128)S(1)} %add.124), channel_id=1, source_target_pairs={{0,4},{1,5},{2,6},{3,7},{4,0},{5,1},{6,2},{7,3},{8,12},{9,13},{10,... | collective-permute-start | bytes 12296 | tf_op jit(solution)/shard_map/ppermute | solution.py:52
  85.8 9.5 %collective-permute-start.7 = (f32[32,32]{0,1:T(8,128)S(1)}, f32[32,32]{0,1:T(8,128)S(1)}, u32[]{:S(2)}, u32[]{:S(2)}) collective-permute-start(f32[32,32]{0,1:T(8,128)S(1)} %add.125), channel_id=1, source_target_pairs={{0,8},{1,9},{2,10},{3,11},{4,12},{5,13},{6,14},{7,15},{8,0},{9,1},... | collective-permute-start | bytes 12296 | tf_op jit(solution)/shard_map/ppermute | solution.py:52
  95.4 5.6 %collective-permute-start.8 = (f32[32,32]{0,1:T(8,128)S(1)}, f32[32,32]{0,1:T(8,128)S(1)}, u32[]{:S(2)}, u32[]{:S(2)}) collective-permute-start(f32[32,32]{0,1:T(8,128)S(1)} %add.126), channel_id=1, source_target_pairs={{0,16},{16,0},{32,48},{48,32},{64,80},{80,64},{96,112},{112,96},{1... | collective-permute-start | bytes 12296 | tf_op jit(solution)/shard_map/ppermute | solution.py:52
  101.0 6.6 %collective-permute-start.9 = (f32[32,32]{0,1:T(8,128)S(1)}, f32[32,32]{0,1:T(8,128)S(1)}, u32[]{:S(2)}, u32[]{:S(2)}) collective-permute-start(f32[32,32]{0,1:T(8,128)S(1)} %add.127), channel_id=1, source_target_pairs={{0,32},{16,48},{32,0},{48,16},{64,96},{80,112},{96,64},{112,80},{1... | collective-permute-start | bytes 12296 | tf_op jit(solution)/shard_map/ppermute | solution.py:52
  107.6 9.5 %collective-permute-start.10 = (f32[32,32]{0,1:T(8,128)S(1)}, f32[32,32]{0,1:T(8,128)S(1)}, u32[]{:S(2)}, u32[]{:S(2)}) collective-permute-start(f32[32,32]{0,1:T(8,128)S(1)} %add.128), channel_id=1, source_target_pairs={{0,64},{16,80},{32,96},{48,112},{64,0},{80,16},{96,32},{112,48},{1... | collective-permute-start | bytes 12296 | tf_op jit(solution)/shard_map/ppermute | solution.py:52
  117.1 5.6 %collective-permute-start.11 = (f32[32,32]{0,1:T(8,128)S(1)}, f32[32,32]{0,1:T(8,128)S(1)}, u32[]{:S(2)}, u32[]{:S(2)}) collective-permute-start(f32[32,32]{0,1:T(8,128)S(1)} %add.129), channel_id=1, source_target_pairs={{0,128},{16,144},{32,160},{48,176},{64,192},{80,208},{96,224},{112... | collective-permute-start | bytes 12296 | tf_op jit(solution)/shard_map/ppermute | solution.py:52
  122.7 7.1 %collective-permute-start.12 = (f32[32,32]{0,1:T(8,128)S(1)}, f32[32,32]{0,1:T(8,128)S(1)}, u32[]{:S(2)}, u32[]{:S(2)}) collective-permute-start(f32[32,32]{0,1:T(8,128)S(1)} %add.130), channel_id=1, source_target_pairs={{0,256},{16,272},{32,288},{48,304},{64,320},{80,336},{96,352},{112... | collective-permute-start | bytes 12296 | tf_op jit(solution)/shard_map/ppermute | solution.py:52
  143.2 3.1 %collective-permute-start.13 = (f32[32,32]{0,1:T(8,128)S(1)}, f32[32,32]{0,1:T(8,128)S(1)}, u32[]{:S(2)}, u32[]{:S(2)}) collective-permute-start(f32[32,32]{0,1:T(8,128)S(1)} %fusion.18), channel_id=1, source_target_pairs={{0,1},{1,0},{2,3},{3,2},{4,5},{5,4},{6,7},{7,6},{8,9},{9,8},{10,11... | collective-permute-start | bytes 12296 | tf_op jit(solution)/shard_map/ppermute | solution.py:52
  146.3 5.6 %collective-permute-start.14 = (f32[32,32]{0,1:T(8,128)S(1)}, f32[32,32]{0,1:T(8,128)S(1)}, u32[]{:S(2)}, u32[]{:S(2)}) collective-permute-start(f32[32,32]{0,1:T(8,128)S(1)} %add.132), channel_id=1, source_target_pairs={{0,2},{1,3},{2,0},{3,1},{4,6},{5,7},{6,4},{7,5},{8,10},{9,11},{10,... | collective-permute-start | bytes 12296 | tf_op jit(solution)/shard_map/ppermute | solution.py:52
  151.9 6.5 %collective-permute-start.15 = (f32[32,32]{0,1:T(8,128)S(1)}, f32[32,32]{0,1:T(8,128)S(1)}, u32[]{:S(2)}, u32[]{:S(2)}) collective-permute-start(f32[32,32]{0,1:T(8,128)S(1)} %add.133), channel_id=1, source_target_pairs={{0,4},{1,5},{2,6},{3,7},{4,0},{5,1},{6,2},{7,3},{8,12},{9,13},{10,... | collective-permute-start | bytes 12296 | tf_op jit(solution)/shard_map/ppermute | solution.py:52
  158.4 9.5 %collective-permute-start.16 = (f32[32,32]{0,1:T(8,128)S(1)}, f32[32,32]{0,1:T(8,128)S(1)}, u32[]{:S(2)}, u32[]{:S(2)}) collective-permute-start(f32[32,32]{0,1:T(8,128)S(1)} %add.134), channel_id=1, source_target_pairs={{0,8},{1,9},{2,10},{3,11},{4,12},{5,13},{6,14},{7,15},{8,0},{9,1},... | collective-permute-start | bytes 12296 | tf_op jit(solution)/shard_map/ppermute | solution.py:52
  168.0 5.6 %collective-permute-start.17 = (f32[32,32]{0,1:T(8,128)S(1)}, f32[32,32]{0,1:T(8,128)S(1)}, u32[]{:S(2)}, u32[]{:S(2)}) collective-permute-start(f32[32,32]{0,1:T(8,128)S(1)} %add.135), channel_id=1, source_target_pairs={{0,16},{16,0},{32,48},{48,32},{64,80},{80,64},{96,112},{112,96},{1... | collective-permute-start | bytes 12296 | tf_op jit(solution)/shard_map/ppermute | solution.py:52
  173.6 6.5 %collective-permute-start.18 = (f32[32,32]{0,1:T(8,128)S(1)}, f32[32,32]{0,1:T(8,128)S(1)}, u32[]{:S(2)}, u32[]{:S(2)}) collective-permute-start(f32[32,32]{0,1:T(8,128)S(1)} %add.136), channel_id=1, source_target_pairs={{0,32},{16,48},{32,0},{48,16},{64,96},{80,112},{96,64},{112,80},{1... | collective-permute-start | bytes 12296 | tf_op jit(solution)/shard_map/ppermute | solution.py:52
  180.1 9.5 %collective-permute-start.19 = (f32[32,32]{0,1:T(8,128)S(1)}, f32[32,32]{0,1:T(8,128)S(1)}, u32[]{:S(2)}, u32[]{:S(2)}) collective-permute-start(f32[32,32]{0,1:T(8,128)S(1)} %add.137), channel_id=1, source_target_pairs={{0,64},{16,80},{32,96},{48,112},{64,0},{80,16},{96,32},{112,48},{1... | collective-permute-start | bytes 12296 | tf_op jit(solution)/shard_map/ppermute | solution.py:52
  189.7 5.6 %collective-permute-start.20 = (f32[32,32]{0,1:T(8,128)S(1)}, f32[32,32]{0,1:T(8,128)S(1)}, u32[]{:S(2)}, u32[]{:S(2)}) collective-permute-start(f32[32,32]{0,1:T(8,128)S(1)} %add.138), channel_id=1, source_target_pairs={{0,128},{16,144},{32,160},{48,176},{64,192},{80,208},{96,224},{112... | collective-permute-start | bytes 12296 | tf_op jit(solution)/shard_map/ppermute | solution.py:52
  195.3 7.1 %collective-permute-start.21 = (f32[32,32]{0,1:T(8,128)S(1)}, f32[32,32]{0,1:T(8,128)S(1)}, u32[]{:S(2)}, u32[]{:S(2)}) collective-permute-start(f32[32,32]{0,1:T(8,128)S(1)} %add.139), channel_id=1, source_target_pairs={{0,256},{16,272},{32,288},{48,304},{64,320},{80,336},{96,352},{112... | collective-permute-start | bytes 12296 | tf_op jit(solution)/shard_map/ppermute | solution.py:52

commit v2 on v1

--- a/solution.py
+++ b/solution.py
@@ -44,13 +44,13 @@
 
 
 def butterfly_sum(value):
-    for axis in ("gy", "gx"):
-        count = lax.axis_size(axis)
-        step = 1
-        while step < count:
-            pairs = [(i, i ^ step) for i in range(count)]
-            value = value + lax.ppermute(value, axis, pairs)
-            step *= 2
+    value = jnp.sum(lax.all_gather(value, "gy"), axis=0)
+    count = lax.axis_size("gx")
+    step = 1
+    while step < count:
+        pairs = [(i, i ^ step) for i in range(count)]
+        value = value + lax.ppermute(value, "gx", pairs)
+        step *= 2
     return value
 
 

time: 215 us -> 199 us (0.926)
  the two profiles are of different devices: /device:TPU:24 before, /device:TPU:28 now
where the time goes in v2:
time: 199 us; the launch traced here: 198 us
  waiting for transfers between devices  52.6 us (26%)
  blocking collectives  41.1 us (21%)
  starting transfers between devices  35.1 us (18%)
  other arithmetic  29.8 us (15%)
  local copies, waits for them, and re-layouts  27.5 us (14%)
  matrix products  11.5 us (6%)
    ppermute x10, waiting for transfers between devices, butterfly_sum(): value = value + lax.ppermute(value, 'gx', pairs)  42.9 us
    all_gather x2, blocking collectives, butterfly_sum(): value = jnp.sum(lax.all_gather(value, 'gy'), axis=0)  41.1 us
    ppermute x10, starting transfers between devices, butterfly_sum(): value = value + lax.ppermute(value, 'gx', pairs)  25.9 us
    slice x3, local copies, waits for them, and re-layouts, extend(): left, right = shifted_in(block[..., -width:], block[..., :width], 'gy')  9.96 us
    another operation x6, other arithmetic, inverse_factor(): factor = jnp.linalg.cholesky(gram_matrix)  7.25 us
    select_n x1, other arithmetic, body(): once = jnp.where(inside_mask(x_cells, y_cells), once, 0.0)  7.04 us
    concatenate x1, other arithmetic, extend(): return jnp.concatenate([left, block, right], axis=3)  6.97 us
    another operation x4, other arithmetic, inverse_factor(): return lax.linalg.triangular_solve(factor, eye, left_side=True, lower=True)  6.16 us
  transfers between devices with their start and end apart: 14, of which 13 were waited for; matrix products, arithmetic and copies ran while one was open for 4% of the time, Pallas kernels for 0%

profile of v2, /device:TPU:28, one launch (start us, length us, event | category | flops | bytes accessed | tf_op | source)
XLA Modules:
  0.0 197.9 jit_solution(16554090063555305462)
XLA Ops:
  0.0 2.5 %copy.13 = f32[32,8,16,128]{3,1,2,0:T(8,128)S(1)} copy(f32[32,8,16,128]{3,2,1,0:T(8,128)} %param.5) | data formatting | bytes 4194304 | tf_op args[0]
  2.6 4.7 %collective-permute-start = (f32[33,8,2,128]{3,1,2,0:T(8,128)S(1)}, f32[33,8,2,128]{3,1,2,0:T(8,128)S(1)}, u32[]{:S(2)}, u32[]{:S(2)}) collective-permute-start(f32[33,8,2,128]{3,1,2,0:T(8,128)S(1)} %get-tuple-element.9), channel_id=1, source_target_pairs={{0,16},{16,32},{32,48},{48,64},{64,80},{80,96},{96,112},{112,128},... | collective-permute-start | bytes 811016 | tf_op jit(solution)/shard_map/ppermute | solution.py:15
  7.3 1.9 collective-permute-start.1
  9.3 3.7 %collective-permute-done = f32[33,8,2,128]{3,1,2,0:T(8,128)S(1)} collective-permute-done((f32[33,8,2,128]{3,1,2,0:T(8,128)S(1)}, f32[33,8,2,128]{3,1,2,0:T(8,128)S(1)}, u32[]{:S(2)}, u32[]{:S(2)}) %collective-permute-start) | collective-permute-done | bytes 270368 | tf_op jit(solution)/shard_map/ppermute | solution.py:15
  13.0 5.3 %collective-permute-done.1 = f32[33,8,2,128]{3,1,2,0:T(8,128)S(1)} collective-permute-done((f32[33,8,2,128]{3,1,2,0:T(8,128)S(1)}, f32[33,8,2,128]{3,1,2,0:T(8,128)S(1)}, u32[]{:S(2)}, u32[]{:S(2)}) %collective-permute-start.1) | collective-permute-done | bytes 270368 | tf_op jit(solution)/shard_map/ppermute | solution.py:16
  18.6 3.3 %fusion.31 = (f32[33,8,20,2]{3,1,2,0:T(8,128)}, f32[33,8,20,2]{3,1,2,0:T(8,128)}) fusion(f32[33,8,20,128]{3,1,2,0:T(8,128)S(1)} %pad_maximum_fusion.9), kind=kLoop, calls=%fused_computation.66 | loop fusion | bytes 168960 | tf_op jit(solution)/shard_map/slice | solution.py:23
  21.9 3.3 %copy.14 = f32[33,8,20,2]{0,1,3,2:T(8,128)S(1)} copy(f32[33,8,20,2]{3,1,2,0:T(8,128)} %get-tuple-element.6) | data formatting | bytes 84480 | tf_op jit(solution)/shard_map/slice | solution.py:23
  25.2 1.3 collective-permute-start.2
  26.5 3.3 %copy.15 = f32[33,8,20,2]{0,1,3,2:T(8,128)S(1)} copy(f32[33,8,20,2]{3,1,2,0:T(8,128)} %get-tuple-element.8) | data formatting | bytes 84480 | tf_op jit(solution)/shard_map/slice | solution.py:23
  29.8 1.3 collective-permute-start.3
  31.3 3.8 %copy.16 = f32[33,8,20,2]{3,1,2,0:T(8,128)} copy(f32[33,8,20,2]{0,1,3,2:T(8,128)S(1)} %collective-permute-done.2) | data formatting | bytes 84480 | tf_op jit(solution)/shard_map/ppermute | solution.py:15
  35.7 3.8 %copy.17 = f32[33,8,20,2]{3,1,2,0:T(8,128)} copy(f32[33,8,20,2]{0,1,3,2:T(8,128)S(1)} %collective-permute-done.3) | data formatting | bytes 84480 | tf_op jit(solution)/shard_map/ppermute | solution.py:16
  39.6 7.0 %pad_maximum_fusion = f32[33,8,20,132]{3,1,2,0:T(8,128)S(1)} fusion(f32[33,8,20,2]{3,1,2,0:T(8,128)} %copy.17, f32[33,8,2,128]{3,1,2,0:T(8,128)S(1)} %collective-permute-done.1, f32[1,8,16,128]{3,1,2,0:T(8,128)S(1)} %bitcast.46, f32[32,8,16,128]{3,1,2,0:T(8,128)S(1)} %copy.13, f32[33,8,2,128]{3,1,2,0:T(8,128)S(1)} %collective-permute-done, ...), kind=kLoop, calls=%fused_computation.2 | loop fusion | flops 3484800 | bytes 5575680 | tf_op jit(solution)/shard_map/concatenate | solution.py:24
  46.6 1.3 slice.97
  49.4 7.0 %fusion.3 = f32[32,8,18,130]{3,1,2,0:T(8,128)S(1)} fusion(f32[32,8,18,130]{3,1,2,0:T(8,128)S(1)} %slice.97, f32[33,8,20,2]{3,1,2,0:T(8,128)S(1)} %copy-done, f32[33,8,2,128]{3,1,2,0:T(8,128)S(1)} %collective-permute-done.1, f32[33,8,2,128]{3,1,2,0:T(8,128)S(1)} %collective-permute-done, f32[1,8,16,128]{3,1,2,0:T(8,128)S(1)} %bitcast.48, ...), kind=kLoop, calls=%fused_computation.8 | loop fusion | flops 9584640 | bytes 12449700 | tf_op jit(solution)/shard_map/jit(_where)/select_n | solution.py:73
  57.0 1.7 fusion.8
  58.7 1.3 copy-done.2
  60.0 2.8 %fusion.15 = f32[32,32]{1,0:T(8,128)S(1)} fusion(f32[32,8,16,128]{3,1,2,0:T(8,128)S(1)} %fusion.8), kind=kOutput, calls=%fused_computation.34 | convolution fusion | flops 201326592 | bytes 2101248 | tf_op jit(solution)/shard_map/czxy,dzxy->cd/dot_general | solution.py:58
  62.9 26.2 %all-gather = f32[512,32]{1,0:T(8,128)S(1)} all-gather(f32[32,32]{1,0:T(8,128)S(1)} %fusion.15), channel_id=2, replica_groups=mesh['gx'=32,'gy'=16] {'gy'}, dimensions={0}, use_global_device_ids=true | all-gather | bytes 69632 | tf_op jit(solution)/shard_map/all_gather | solution.py:47
  89.2 1.9 collective-permute-start.4
  91.1 3.7 %collective-permute-done.4 = f32[32,32]{0,1:T(8,128)S(1)} collective-permute-done((f32[32,32]{0,1:T(8,128)S(1)}, f32[32,32]{0,1:T(8,128)S(1)}, u32[]{:S(2)}, u32[]{:S(2)}) %collective-permute-start.4) | collective-permute-done | bytes 4128 | tf_op jit(solution)/shard_map/ppermute | solution.py:52
  94.8 1.9 collective-permute-start.5
  96.7 4.6 %collective-permute-done.5 = f32[32,32]{0,1:T(8,128)S(1)} collective-permute-done((f32[32,32]{0,1:T(8,128)S(1)}, f32[32,32]{0,1:T(8,128)S(1)}, u32[]{:S(2)}, u32[]{:S(2)}) %collective-permute-start.5) | collective-permute-done | bytes 4128 | tf_op jit(solution)/shard_map/ppermute | solution.py:52
  101.3 3.5 %collective-permute-start.6 = (f32[32,32]{0,1:T(8,128)S(1)}, f32[32,32]{0,1:T(8,128)S(1)}, u32[]{:S(2)}, u32[]{:S(2)}) collective-permute-start(f32[32,32]{0,1:T(8,128)S(1)} %add.100), channel_id=1, source_target_pairs={{0,64},{16,80},{32,96},{48,112},{64,0},{80,16},{96,32},{112,48},{1... | collective-permute-start | bytes 12296 | tf_op jit(solution)/shard_map/ppermute | solution.py:52
  104.9 6.0 %collective-permute-done.6 = f32[32,32]{0,1:T(8,128)S(1)} collective-permute-done((f32[32,32]{0,1:T(8,128)S(1)}, f32[32,32]{0,1:T(8,128)S(1)}, u32[]{:S(2)}, u32[]{:S(2)}) %collective-permute-start.6) | collective-permute-done | bytes 4128 | tf_op jit(solution)/shard_map/ppermute | solution.py:52
  110.9 3.1 %collective-permute-start.7 = (f32[32,32]{0,1:T(8,128)S(1)}, f32[32,32]{0,1:T(8,128)S(1)}, u32[]{:S(2)}, u32[]{:S(2)}) collective-permute-start(f32[32,32]{0,1:T(8,128)S(1)} %add.101), channel_id=1, source_target_pairs={{0,128},{16,144},{32,160},{48,176},{64,192},{80,208},{96,224},{112... | collective-permute-start | bytes 12296 | tf_op jit(solution)/shard_map/ppermute | solution.py:52
  114.0 2.5 %collective-permute-done.7 = f32[32,32]{0,1:T(8,128)S(1)} collective-permute-done((f32[32,32]{0,1:T(8,128)S(1)}, f32[32,32]{0,1:T(8,128)S(1)}, u32[]{:S(2)}, u32[]{:S(2)}) %collective-permute-start.7) | collective-permute-done | bytes 4128 | tf_op jit(solution)/shard_map/ppermute | solution.py:52
  116.5 2.6 %collective-permute-start.8 = (f32[32,32]{0,1:T(8,128)S(1)}, f32[32,32]{0,1:T(8,128)S(1)}, u32[]{:S(2)}, u32[]{:S(2)}) collective-permute-start(f32[32,32]{0,1:T(8,128)S(1)} %add.102), channel_id=1, source_target_pairs={{0,256},{16,272},{32,288},{48,304},{64,320},{80,336},{96,352},{112... | collective-permute-start | bytes 12296 | tf_op jit(solution)/shard_map/ppermute | solution.py:52
  119.1 4.5 %collective-permute-done.8 = f32[32,32]{0,1:T(8,128)S(1)} collective-permute-done((f32[32,32]{0,1:T(8,128)S(1)}, f32[32,32]{0,1:T(8,128)S(1)}, u32[]{:S(2)}, u32[]{:S(2)}) %collective-permute-start.8) | collective-permute-done | bytes 4128 | tf_op jit(solution)/shard_map/ppermute | solution.py:52
  123.7 2.9 %cholesky.44 = f32[32,32]{1,0:T(8,128)S(1)} custom-call(f32[32,32]{1,0:T(8,128)S(1)} %fusion.28), custom_call_target="Cholesky" | custom-call | tf_op jit(solution)/shard_map/jit(cholesky)/cholesky | solution.py:62
  128.0 2.4 %custom-call.6 = f32[1,32,32]{1,2,0:T(8,128)S(1)} custom-call(f32[1,32,32]{2,1,0:T(8,128)S(1)} %fusion.23), custom_call_target="InvertDiagBlocksLowerTriangular" | custom-call | tf_op jit(solution)/shard_map/triangular_solve/custom-call.0 | solution.py:64
  130.7 4.5 %fusion.11 = f32[32,8,16,128]{3,0,2,1:T(8,128)S(1)} fusion(f32[32,32,1,1]{1,0,3,2:T(8,128)S(1)} %convolution_bitcast_fusion.1, f32[32,8,16,128]{3,1,2,0:T(8,128)} %copy-done.2), kind=kOutput, calls=%fused_computation.29 | convolution fusion | flops 201326592 | bytes 4198400 | tf_op jit(solution)/shard_map/cd,dzxy->czxy/dot_general | solution.py:76
  135.2 1.8 fusion.18
  137.0 14.9 %all-gather.1 = f32[512,32]{1,0:T(8,128)S(1)} all-gather(f32[32,32]{1,0:T(8,128)S(1)} %fusion.18), channel_id=3, replica_groups=mesh['gx'=32,'gy'=16] {'gy'}, dimensions={0}, use_global_device_ids=true | all-gather | bytes 69632 | tf_op jit(solution)/shard_map/all_gather | solution.py:47
  152.0 1.9 collective-permute-start.9
  153.9 3.7 %collective-permute-done.9 = f32[32,32]{0,1:T(8,128)S(1)} collective-permute-done((f32[32,32]{0,1:T(8,128)S(1)}, f32[32,32]{0,1:T(8,128)S(1)}, u32[]{:S(2)}, u32[]{:S(2)}) %collective-permute-start.9) | collective-permute-done | bytes 4128 | tf_op jit(solution)/shard_map/ppermute | solution.py:52
  157.6 1.9 collective-permute-start.10
  159.5 4.6 %collective-permute-done.10 = f32[32,32]{0,1:T(8,128)S(1)} collective-permute-done((f32[32,32]{0,1:T(8,128)S(1)}, f32[32,32]{0,1:T(8,128)S(1)}, u32[]{:S(2)}, u32[]{:S(2)}) %collective-permute-start.10) | collective-permute-done | bytes 4128 | tf_op jit(solution)/shard_map/ppermute | solution.py:52
  164.1 3.5 %collective-permute-start.11 = (f32[32,32]{0,1:T(8,128)S(1)}, f32[32,32]{0,1:T(8,128)S(1)}, u32[]{:S(2)}, u32[]{:S(2)}) collective-permute-start(f32[32,32]{0,1:T(8,128)S(1)} %add.105), channel_id=1, source_target_pairs={{0,64},{16,80},{32,96},{48,112},{64,0},{80,16},{96,32},{112,48},{1... | collective-permute-start | bytes 12296 | tf_op jit(solution)/shard_map/ppermute | solution.py:52
  167.7 6.0 %collective-permute-done.11 = f32[32,32]{0,1:T(8,128)S(1)} collective-permute-done((f32[32,32]{0,1:T(8,128)S(1)}, f32[32,32]{0,1:T(8,128)S(1)}, u32[]{:S(2)}, u32[]{:S(2)}) %collective-permute-start.11) | collective-permute-done | bytes 4128 | tf_op jit(solution)/shard_map/ppermute | solution.py:52
  173.7 3.1 %collective-permute-start.12 = (f32[32,32]{0,1:T(8,128)S(1)}, f32[32,32]{0,1:T(8,128)S(1)}, u32[]{:S(2)}, u32[]{:S(2)}) collective-permute-start(f32[32,32]{0,1:T(8,128)S(1)} %add.106), channel_id=1, source_target_pairs={{0,128},{16,144},{32,160},{48,176},{64,192},{80,208},{96,224},{112... | collective-permute-start | bytes 12296 | tf_op jit(solution)/shard_map/ppermute | solution.py:52
  176.8 2.5 %collective-permute-done.12 = f32[32,32]{0,1:T(8,128)S(1)} collective-permute-done((f32[32,32]{0,1:T(8,128)S(1)}, f32[32,32]{0,1:T(8,128)S(1)}, u32[]{:S(2)}, u32[]{:S(2)}) %collective-permute-start.12) | collective-permute-done | bytes 4128 | tf_op jit(solution)/shard_map/ppermute | solution.py:52
  179.3 2.4 %collective-permute-start.13 = (f32[32,32]{0,1:T(8,128)S(1)}, f32[32,32]{0,1:T(8,128)S(1)}, u32[]{:S(2)}, u32[]{:S(2)}) collective-permute-start(f32[32,32]{0,1:T(8,128)S(1)} %add.107), channel_id=1, source_target_pairs={{0,256},{16,272},{32,288},{48,304},{64,320},{80,336},{96,352},{112... | collective-permute-start | bytes 12296 | tf_op jit(solution)/shard_map/ppermute | solution.py:52
  181.7 4.7 %collective-permute-done.13 = f32[32,32]{0,1:T(8,128)S(1)} collective-permute-done((f32[32,32]{0,1:T(8,128)S(1)}, f32[32,32]{0,1:T(8,128)S(1)}, u32[]{:S(2)}, u32[]{:S(2)}) %collective-permute-start.13) | collective-permute-done | bytes 4128 | tf_op jit(solution)/shard_map/ppermute | solution.py:52
  186.5 2.9 %cholesky.55 = f32[32,32]{1,0:T(8,128)S(1)} custom-call(f32[32,32]{1,0:T(8,128)S(1)} %fusion.26), custom_call_target="Cholesky" | custom-call | tf_op jit(solution)/shard_map/jit(cholesky)/cholesky | solution.py:62
  190.8 2.4 %custom-call.7 = f32[1,32,32]{1,2,0:T(8,128)S(1)} custom-call(f32[1,32,32]{2,1,0:T(8,128)S(1)} %fusion.24), custom_call_target="InvertDiagBlocksLowerTriangular" | custom-call | tf_op jit(solution)/shard_map/triangular_solve/custom-call.0 | solution.py:64
  193.5 1.9 convolution_multiply_fusion
  195.4 2.5 %copy.31 = f32[32,8,16,128]{3,2,1,0:T(8,128)} copy(f32[32,8,16,128]{3,0,2,1:T(8,128)S(1)} %convolution_multiply_fusion) | data formatting | bytes 4194304 | tf_op jit(solution)/shard_map/mul | solution.py:80
  (46 shorter events, 6.8 us)
Async XLA Ops:
  0.0 2.5 %copy-start.3 = (f32[8,16,128]{2,1,0:T(8,128)S(1)}, f32[8,16,128]{2,1,0:T(8,128)}, u32[]{:S(2)}) copy-start(f32[8,16,128]{2,1,0:T(8,128)} %param.6) | copy-start | bytes 196612
  2.6 10.4 %collective-permute-start = (f32[33,8,2,128]{3,1,2,0:T(8,128)S(1)}, f32[33,8,2,128]{3,1,2,0:T(8,128)S(1)}, u32[]{:S(2)}, u32[]{:S(2)}) collective-permute-start(f32[33,8,2,128]{3,1,2,0:T(8,128)S(1)} %get-tuple-element.9), channel_id=1, source_target_pairs={{0,16},{16,32},{32,48},{48,64},{64,80},{80,96},{96,112},{112,128},... | collective-permute-start | bytes 811016 | tf_op jit(solution)/shard_map/ppermute | solution.py:15
  7.3 11.0 %collective-permute-start.1 = (f32[33,8,2,128]{3,1,2,0:T(8,128)S(1)}, f32[33,8,2,128]{3,1,2,0:T(8,128)S(1)}, u32[]{:S(2)}, u32[]{:S(2)}) collective-permute-start(f32[33,8,2,128]{3,1,2,0:T(8,128)S(1)} %get-tuple-element.10), channel_id=1, source_target_pairs={{16,0},{32,16},{48,32},{64,48},{80,64},{96,80},{112,96},{128,112},... | collective-permute-start | bytes 811016 | tf_op jit(solution)/shard_map/ppermute | solution.py:16
  25.2 6.0 %collective-permute-start.2 = (f32[33,8,20,2]{0,1,3,2:T(8,128)S(1)}, f32[33,8,20,2]{0,1,3,2:T(8,128)S(1)}, u32[]{:S(2)}, u32[]{:S(2)}) collective-permute-start(f32[33,8,20,2]{0,1,3,2:T(8,128)S(1)} %copy.14), channel_id=1, source_target_pairs={{0,1},{1,2},{2,3},{3,4},{4,5},{5,6},{6,7},{7,8},{8,9},{9,10},{10,1... | collective-permute-start | bytes 126728 | tf_op jit(solution)/shard_map/ppermute | solution.py:15
  29.8 5.9 %collective-permute-start.3 = (f32[33,8,20,2]{0,1,3,2:T(8,128)S(1)}, f32[33,8,20,2]{0,1,3,2:T(8,128)S(1)}, u32[]{:S(2)}, u32[]{:S(2)}) collective-permute-start(f32[33,8,20,2]{0,1,3,2:T(8,128)S(1)} %copy.15), channel_id=1, source_target_pairs={{1,0},{2,1},{3,2},{4,3},{5,4},{6,5},{7,6},{8,7},{9,8},{10,9},{11,1... | collective-permute-start | bytes 126728 | tf_op jit(solution)/shard_map/ppermute | solution.py:16
  46.5 1.8 copy-start
  46.6 2.6 %copy-start.1 = (f32[33,8,20,2]{3,1,2,0:T(8,128)S(1)}, f32[33,8,20,2]{3,1,2,0:T(8,128)}, u32[]{:S(2)}) copy-start(f32[33,8,20,2]{3,1,2,0:T(8,128)} %copy.17) | copy-start | bytes 126724
  58.7 1.3 copy-start.2
  89.2 5.6 %collective-permute-start.4 = (f32[32,32]{0,1:T(8,128)S(1)}, f32[32,32]{0,1:T(8,128)S(1)}, u32[]{:S(2)}, u32[]{:S(2)}) collective-permute-start(f32[32,32]{0,1:T(8,128)S(1)} %copy.23), channel_id=1, source_target_pairs={{0,16},{16,0},{32,48},{48,32},{64,80},{80,64},{96,112},{112,96},{1... | collective-permute-start | bytes 12296 | tf_op jit(solution)/shard_map/ppermute | solution.py:52
  94.8 6.5 %collective-permute-start.5 = (f32[32,32]{0,1:T(8,128)S(1)}, f32[32,32]{0,1:T(8,128)S(1)}, u32[]{:S(2)}, u32[]{:S(2)}) collective-permute-start(f32[32,32]{0,1:T(8,128)S(1)} %add.99), channel_id=1, source_target_pairs={{0,32},{16,48},{32,0},{48,16},{64,96},{80,112},{96,64},{112,80},{1... | collective-permute-start | bytes 12296 | tf_op jit(solution)/shard_map/ppermute | solution.py:52
  101.3 9.5 %collective-permute-start.6 = (f32[32,32]{0,1:T(8,128)S(1)}, f32[32,32]{0,1:T(8,128)S(1)}, u32[]{:S(2)}, u32[]{:S(2)}) collective-permute-start(f32[32,32]{0,1:T(8,128)S(1)} %add.100), channel_id=1, source_target_pairs={{0,64},{16,80},{32,96},{48,112},{64,0},{80,16},{96,32},{112,48},{1... | collective-permute-start | bytes 12296 | tf_op jit(solution)/shard_map/ppermute | solution.py:52
  110.9 5.6 %collective-permute-start.7 = (f32[32,32]{0,1:T(8,128)S(1)}, f32[32,32]{0,1:T(8,128)S(1)}, u32[]{:S(2)}, u32[]{:S(2)}) collective-permute-start(f32[32,32]{0,1:T(8,128)S(1)} %add.101), channel_id=1, source_target_pairs={{0,128},{16,144},{32,160},{48,176},{64,192},{80,208},{96,224},{112... | collective-permute-start | bytes 12296 | tf_op jit(solution)/shard_map/ppermute | solution.py:52
  116.5 7.1 %collective-permute-start.8 = (f32[32,32]{0,1:T(8,128)S(1)}, f32[32,32]{0,1:T(8,128)S(1)}, u32[]{:S(2)}, u32[]{:S(2)}) collective-permute-start(f32[32,32]{0,1:T(8,128)S(1)} %add.102), channel_id=1, source_target_pairs={{0,256},{16,272},{32,288},{48,304},{64,320},{80,336},{96,352},{112... | collective-permute-start | bytes 12296 | tf_op jit(solution)/shard_map/ppermute | solution.py:52
  152.0 5.6 %collective-permute-start.9 = (f32[32,32]{0,1:T(8,128)S(1)}, f32[32,32]{0,1:T(8,128)S(1)}, u32[]{:S(2)}, u32[]{:S(2)}) collective-permute-start(f32[32,32]{0,1:T(8,128)S(1)} %copy.29), channel_id=1, source_target_pairs={{0,16},{16,0},{32,48},{48,32},{64,80},{80,64},{96,112},{112,96},{1... | collective-permute-start | bytes 12296 | tf_op jit(solution)/shard_map/ppermute | solution.py:52
  157.6 6.5 %collective-permute-start.10 = (f32[32,32]{0,1:T(8,128)S(1)}, f32[32,32]{0,1:T(8,128)S(1)}, u32[]{:S(2)}, u32[]{:S(2)}) collective-permute-start(f32[32,32]{0,1:T(8,128)S(1)} %add.104), channel_id=1, source_target_pairs={{0,32},{16,48},{32,0},{48,16},{64,96},{80,112},{96,64},{112,80},{1... | collective-permute-start | bytes 12296 | tf_op jit(solution)/shard_map/ppermute | solution.py:52
  164.1 9.5 %collective-permute-start.11 = (f32[32,32]{0,1:T(8,128)S(1)}, f32[32,32]{0,1:T(8,128)S(1)}, u32[]{:S(2)}, u32[]{:S(2)}) collective-permute-start(f32[32,32]{0,1:T(8,128)S(1)} %add.105), channel_id=1, source_target_pairs={{0,64},{16,80},{32,96},{48,112},{64,0},{80,16},{96,32},{112,48},{1... | collective-permute-start | bytes 12296 | tf_op jit(solution)/shard_map/ppermute | solution.py:52
  173.7 5.6 %collective-permute-start.12 = (f32[32,32]{0,1:T(8,128)S(1)}, f32[32,32]{0,1:T(8,128)S(1)}, u32[]{:S(2)}, u32[]{:S(2)}) collective-permute-start(f32[32,32]{0,1:T(8,128)S(1)} %add.106), channel_id=1, source_target_pairs={{0,128},{16,144},{32,160},{48,176},{64,192},{80,208},{96,224},{112... | collective-permute-start | bytes 12296 | tf_op jit(solution)/shard_map/ppermute | solution.py:52
  179.3 7.1 %collective-permute-start.13 = (f32[32,32]{0,1:T(8,128)S(1)}, f32[32,32]{0,1:T(8,128)S(1)}, u32[]{:S(2)}, u32[]{:S(2)}) collective-permute-start(f32[32,32]{0,1:T(8,128)S(1)} %add.107), channel_id=1, source_target_pairs={{0,256},{16,272},{32,288},{48,304},{64,320},{80,336},{96,352},{112... | collective-permute-start | bytes 12296 | tf_op jit(solution)/shard_map/ppermute | solution.py:52

commit v3 on v2

--- a/solution.py
+++ b/solution.py
@@ -45,13 +45,37 @@
 
 def butterfly_sum(value):
     value = jnp.sum(lax.all_gather(value, "gy"), axis=0)
-    count = lax.axis_size("gx")
-    step = 1
-    while step < count:
-        pairs = [(i, i ^ step) for i in range(count)]
-        value = value + lax.ppermute(value, "gx", pairs)
-        step *= 2
+    for partner in gx_partners(lax.axis_size("gx")):
+        value = value + lax.ppermute(value, "gx", [(i, partner(i)) for i in range(len(partner.table))])
     return value
+
+
+class Partner:
+    def __init__(self, table):
+        self.table = table
+
+    def __call__(self, i):
+        return self.table[i]
+
+
+def gx_partners(count):
+    inner = 8 if count % 8 == 0 else count
+    rounds = []
+    for size, stride in ((inner, 1), (count // inner, inner)):
+        group = 2
+        while group <= size:
+            table = []
+            for i in range(count):
+                digit = (i // stride) % size
+                base = digit - digit % group
+                if group == size and size > 2:
+                    other = base + (group - 1 - (digit - base))
+                else:
+                    other = digit ^ (group // 2)
+                table.append(i + (other - digit) * stride)
+            rounds.append(Partner(table))
+            group *= 2
+    return rounds
 
 
 def gram(block):

time: 199 us -> 196 us (0.985)
  the two profiles are of different devices: /device:TPU:28 before, /device:TPU:8 now
where the time goes in v3:
time: 196 us; the launch traced here: 195 us
  starting transfers between devices  48.6 us (25%)
  blocking collectives  41.1 us (21%)
  waiting for transfers between devices  36.3 us (19%)
  other arithmetic  29.8 us (15%)
  local copies, waits for them, and re-layouts  27.5 us (14%)
  matrix products  11.5 us (6%)
    all_gather x2, blocking collectives, butterfly_sum(): value = jnp.sum(lax.all_gather(value, 'gy'), axis=0)  41.1 us
    ppermute x10, starting transfers between devices, butterfly_sum(): lax.ppermute(value, 'gx', [(i, partner(i)) for i in range(len(partner.tab...  37 us
    ppermute x10, waiting for transfers between devices, butterfly_sum(): lax.ppermute(value, 'gx', [(i, partner(i)) for i in range(len(partner.tab...  31.4 us
    slice x3, local copies, waits for them, and re-layouts, extend(): left, right = shifted_in(block[..., -width:], block[..., :width], 'gy')  9.96 us
    another operation x6, other arithmetic, inverse_factor(): factor = jnp.linalg.cholesky(gram_matrix)  7.25 us
    select_n x1, other arithmetic, body(): once = jnp.where(inside_mask(x_cells, y_cells), once, 0.0)  7.04 us
    concatenate x1, other arithmetic, extend(): return jnp.concatenate([left, block, right], axis=3)  6.97 us
    ppermute x2, starting transfers between devices, shifted_in(): from_above = lax.ppermute(upper_part, axis, backward)  6.81 us
  transfers between devices with their start and end apart: 14, of which 13 were waited for; matrix products, arithmetic and copies ran while one was open for 4% of the time, Pallas kernels for 0%

profile of v3, /device:TPU:8, one launch (start us, length us, event | category | flops | bytes accessed | tf_op | source)
XLA Modules:
  0.0 195.2 jit_solution(17458822562988341651)
XLA Ops:
  0.0 2.5 %copy.13 = f32[32,8,16,128]{3,1,2,0:T(8,128)S(1)} copy(f32[32,8,16,128]{3,2,1,0:T(8,128)} %param.5) | data formatting | bytes 4194304 | tf_op args[0]
  2.6 3.5 %collective-permute-start = (f32[33,8,2,128]{3,1,2,0:T(8,128)S(1)}, f32[33,8,2,128]{3,1,2,0:T(8,128)S(1)}, u32[]{:S(2)}, u32[]{:S(2)}) collective-permute-start(f32[33,8,2,128]{3,1,2,0:T(8,128)S(1)} %get-tuple-element.9), channel_id=1, source_target_pairs={{0,16},{16,32},{32,48},{48,64},{64,80},{80,96},{96,112},{112,128},... | collective-permute-start | bytes 811016 | tf_op jit(solution)/shard_map/ppermute | solution.py:15
  6.1 5.5 %collective-permute-start.1 = (f32[33,8,2,128]{3,1,2,0:T(8,128)S(1)}, f32[33,8,2,128]{3,1,2,0:T(8,128)S(1)}, u32[]{:S(2)}, u32[]{:S(2)}) collective-permute-start(f32[33,8,2,128]{3,1,2,0:T(8,128)S(1)} %get-tuple-element.10), channel_id=1, source_target_pairs={{16,0},{32,16},{48,32},{64,48},{80,64},{96,80},{112,96},{128,112},... | collective-permute-start | bytes 811016 | tf_op jit(solution)/shard_map/ppermute | solution.py:16
  11.7 2.4 %collective-permute-done = f32[33,8,2,128]{3,1,2,0:T(8,128)S(1)} collective-permute-done((f32[33,8,2,128]{3,1,2,0:T(8,128)S(1)}, f32[33,8,2,128]{3,1,2,0:T(8,128)S(1)}, u32[]{:S(2)}, u32[]{:S(2)}) %collective-permute-start) | collective-permute-done | bytes 270368 | tf_op jit(solution)/shard_map/ppermute | solution.py:15
  14.1 1.8 collective-permute-done.1
  16.2 3.3 %fusion.31 = (f32[33,8,20,2]{3,1,2,0:T(8,128)}, f32[33,8,20,2]{3,1,2,0:T(8,128)}) fusion(f32[33,8,20,128]{3,1,2,0:T(8,128)S(1)} %pad_maximum_fusion.9), kind=kLoop, calls=%fused_computation.66 | loop fusion | bytes 168960 | tf_op jit(solution)/shard_map/slice | solution.py:23
  19.5 3.3 %copy.14 = f32[33,8,20,2]{0,1,3,2:T(8,128)S(1)} copy(f32[33,8,20,2]{3,1,2,0:T(8,128)} %get-tuple-element.6) | data formatting | bytes 84480 | tf_op jit(solution)/shard_map/slice | solution.py:23
  22.8 1.3 collective-permute-start.2
  24.1 3.3 %copy.15 = f32[33,8,20,2]{0,1,3,2:T(8,128)S(1)} copy(f32[33,8,20,2]{3,1,2,0:T(8,128)} %get-tuple-element.8) | data formatting | bytes 84480 | tf_op jit(solution)/shard_map/slice | solution.py:23
  27.4 1.3 collective-permute-start.3
  28.8 3.8 %copy.16 = f32[33,8,20,2]{3,1,2,0:T(8,128)} copy(f32[33,8,20,2]{0,1,3,2:T(8,128)S(1)} %collective-permute-done.2) | data formatting | bytes 84480 | tf_op jit(solution)/shard_map/ppermute | solution.py:15
  33.3 3.8 %copy.17 = f32[33,8,20,2]{3,1,2,0:T(8,128)} copy(f32[33,8,20,2]{0,1,3,2:T(8,128)S(1)} %collective-permute-done.3) | data formatting | bytes 84480 | tf_op jit(solution)/shard_map/ppermute | solution.py:16
  37.1 7.0 %pad_maximum_fusion = f32[33,8,20,132]{3,1,2,0:T(8,128)S(1)} fusion(f32[33,8,20,2]{3,1,2,0:T(8,128)} %copy.17, f32[33,8,2,128]{3,1,2,0:T(8,128)S(1)} %collective-permute-done.1, f32[1,8,16,128]{3,1,2,0:T(8,128)S(1)} %bitcast.46, f32[32,8,16,128]{3,1,2,0:T(8,128)S(1)} %copy.13, f32[33,8,2,128]{3,1,2,0:T(8,128)S(1)} %collective-permute-done, ...), kind=kLoop, calls=%fused_computation.2 | loop fusion | flops 3484800 | bytes 5575680 | tf_op jit(solution)/shard_map/concatenate | solution.py:24
  44.1 1.3 slice.97
  47.0 7.0 %fusion.3 = f32[32,8,18,130]{3,1,2,0:T(8,128)S(1)} fusion(f32[32,8,18,130]{3,1,2,0:T(8,128)S(1)} %slice.97, f32[33,8,20,2]{3,1,2,0:T(8,128)S(1)} %copy-done, f32[33,8,2,128]{3,1,2,0:T(8,128)S(1)} %collective-permute-done.1, f32[33,8,2,128]{3,1,2,0:T(8,128)S(1)} %collective-permute-done, f32[1,8,16,128]{3,1,2,0:T(8,128)S(1)} %bitcast.48, ...), kind=kLoop, calls=%fused_computation.8 | loop fusion | flops 9584640 | bytes 12449700 | tf_op jit(solution)/shard_map/jit(_where)/select_n | solution.py:97
  54.6 1.7 fusion.8
  56.3 1.3 copy-done.2
  57.6 2.8 %fusion.15 = f32[32,32]{1,0:T(8,128)S(1)} fusion(f32[32,8,16,128]{3,1,2,0:T(8,128)S(1)} %fusion.8), kind=kOutput, calls=%fused_computation.34 | convolution fusion | flops 201326592 | bytes 2101248 | tf_op jit(solution)/shard_map/czxy,dzxy->cd/dot_general | solution.py:82
  60.4 26.2 %all-gather = f32[512,32]{1,0:T(8,128)S(1)} all-gather(f32[32,32]{1,0:T(8,128)S(1)} %fusion.15), channel_id=2, replica_groups=mesh['gx'=32,'gy'=16] {'gy'}, dimensions={0}, use_global_device_ids=true | all-gather | bytes 69632 | tf_op jit(solution)/shard_map/all_gather | solution.py:47
  86.8 2.4 %collective-permute-start.4 = (f32[32,32]{0,1:T(8,128)S(1)}, f32[32,32]{0,1:T(8,128)S(1)}, u32[]{:S(2)}, u32[]{:S(2)}) collective-permute-start(f32[32,32]{0,1:T(8,128)S(1)} %copy.23), channel_id=1, source_target_pairs={{0,16},{16,0},{32,48},{48,32},{64,80},{80,64},{96,112},{112,96},{1... | collective-permute-start | bytes 12296 | tf_op jit(solution)/shard_map/ppermute | solution.py:49
  89.2 3.2 %collective-permute-done.4 = f32[32,32]{0,1:T(8,128)S(1)} collective-permute-done((f32[32,32]{0,1:T(8,128)S(1)}, f32[32,32]{0,1:T(8,128)S(1)}, u32[]{:S(2)}, u32[]{:S(2)}) %collective-permute-start.4) | collective-permute-done | bytes 4128 | tf_op jit(solution)/shard_map/ppermute | solution.py:49
  92.4 6.9 %collective-permute-start.5 = (f32[32,32]{0,1:T(8,128)S(1)}, f32[32,32]{0,1:T(8,128)S(1)}, u32[]{:S(2)}, u32[]{:S(2)}) collective-permute-start(f32[32,32]{0,1:T(8,128)S(1)} %add.99), channel_id=1, source_target_pairs={{0,32},{16,48},{32,0},{48,16},{64,96},{80,112},{96,64},{112,80},{1... | collective-permute-start | bytes 12296 | tf_op jit(solution)/shard_map/ppermute | solution.py:49
  99.3 1.7 collective-permute-done.5
  101.0 3.9 %collective-permute-start.6 = (f32[32,32]{0,1:T(8,128)S(1)}, f32[32,32]{0,1:T(8,128)S(1)}, u32[]{:S(2)}, u32[]{:S(2)}) collective-permute-start(f32[32,32]{0,1:T(8,128)S(1)} %add.100), channel_id=1, source_target_pairs={{0,112},{16,96},{32,80},{48,64},{64,48},{80,32},{96,16},{112,0},{1... | collective-permute-start | bytes 12296 | tf_op jit(solution)/shard_map/ppermute | solution.py:49
  104.9 4.7 %collective-permute-done.6 = f32[32,32]{0,1:T(8,128)S(1)} collective-permute-done((f32[32,32]{0,1:T(8,128)S(1)}, f32[32,32]{0,1:T(8,128)S(1)}, u32[]{:S(2)}, u32[]{:S(2)}) %collective-permute-start.6) | collective-permute-done | bytes 4128 | tf_op jit(solution)/shard_map/ppermute | solution.py:49
  109.6 3.4 %collective-permute-start.7 = (f32[32,32]{0,1:T(8,128)S(1)}, f32[32,32]{0,1:T(8,128)S(1)}, u32[]{:S(2)}, u32[]{:S(2)}) collective-permute-start(f32[32,32]{0,1:T(8,128)S(1)} %add.101), channel_id=1, source_target_pairs={{0,128},{16,144},{32,160},{48,176},{64,192},{80,208},{96,224},{112... | collective-permute-start | bytes 12296 | tf_op jit(solution)/shard_map/ppermute | solution.py:49
  113.0 2.2 %collective-permute-done.7 = f32[32,32]{0,1:T(8,128)S(1)} collective-permute-done((f32[32,32]{0,1:T(8,128)S(1)}, f32[32,32]{0,1:T(8,128)S(1)}, u32[]{:S(2)}, u32[]{:S(2)}) %collective-permute-start.7) | collective-permute-done | bytes 4128 | tf_op jit(solution)/shard_map/ppermute | solution.py:49
  115.3 4.9 %collective-permute-start.8 = (f32[32,32]{0,1:T(8,128)S(1)}, f32[32,32]{0,1:T(8,128)S(1)}, u32[]{:S(2)}, u32[]{:S(2)}) collective-permute-start(f32[32,32]{0,1:T(8,128)S(1)} %add.102), channel_id=1, source_target_pairs={{0,384},{16,400},{32,416},{48,432},{64,448},{80,464},{96,480},{112... | collective-permute-start | bytes 12296 | tf_op jit(solution)/shard_map/ppermute | solution.py:49
  120.2 1.9 collective-permute-done.8
  122.2 2.9 %cholesky.44 = f32[32,32]{1,0:T(8,128)S(1)} custom-call(f32[32,32]{1,0:T(8,128)S(1)} %fusion.28), custom_call_target="Cholesky" | custom-call | tf_op jit(solution)/shard_map/jit(cholesky)/cholesky | solution.py:86
  126.5 2.4 %custom-call.6 = f32[1,32,32]{1,2,0:T(8,128)S(1)} custom-call(f32[1,32,32]{2,1,0:T(8,128)S(1)} %fusion.23), custom_call_target="InvertDiagBlocksLowerTriangular" | custom-call | tf_op jit(solution)/shard_map/triangular_solve/custom-call.0 | solution.py:88
  129.2 4.5 %fusion.11 = f32[32,8,16,128]{3,0,2,1:T(8,128)S(1)} fusion(f32[32,32,1,1]{1,0,3,2:T(8,128)S(1)} %convolution_bitcast_fusion.1, f32[32,8,16,128]{3,1,2,0:T(8,128)} %copy-done.2), kind=kOutput, calls=%fused_computation.29 | convolution fusion | flops 201326592 | bytes 4198400 | tf_op jit(solution)/shard_map/cd,dzxy->czxy/dot_general | solution.py:100
  133.7 1.8 fusion.18
  135.5 14.9 %all-gather.1 = f32[512,32]{1,0:T(8,128)S(1)} all-gather(f32[32,32]{1,0:T(8,128)S(1)} %fusion.18), channel_id=3, replica_groups=mesh['gx'=32,'gy'=16] {'gy'}, dimensions={0}, use_global_device_ids=true | all-gather | bytes 69632 | tf_op jit(solution)/shard_map/all_gather | solution.py:47
  150.5 1.9 collective-permute-start.9
  152.4 3.7 %collective-permute-done.9 = f32[32,32]{0,1:T(8,128)S(1)} collective-permute-done((f32[32,32]{0,1:T(8,128)S(1)}, f32[32,32]{0,1:T(8,128)S(1)}, u32[]{:S(2)}, u32[]{:S(2)}) %collective-permute-start.9) | collective-permute-done | bytes 4128 | tf_op jit(solution)/shard_map/ppermute | solution.py:49
  156.1 3.0 %collective-permute-start.10 = (f32[32,32]{0,1:T(8,128)S(1)}, f32[32,32]{0,1:T(8,128)S(1)}, u32[]{:S(2)}, u32[]{:S(2)}) collective-permute-start(f32[32,32]{0,1:T(8,128)S(1)} %add.104), channel_id=1, source_target_pairs={{0,32},{16,48},{32,0},{48,16},{64,96},{80,112},{96,64},{112,80},{1... | collective-permute-start | bytes 12296 | tf_op jit(solution)/shard_map/ppermute | solution.py:49
  159.1 3.5 %collective-permute-done.10 = f32[32,32]{0,1:T(8,128)S(1)} collective-permute-done((f32[32,32]{0,1:T(8,128)S(1)}, f32[32,32]{0,1:T(8,128)S(1)}, u32[]{:S(2)}, u32[]{:S(2)}) %collective-permute-start.10) | collective-permute-done | bytes 4128 | tf_op jit(solution)/shard_map/ppermute | solution.py:49
  162.6 3.9 %collective-permute-start.11 = (f32[32,32]{0,1:T(8,128)S(1)}, f32[32,32]{0,1:T(8,128)S(1)}, u32[]{:S(2)}, u32[]{:S(2)}) collective-permute-start(f32[32,32]{0,1:T(8,128)S(1)} %add.105), channel_id=1, source_target_pairs={{0,112},{16,96},{32,80},{48,64},{64,48},{80,32},{96,16},{112,0},{1... | collective-permute-start | bytes 12296 | tf_op jit(solution)/shard_map/ppermute | solution.py:49
  166.5 4.8 %collective-permute-done.11 = f32[32,32]{0,1:T(8,128)S(1)} collective-permute-done((f32[32,32]{0,1:T(8,128)S(1)}, f32[32,32]{0,1:T(8,128)S(1)}, u32[]{:S(2)}, u32[]{:S(2)}) %collective-permute-start.11) | collective-permute-done | bytes 4128 | tf_op jit(solution)/shard_map/ppermute | solution.py:49
  171.3 2.2 %collective-permute-start.12 = (f32[32,32]{0,1:T(8,128)S(1)}, f32[32,32]{0,1:T(8,128)S(1)}, u32[]{:S(2)}, u32[]{:S(2)}) collective-permute-start(f32[32,32]{0,1:T(8,128)S(1)} %add.106), channel_id=1, source_target_pairs={{0,128},{16,144},{32,160},{48,176},{64,192},{80,208},{96,224},{112... | collective-permute-start | bytes 12296 | tf_op jit(solution)/shard_map/ppermute | solution.py:49
  173.4 3.5 %collective-permute-done.12 = f32[32,32]{0,1:T(8,128)S(1)} collective-permute-done((f32[32,32]{0,1:T(8,128)S(1)}, f32[32,32]{0,1:T(8,128)S(1)}, u32[]{:S(2)}, u32[]{:S(2)}) %collective-permute-start.12) | collective-permute-done | bytes 4128 | tf_op jit(solution)/shard_map/ppermute | solution.py:49
  176.9 4.7 %collective-permute-start.13 = (f32[32,32]{0,1:T(8,128)S(1)}, f32[32,32]{0,1:T(8,128)S(1)}, u32[]{:S(2)}, u32[]{:S(2)}) collective-permute-start(f32[32,32]{0,1:T(8,128)S(1)} %add.107), channel_id=1, source_target_pairs={{0,384},{16,400},{32,416},{48,432},{64,448},{80,464},{96,480},{112... | collective-permute-start | bytes 12296 | tf_op jit(solution)/shard_map/ppermute | solution.py:49
  181.5 2.2 %collective-permute-done.13 = f32[32,32]{0,1:T(8,128)S(1)} collective-permute-done((f32[32,32]{0,1:T(8,128)S(1)}, f32[32,32]{0,1:T(8,128)S(1)}, u32[]{:S(2)}, u32[]{:S(2)}) %collective-permute-start.13) | collective-permute-done | bytes 4128 | tf_op jit(solution)/shard_map/ppermute | solution.py:49
  183.8 2.9 %cholesky.55 = f32[32,32]{1,0:T(8,128)S(1)} custom-call(f32[32,32]{1,0:T(8,128)S(1)} %fusion.26), custom_call_target="Cholesky" | custom-call | tf_op jit(solution)/shard_map/jit(cholesky)/cholesky | solution.py:86
  188.1 2.4 %custom-call.7 = f32[1,32,32]{1,2,0:T(8,128)S(1)} custom-call(f32[1,32,32]{2,1,0:T(8,128)S(1)} %fusion.24), custom_call_target="InvertDiagBlocksLowerTriangular" | custom-call | tf_op jit(solution)/shard_map/triangular_solve/custom-call.0 | solution.py:88
  190.7 1.9 convolution_multiply_fusion
  192.7 2.5 %copy.31 = f32[32,8,16,128]{3,2,1,0:T(8,128)} copy(f32[32,8,16,128]{3,0,2,1:T(8,128)S(1)} %convolution_multiply_fusion) | data formatting | bytes 4194304 | tf_op jit(solution)/shard_map/mul | solution.py:104
  (46 shorter events, 6.8 us)
Async XLA Ops:
  0.0 2.5 %copy-start.3 = (f32[8,16,128]{2,1,0:T(8,128)S(1)}, f32[8,16,128]{2,1,0:T(8,128)}, u32[]{:S(2)}) copy-start(f32[8,16,128]{2,1,0:T(8,128)} %param.6) | copy-start | bytes 196612
  2.6 11.5 %collective-permute-start = (f32[33,8,2,128]{3,1,2,0:T(8,128)S(1)}, f32[33,8,2,128]{3,1,2,0:T(8,128)S(1)}, u32[]{:S(2)}, u32[]{:S(2)}) collective-permute-start(f32[33,8,2,128]{3,1,2,0:T(8,128)S(1)} %get-tuple-element.9), channel_id=1, source_target_pairs={{0,16},{16,32},{32,48},{48,64},{64,80},{80,96},{96,112},{112,128},... | collective-permute-start | bytes 811016 | tf_op jit(solution)/shard_map/ppermute | solution.py:15
  6.1 9.8 %collective-permute-start.1 = (f32[33,8,2,128]{3,1,2,0:T(8,128)S(1)}, f32[33,8,2,128]{3,1,2,0:T(8,128)S(1)}, u32[]{:S(2)}, u32[]{:S(2)}) collective-permute-start(f32[33,8,2,128]{3,1,2,0:T(8,128)S(1)} %get-tuple-element.10), channel_id=1, source_target_pairs={{16,0},{32,16},{48,32},{64,48},{80,64},{96,80},{112,96},{128,112},... | collective-permute-start | bytes 811016 | tf_op jit(solution)/shard_map/ppermute | solution.py:16
  22.8 6.0 %collective-permute-start.2 = (f32[33,8,20,2]{0,1,3,2:T(8,128)S(1)}, f32[33,8,20,2]{0,1,3,2:T(8,128)S(1)}, u32[]{:S(2)}, u32[]{:S(2)}) collective-permute-start(f32[33,8,20,2]{0,1,3,2:T(8,128)S(1)} %copy.14), channel_id=1, source_target_pairs={{0,1},{1,2},{2,3},{3,4},{4,5},{5,6},{6,7},{7,8},{8,9},{9,10},{10,1... | collective-permute-start | bytes 126728 | tf_op jit(solution)/shard_map/ppermute | solution.py:15
  27.4 5.9 %collective-permute-start.3 = (f32[33,8,20,2]{0,1,3,2:T(8,128)S(1)}, f32[33,8,20,2]{0,1,3,2:T(8,128)S(1)}, u32[]{:S(2)}, u32[]{:S(2)}) collective-permute-start(f32[33,8,20,2]{0,1,3,2:T(8,128)S(1)} %copy.15), channel_id=1, source_target_pairs={{1,0},{2,1},{3,2},{4,3},{5,4},{6,5},{7,6},{8,7},{9,8},{10,9},{11,1... | collective-permute-start | bytes 126728 | tf_op jit(solution)/shard_map/ppermute | solution.py:16
  44.1 1.8 copy-start
  44.1 2.6 %copy-start.1 = (f32[33,8,20,2]{3,1,2,0:T(8,128)S(1)}, f32[33,8,20,2]{3,1,2,0:T(8,128)}, u32[]{:S(2)}) copy-start(f32[33,8,20,2]{3,1,2,0:T(8,128)} %copy.17) | copy-start | bytes 126724
  56.3 1.3 copy-start.2
  86.8 5.6 %collective-permute-start.4 = (f32[32,32]{0,1:T(8,128)S(1)}, f32[32,32]{0,1:T(8,128)S(1)}, u32[]{:S(2)}, u32[]{:S(2)}) collective-permute-start(f32[32,32]{0,1:T(8,128)S(1)} %copy.23), channel_id=1, source_target_pairs={{0,16},{16,0},{32,48},{48,32},{64,80},{80,64},{96,112},{112,96},{1... | collective-permute-start | bytes 12296 | tf_op jit(solution)/shard_map/ppermute | solution.py:49
  92.4 8.6 %collective-permute-start.5 = (f32[32,32]{0,1:T(8,128)S(1)}, f32[32,32]{0,1:T(8,128)S(1)}, u32[]{:S(2)}, u32[]{:S(2)}) collective-permute-start(f32[32,32]{0,1:T(8,128)S(1)} %add.99), channel_id=1, source_target_pairs={{0,32},{16,48},{32,0},{48,16},{64,96},{80,112},{96,64},{112,80},{1... | collective-permute-start | bytes 12296 | tf_op jit(solution)/shard_map/ppermute | solution.py:49
  101.0 8.6 %collective-permute-start.6 = (f32[32,32]{0,1:T(8,128)S(1)}, f32[32,32]{0,1:T(8,128)S(1)}, u32[]{:S(2)}, u32[]{:S(2)}) collective-permute-start(f32[32,32]{0,1:T(8,128)S(1)} %add.100), channel_id=1, source_target_pairs={{0,112},{16,96},{32,80},{48,64},{64,48},{80,32},{96,16},{112,0},{1... | collective-permute-start | bytes 12296 | tf_op jit(solution)/shard_map/ppermute | solution.py:49
  109.6 5.6 %collective-permute-start.7 = (f32[32,32]{0,1:T(8,128)S(1)}, f32[32,32]{0,1:T(8,128)S(1)}, u32[]{:S(2)}, u32[]{:S(2)}) collective-permute-start(f32[32,32]{0,1:T(8,128)S(1)} %add.101), channel_id=1, source_target_pairs={{0,128},{16,144},{32,160},{48,176},{64,192},{80,208},{96,224},{112... | collective-permute-start | bytes 12296 | tf_op jit(solution)/shard_map/ppermute | solution.py:49
  115.3 6.8 %collective-permute-start.8 = (f32[32,32]{0,1:T(8,128)S(1)}, f32[32,32]{0,1:T(8,128)S(1)}, u32[]{:S(2)}, u32[]{:S(2)}) collective-permute-start(f32[32,32]{0,1:T(8,128)S(1)} %add.102), channel_id=1, source_target_pairs={{0,384},{16,400},{32,416},{48,432},{64,448},{80,464},{96,480},{112... | collective-permute-start | bytes 12296 | tf_op jit(solution)/shard_map/ppermute | solution.py:49
  150.5 5.6 %collective-permute-start.9 = (f32[32,32]{0,1:T(8,128)S(1)}, f32[32,32]{0,1:T(8,128)S(1)}, u32[]{:S(2)}, u32[]{:S(2)}) collective-permute-start(f32[32,32]{0,1:T(8,128)S(1)} %copy.29), channel_id=1, source_target_pairs={{0,16},{16,0},{32,48},{48,32},{64,80},{80,64},{96,112},{112,96},{1... | collective-permute-start | bytes 12296 | tf_op jit(solution)/shard_map/ppermute | solution.py:49
  156.1 6.5 %collective-permute-start.10 = (f32[32,32]{0,1:T(8,128)S(1)}, f32[32,32]{0,1:T(8,128)S(1)}, u32[]{:S(2)}, u32[]{:S(2)}) collective-permute-start(f32[32,32]{0,1:T(8,128)S(1)} %add.104), channel_id=1, source_target_pairs={{0,32},{16,48},{32,0},{48,16},{64,96},{80,112},{96,64},{112,80},{1... | collective-permute-start | bytes 12296 | tf_op jit(solution)/shard_map/ppermute | solution.py:49
  162.6 8.6 %collective-permute-start.11 = (f32[32,32]{0,1:T(8,128)S(1)}, f32[32,32]{0,1:T(8,128)S(1)}, u32[]{:S(2)}, u32[]{:S(2)}) collective-permute-start(f32[32,32]{0,1:T(8,128)S(1)} %add.105), channel_id=1, source_target_pairs={{0,112},{16,96},{32,80},{48,64},{64,48},{80,32},{96,16},{112,0},{1... | collective-permute-start | bytes 12296 | tf_op jit(solution)/shard_map/ppermute | solution.py:49
  171.3 5.6 %collective-permute-start.12 = (f32[32,32]{0,1:T(8,128)S(1)}, f32[32,32]{0,1:T(8,128)S(1)}, u32[]{:S(2)}, u32[]{:S(2)}) collective-permute-start(f32[32,32]{0,1:T(8,128)S(1)} %add.106), channel_id=1, source_target_pairs={{0,128},{16,144},{32,160},{48,176},{64,192},{80,208},{96,224},{112... | collective-permute-start | bytes 12296 | tf_op jit(solution)/shard_map/ppermute | solution.py:49
  176.9 6.8 %collective-permute-start.13 = (f32[32,32]{0,1:T(8,128)S(1)}, f32[32,32]{0,1:T(8,128)S(1)}, u32[]{:S(2)}, u32[]{:S(2)}) collective-permute-start(f32[32,32]{0,1:T(8,128)S(1)} %add.107), channel_id=1, source_target_pairs={{0,384},{16,400},{32,416},{48,432},{64,448},{80,464},{96,480},{112... | collective-permute-start | bytes 12296 | tf_op jit(solution)/shard_map/ppermute | solution.py:49

commit v4 on v3

--- a/solution.py
+++ b/solution.py
@@ -3,6 +3,8 @@
 import jax
 import jax.numpy as jnp
 from jax import lax
+from jax.experimental import pallas as pl
+from jax.experimental.pallas import tpu as pltpu
 from jax.sharding import PartitionSpec as P
 
 HIGHEST = lax.Precision.HIGHEST
@@ -17,30 +19,74 @@
     return from_below, from_above
 
 
-def extend(block, width):
-    below, above = shifted_in(block[:, :, -width:, :], block[:, :, :width, :], "gx")
-    block = jnp.concatenate([below, block, above], axis=2)
-    left, right = shifted_in(block[..., -width:], block[..., :width], "gy")
-    return jnp.concatenate([left, block, right], axis=3)
+def _zs(v, up):
+    zero = jnp.zeros_like(v[:1])
+    return jnp.concatenate([v[1:], zero], 0) if up else jnp.concatenate([zero, v[:-1]], 0)
 
 
-def stencil(padded, coefficient):
-    center = padded[:, :, 1:-1, 1:-1]
-    neighbours = padded[:, :, 2:, 1:-1] + padded[:, :, :-2, 1:-1]
-    neighbours = neighbours + padded[:, :, 1:-1, 2:] + padded[:, :, 1:-1, :-2]
-    z_padded = jnp.pad(center, ((0, 0), (1, 1), (0, 0), (0, 0)))
-    neighbours = neighbours + z_padded[:, 2:] + z_padded[:, :-2]
-    return (6.0 + coefficient) * center - neighbours
+def _sten(center, xu, xd, yu, yd, coef):
+    nb = xu + xd
+    nb = nb + yu + yd
+    nb = nb + _zs(center, True) + _zs(center, False)
+    return (6.0 + coef) * center - nb
 
 
-def inside_mask(x_cells, y_cells):
-    ix, iy = lax.axis_index("gx"), lax.axis_index("gy")
-    nx, ny = lax.axis_size("gx"), lax.axis_size("gy")
-    rows = lax.broadcasted_iota(jnp.int32, (x_cells + 2, y_cells + 2), 0)
-    cols = lax.broadcasted_iota(jnp.int32, (x_cells + 2, y_cells + 2), 1)
-    row_ok = ((rows > 0) | (ix > 0)) & ((rows < x_cells + 1) | (ix < nx - 1))
-    col_ok = ((cols > 0) | (iy > 0)) & ((cols < y_cells + 1) | (iy < ny - 1))
-    return row_ok & col_ok
+def _kernel(flags, f_ref, k_ref, xl_ref, xh_ref, kxl_ref, kxh_ref, yl_ref, yr_ref, kyl_ref, kyr_ref, o_ref):
+    f = f_ref[0]
+    k = k_ref[...]
+    xl = xl_ref[0]; xh = xh_ref[0]
+    kxl = kxl_ref[...]; kxh = kxh_ref[...]
+    yl = yl_ref[0]; yr = yr_ref[0]
+    kyl = kyl_ref[...]; kyr = kyr_ref[...]
+    nz, nx, ny = f.shape
+    row = lax.broadcasted_iota(jnp.int32, f.shape, 1)
+    lane = lax.broadcasted_iota(jnp.int32, f.shape, 2)
+    lane_r = lax.broadcasted_iota(jnp.int32, (nz, 1, ny), 2)
+
+    def xshift(v, top, bot, up):
+        if up:
+            return jnp.where(row == nx - 1, bot, pltpu.roll(v, nx - 1, 1))
+        return jnp.where(row == 0, top, pltpu.roll(v, 1, 1))
+
+    def yshift(v, left, right, up, lanes):
+        if up:
+            return jnp.where(lanes == ny - 1, right, pltpu.roll(v, ny - 1, 2))
+        return jnp.where(lanes == 0, left, pltpu.roll(v, 1, 2))
+
+    ycl, ycr = yl[:, 2:nx + 2, 1:2], yr[:, 2:nx + 2, 0:1]
+    main = _sten(f, xshift(f, xl[:, 1:2], xh[:, 0:1], True), xshift(f, xl[:, 1:2], xh[:, 0:1], False),
+                 yshift(f, ycl, ycr, True, lane), yshift(f, ycl, ycr, False, lane), k)
+    top_c, bot_c = xl[:, 1:2], xh[:, 0:1]
+    top = _sten(top_c, f[:, 0:1], xl[:, 0:1],
+                yshift(top_c, yl[:, 1:2, 1:2], yr[:, 1:2, 0:1], True, lane_r),
+                yshift(top_c, yl[:, 1:2, 1:2], yr[:, 1:2, 0:1], False, lane_r), kxl)
+    bot = _sten(bot_c, xh[:, 1:2], f[:, nx - 1:nx],
+                yshift(bot_c, yl[:, nx + 2:nx + 3, 1:2], yr[:, nx + 2:nx + 3, 0:1], True, lane_r),
+                yshift(bot_c, yl[:, nx + 2:nx + 3, 1:2], yr[:, nx + 2:nx + 3, 0:1], False, lane_r), kxh)
+    left = _sten(ycl, yl[:, 3:nx + 3, 1:2], yl[:, 1:nx + 1, 1:2], f[:, :, 0:1], yl[:, 2:nx + 2, 0:1], kyl)
+    right = _sten(ycr, yr[:, 3:nx + 3, 0:1], yr[:, 1:nx + 1, 0:1], yr[:, 2:nx + 2, 1:2], f[:, :, ny - 1:ny], kyr)
+    top = jnp.where(flags[0] > 0, top, 0.0)
+    bot = jnp.where(flags[1] > 0, bot, 0.0)
+    left = jnp.where(flags[2] > 0, left, 0.0)
+    right = jnp.where(flags[3] > 0, right, 0.0)
+    o_ref[0] = _sten(main, xshift(main, top, bot, True), xshift(main, top, bot, False),
+                     yshift(main, left, right, True, lane), yshift(main, left, right, False, lane), k)
+
+
+def twice_kernel(flags, f, k, xl, xh, kxl, kxh, yl, yr, kyl, kyr):
+    cols, nz, nx, ny = f.shape
+    blk = lambda shape: pl.BlockSpec((1,) + shape, lambda c, fl: (c,) + (0,) * len(shape))
+    full = lambda shape: pl.BlockSpec(shape, lambda c, fl: (0,) * len(shape))
+    gs = pltpu.PrefetchScalarGridSpec(
+        num_scalar_prefetch=1, grid=(cols,),
+        in_specs=[blk((nz, nx, ny)), full((nz, nx, ny)), blk((nz, 2, ny)), blk((nz, 2, ny)),
+                  full((nz, 1, ny)), full((nz, 1, ny)), blk((nz, nx + 4, 2)), blk((nz, nx + 4, 2)),
+                  full((nz, nx, 1)), full((nz, nx, 1))],
+        out_specs=blk((nz, nx, ny)))
+    return pl.pallas_call(
+        _kernel, grid_spec=gs, out_shape=jax.ShapeDtypeStruct(f.shape, f.dtype),
+        cost_estimate=pl.CostEstimate(flops=40 * f.size, bytes_accessed=8 * f.size, transcendentals=0),
+    )(flags, f, k, xl, xh, kxl, kxh, yl, yr, kyl, kyr)
 
 
 def butterfly_sum(value):
@@ -91,11 +137,17 @@
 def body(test_block, kappa_sq):
     cols_here, depth_here, x_cells, y_cells = test_block.shape
     joined = jnp.concatenate([test_block, kappa_sq[None]], axis=0)
-    padded = extend(joined, 2)
-    field_ext, kappa_ext = padded[:cols_here], padded[cols_here]
-    once = stencil(field_ext, kappa_ext[None, :, 1:-1, 1:-1])
-    once = jnp.where(inside_mask(x_cells, y_cells), once, 0.0)
-    sample = stencil(once, kappa_sq)
+    below, above = shifted_in(joined[:, :, -2:, :], joined[:, :, :2, :], "gx")
+    ext = jnp.concatenate([below, joined, above], axis=2)
+    left, right = shifted_in(ext[..., -2:], ext[..., :2], "gy")
+    ix, iy = lax.axis_index("gx"), lax.axis_index("gy")
+    nx, ny = lax.axis_size("gx"), lax.axis_size("gy")
+    flags = jnp.stack([ix > 0, ix < nx - 1, iy > 0, iy < ny - 1]).astype(jnp.int32)
+    c = cols_here
+    sample = twice_kernel(
+        flags, test_block, kappa_sq, below[:c], above[:c], below[c][:, 1:2], above[c][:, 0:1],
+        left[:c], right[:c], left[c][:, 2:x_cells + 2, 1:2], right[c][:, 2:x_cells + 2, 0:1],
+    )
     inverse_one = inverse_factor(butterfly_sum(gram(sample)))
     partial_value = jnp.einsum("cd,dzxy->czxy", inverse_one, sample, precision=HIGHEST)
     inverse_two = inverse_factor(butterfly_sum(gram(partial_value)))

time: 196 us -> 221 us (1.13)
  the two profiles are of different devices: /device:TPU:8 before, /device:TPU:14 now
where the time goes in v4:
time: 221 us; the launch traced here: 220 us
  waiting for transfers between devices  49.6 us (22%)
  blocking collectives  41.7 us (19%)
  starting transfers between devices  34.9 us (16%)
  local copies, waits for them, and re-layouts  33.5 us (15%)
  Pallas kernels  27.9 us (13%)
  other arithmetic  16.7 us (8%)
  matrix products  15 us (7%)
    ppermute x10, waiting for transfers between devices, butterfly_sum(): lax.ppermute(value, 'gx', [(i, partner(i)) for i in range(len(partner.tab...  41.9 us
    all_gather x2, blocking collectives, butterfly_sum(): value = jnp.sum(lax.all_gather(value, 'gy'), axis=0)  41.7 us
    pallas_call x1, Pallas kernels, twice_kernel(): pl.pallas_call(_kernel, grid_spec=gs, out_shape=jax.ShapeDtypeStruct(f.sh...  27.9 us
    ppermute x10, starting transfers between devices, butterfly_sum(): lax.ppermute(value, 'gx', [(i, partner(i)) for i in range(len(partner.tab...  26.3 us
    unnamed x14, local copies, waits for them, and re-layouts  13.2 us
    slice x3, local copies, waits for them, and re-layouts, body(): left, right = shifted_in(ext[..., -2:], ext[..., :2], 'gy')  11.6 us
    dot_general x2, matrix products, gram(): return jnp.einsum('czxy,dzxy->cd', block, block, precision=HIGHEST)  8.08 us
    another operation x6, other arithmetic, inverse_factor(): factor = jnp.linalg.cholesky(gram_matrix)  7.25 us
  transfers between devices with their start and end apart: 14, of which 12 were waited for; matrix products, arithmetic and copies ran while one was open for 3% of the time, Pallas kernels for 0%

profile of v4, /device:TPU:14, one launch (start us, length us, event | category | flops | bytes accessed | tf_op | source)
XLA Modules:
  0.0 219.5 jit_solution(3721120217855003385)
XLA Ops:
  0.0 2.0 pad_maximum_fusion.1
  2.0 2.4 %collective-permute-start.1 = (f32[33,8,2,128]{3,2,1,0:T(2,128)S(1)}, f32[33,8,2,128]{3,2,1,0:T(2,128)S(1)}, u32[]{:S(2)}, u32[]{:S(2)}) collective-permute-start(f32[33,8,2,128]{3,2,1,0:T(2,128)S(1)} %get-tuple-element.9), channel_id=1, source_target_pairs={{16,0},{32,16},{48,32},{64,48},{80,64},{96,80},{112,96},{128,112},... | collective-permute-start | bytes 811016 | tf_op jit(solution)/shard_map/ppermute | solution.py:18
  4.3 3.5 %collective-permute-start = (f32[33,8,2,128]{3,2,1,0:T(2,128)S(1)}, f32[33,8,2,128]{3,2,1,0:T(2,128)S(1)}, u32[]{:S(2)}, u32[]{:S(2)}) collective-permute-start(f32[33,8,2,128]{3,2,1,0:T(2,128)S(1)} %get-tuple-element.10), channel_id=1, source_target_pairs={{0,16},{16,32},{32,48},{48,64},{64,80},{80,96},{96,112},{112,128},... | collective-permute-start | bytes 811016 | tf_op jit(solution)/shard_map/ppermute | solution.py:17
  8.5 3.6 %collective-permute-done.1 = f32[33,8,2,128]{3,2,1,0:T(2,128)S(1)} collective-permute-done((f32[33,8,2,128]{3,2,1,0:T(2,128)S(1)}, f32[33,8,2,128]{3,2,1,0:T(2,128)S(1)}, u32[]{:S(2)}, u32[]{:S(2)}) %collective-permute-start.1) | collective-permute-done | bytes 270368 | tf_op jit(solution)/shard_map/ppermute | solution.py:18
  12.1 4.1 %collective-permute-done = f32[33,8,2,128]{3,2,1,0:T(2,128)S(1)} collective-permute-done((f32[33,8,2,128]{3,2,1,0:T(2,128)S(1)}, f32[33,8,2,128]{3,2,1,0:T(2,128)S(1)}, u32[]{:S(2)}, u32[]{:S(2)}) %collective-permute-start) | collective-permute-done | bytes 270368 | tf_op jit(solution)/shard_map/ppermute | solution.py:17
  17.5 2.9 %fusion.22 = (f32[33,8,20,2]{3,2,1,0:T(8,128)}, f32[33,8,20,2]{3,2,1,0:T(8,128)S(1)}) fusion(f32[33,8,20,128]{3,2,1,0:T(8,128)S(1)} %pad_maximum_fusion), kind=kLoop, calls=%fused_computation.36 | loop fusion | bytes 168960 | tf_op jit(solution)/shard_map/slice | solution.py:142
  20.3 5.1 %copy.13 = f32[33,8,20,2]{0,1,3,2:T(8,128)} copy(f32[33,8,20,2]{3,2,1,0:T(8,128)} %get-tuple-element.6) | data formatting | bytes 84480 | tf_op jit(solution)/shard_map/slice | solution.py:142
  25.4 3.7 %copy.11 = f32[33,8,20,2]{0,1,3,2:T(8,128)} copy(f32[33,8,20,2]{3,2,1,0:T(8,128)S(1)} %get-tuple-element.8) | data formatting | bytes 84480 | tf_op jit(solution)/shard_map/slice | solution.py:142
  29.1 1.3 collective-permute-start.2
  30.4 1.5 collective-permute-start.3
  34.5 1.7 slice.70.xl_ref
  36.3 1.2 copy.35
  38.4 1.2 copy.36
  40.2 4.3 %copy.34.yr_ref = f32[32,8,20,2]{3,2,1,0:T(8,128)} copy(f32[32,8,20,2]{0,1,3,2:T(8,128)S(1)} %bitcast.55) | data formatting | bytes 81920
  44.6 4.3 %copy.33.yl_ref = f32[32,8,20,2]{3,2,1,0:T(8,128)} copy(f32[32,8,20,2]{0,1,3,2:T(8,128)S(1)} %bitcast.54) | data formatting | bytes 81920
  48.9 27.9 %shard_map.28 = f32[32,8,16,128]{3,2,1,0:T(8,128)} custom-call(s32[4]{0:T(128)} %add_convert_fusion.flags, f32[32,8,16,128]{3,2,1,0:T(8,128)} %f_ref.1, f32[8,16,128]{2,1,0:T(8,128)} %k_ref.1, f32[32,8,2,128]{3,2,1,0:T(2,128)} %slice.70.xl_ref, f32[32,8,2,128]{3,2,1,0:T(2,128)} %slice.71.xh_ref, f32[8,1,128]{2,1,0:T(1,128)} %slice.73.kxl_ref, ...), custom_call_target="tpu_custom_call" | custom-call | flops 20971520 | bytes 4194304 | tf_op jit(solution)/shard_map/pallas_call | solution.py:86
  76.8 6.3 %fusion.6 = f32[32,32]{1,0:T(8,128)S(1)} fusion(f32[32,8,16,128]{3,2,1,0:T(8,128)} %shard_map.28), kind=kOutput, calls=%fused_computation.8 | convolution fusion | flops 201326592 | bytes 2101248 | tf_op jit(solution)/shard_map/czxy,dzxy->cd/dot_general | solution.py:128
  83.1 26.8 %all-gather = f32[512,32]{1,0:T(8,128)S(1)} all-gather(f32[32,32]{1,0:T(8,128)S(1)} %fusion.6), channel_id=2, replica_groups=mesh['gx'=32,'gy'=16] {'gy'}, dimensions={0}, use_global_device_ids=true | all-gather | bytes 69632 | tf_op jit(solution)/shard_map/all_gather | solution.py:93
  110.1 5.7 %collective-permute-start.4 = (f32[32,32]{0,1:T(8,128)S(1)}, f32[32,32]{0,1:T(8,128)S(1)}, u32[]{:S(2)}, u32[]{:S(2)}) collective-permute-start(f32[32,32]{0,1:T(8,128)S(1)} %copy.20), channel_id=1, source_target_pairs={{0,16},{16,0},{32,48},{48,32},{64,80},{80,64},{96,112},{112,96},{1... | collective-permute-start | bytes 12296 | tf_op jit(solution)/shard_map/ppermute | solution.py:95
  115.8 1.7 collective-permute-done.4
  117.5 1.9 collective-permute-start.5
  119.4 4.6 %collective-permute-done.5 = f32[32,32]{0,1:T(8,128)S(1)} collective-permute-done((f32[32,32]{0,1:T(8,128)S(1)}, f32[32,32]{0,1:T(8,128)S(1)}, u32[]{:S(2)}, u32[]{:S(2)}) %collective-permute-start.5) | collective-permute-done | bytes 4128 | tf_op jit(solution)/shard_map/ppermute | solution.py:95
  124.0 3.1 %collective-permute-start.6 = (f32[32,32]{0,1:T(8,128)S(1)}, f32[32,32]{0,1:T(8,128)S(1)}, u32[]{:S(2)}, u32[]{:S(2)}) collective-permute-start(f32[32,32]{0,1:T(8,128)S(1)} %add.39), channel_id=1, source_target_pairs={{0,112},{16,96},{32,80},{48,64},{64,48},{80,32},{96,16},{112,0},{1... | collective-permute-start | bytes 12296 | tf_op jit(solution)/shard_map/ppermute | solution.py:95
  127.2 5.5 %collective-permute-done.6 = f32[32,32]{0,1:T(8,128)S(1)} collective-permute-done((f32[32,32]{0,1:T(8,128)S(1)}, f32[32,32]{0,1:T(8,128)S(1)}, u32[]{:S(2)}, u32[]{:S(2)}) %collective-permute-start.6) | collective-permute-done | bytes 4128 | tf_op jit(solution)/shard_map/ppermute | solution.py:95
  132.7 2.4 %collective-permute-start.7 = (f32[32,32]{0,1:T(8,128)S(1)}, f32[32,32]{0,1:T(8,128)S(1)}, u32[]{:S(2)}, u32[]{:S(2)}) collective-permute-start(f32[32,32]{0,1:T(8,128)S(1)} %add.40), channel_id=1, source_target_pairs={{0,128},{16,144},{32,160},{48,176},{64,192},{80,208},{96,224},{112... | collective-permute-start | bytes 12296 | tf_op jit(solution)/shard_map/ppermute | solution.py:95
  135.1 3.2 %collective-permute-done.7 = f32[32,32]{0,1:T(8,128)S(1)} collective-permute-done((f32[32,32]{0,1:T(8,128)S(1)}, f32[32,32]{0,1:T(8,128)S(1)}, u32[]{:S(2)}, u32[]{:S(2)}) %collective-permute-start.7) | collective-permute-done | bytes 4128 | tf_op jit(solution)/shard_map/ppermute | solution.py:95
  138.3 2.1 collective-permute-start.8
  140.4 4.7 %collective-permute-done.8 = f32[32,32]{0,1:T(8,128)S(1)} collective-permute-done((f32[32,32]{0,1:T(8,128)S(1)}, f32[32,32]{0,1:T(8,128)S(1)}, u32[]{:S(2)}, u32[]{:S(2)}) %collective-permute-start.8) | collective-permute-done | bytes 4128 | tf_op jit(solution)/shard_map/ppermute | solution.py:95
  145.2 2.9 %cholesky.44 = f32[32,32]{1,0:T(8,128)S(1)} custom-call(f32[32,32]{1,0:T(8,128)S(1)} %fusion.19), custom_call_target="Cholesky" | custom-call | tf_op jit(solution)/shard_map/jit(cholesky)/cholesky | solution.py:132
  149.5 2.4 %custom-call.6 = f32[1,32,32]{1,2,0:T(8,128)S(1)} custom-call(f32[1,32,32]{2,1,0:T(8,128)S(1)} %fusion.14), custom_call_target="InvertDiagBlocksLowerTriangular" | custom-call | tf_op jit(solution)/shard_map/triangular_solve/custom-call.0 | solution.py:134
  152.2 3.0 %fusion.2 = f32[32,8,16,128]{3,0,2,1:T(8,128)S(1)} fusion(f32[32,32,1,1]{1,0,3,2:T(8,128)S(1)} %convolution_bitcast_fusion.1, f32[32,8,16,128]{3,2,1,0:T(8,128)S(1)} %copy-done.1), kind=kOutput, calls=%fused_computation.3 | convolution fusion | flops 201326592 | bytes 4198400 | tf_op jit(solution)/shard_map/cd,dzxy->czxy/dot_general | solution.py:152
  155.2 1.3 copy-done.2
  156.5 1.8 fusion.9
  158.3 14.9 %all-gather.1 = f32[512,32]{1,0:T(8,128)S(1)} all-gather(f32[32,32]{1,0:T(8,128)S(1)} %fusion.9), channel_id=3, replica_groups=mesh['gx'=32,'gy'=16] {'gy'}, dimensions={0}, use_global_device_ids=true | all-gather | bytes 69632 | tf_op jit(solution)/shard_map/all_gather | solution.py:93
  173.2 2.1 collective-permute-start.9
  175.4 3.5 %collective-permute-done.9 = f32[32,32]{0,1:T(8,128)S(1)} collective-permute-done((f32[32,32]{0,1:T(8,128)S(1)}, f32[32,32]{0,1:T(8,128)S(1)}, u32[]{:S(2)}, u32[]{:S(2)}) %collective-permute-start.9) | collective-permute-done | bytes 4128 | tf_op jit(solution)/shard_map/ppermute | solution.py:95
  178.9 1.9 collective-permute-start.10
  180.8 4.6 %collective-permute-done.10 = f32[32,32]{0,1:T(8,128)S(1)} collective-permute-done((f32[32,32]{0,1:T(8,128)S(1)}, f32[32,32]{0,1:T(8,128)S(1)}, u32[]{:S(2)}, u32[]{:S(2)}) %collective-permute-start.10) | collective-permute-done | bytes 4128 | tf_op jit(solution)/shard_map/ppermute | solution.py:95
  185.4 3.1 %collective-permute-start.11 = (f32[32,32]{0,1:T(8,128)S(1)}, f32[32,32]{0,1:T(8,128)S(1)}, u32[]{:S(2)}, u32[]{:S(2)}) collective-permute-start(f32[32,32]{0,1:T(8,128)S(1)} %add.44), channel_id=1, source_target_pairs={{0,112},{16,96},{32,80},{48,64},{64,48},{80,32},{96,16},{112,0},{1... | collective-permute-start | bytes 12296 | tf_op jit(solution)/shard_map/ppermute | solution.py:95
  188.5 5.5 %collective-permute-done.11 = f32[32,32]{0,1:T(8,128)S(1)} collective-permute-done((f32[32,32]{0,1:T(8,128)S(1)}, f32[32,32]{0,1:T(8,128)S(1)}, u32[]{:S(2)}, u32[]{:S(2)}) %collective-permute-start.11) | collective-permute-done | bytes 4128 | tf_op jit(solution)/shard_map/ppermute | solution.py:95
  194.0 1.9 collective-permute-start.12
  195.9 3.7 %collective-permute-done.12 = f32[32,32]{0,1:T(8,128)S(1)} collective-permute-done((f32[32,32]{0,1:T(8,128)S(1)}, f32[32,32]{0,1:T(8,128)S(1)}, u32[]{:S(2)}, u32[]{:S(2)}) %collective-permute-start.12) | collective-permute-done | bytes 4128 | tf_op jit(solution)/shard_map/ppermute | solution.py:95
  199.7 1.9 collective-permute-start.13
  201.6 4.9 %collective-permute-done.13 = f32[32,32]{0,1:T(8,128)S(1)} collective-permute-done((f32[32,32]{0,1:T(8,128)S(1)}, f32[32,32]{0,1:T(8,128)S(1)}, u32[]{:S(2)}, u32[]{:S(2)}) %collective-permute-start.13) | collective-permute-done | bytes 4128 | tf_op jit(solution)/shard_map/ppermute | solution.py:95
  206.6 2.9 %cholesky.55 = f32[32,32]{1,0:T(8,128)S(1)} custom-call(f32[32,32]{1,0:T(8,128)S(1)} %fusion.17), custom_call_target="Cholesky" | custom-call | tf_op jit(solution)/shard_map/jit(cholesky)/cholesky | solution.py:132
  210.8 2.4 %custom-call.7 = f32[1,32,32]{1,2,0:T(8,128)S(1)} custom-call(f32[1,32,32]{2,1,0:T(8,128)S(1)} %fusion.15), custom_call_target="InvertDiagBlocksLowerTriangular" | custom-call | tf_op jit(solution)/shard_map/triangular_solve/custom-call.0 | solution.py:134
  213.5 3.5 %convolution_multiply_fusion = f32[32,8,16,128]{3,0,2,1:T(8,128)S(1)} fusion(f32[32,32,1,1]{1,0,3,2:T(8,128)S(1)} %convolution_bitcast_fusion, f32[32,8,16,128]{3,0,2,1:T(8,128)} %copy-done.2), kind=kOutput, calls=%fused_computation.7 | convolution fusion | flops 201850880 | bytes 4198400 | tf_op jit(solution)/shard_map/cd,dzxy->czxy/dot_general | solution.py:155
  217.0 2.5 %copy.28 = f32[32,8,16,128]{3,2,1,0:T(8,128)} copy(f32[32,8,16,128]{3,0,2,1:T(8,128)S(1)} %convolution_multiply_fusion) | data formatting | bytes 4194304 | tf_op jit(solution)/shard_map/mul | solution.py:156
  (48 shorter events, 9.6 us)
Async XLA Ops:
  0.0 16.9 %copy-start = (f32[32,8,16,128]{3,2,1,0:T(8,128)S(1)}, f32[32,8,16,128]{3,2,1,0:T(8,128)}, u32[]{:S(2)}) copy-start(f32[32,8,16,128]{3,2,1,0:T(8,128)} %f_ref.1) | copy-start | bytes 6291460
  0.0 16.9 %copy-start.4 = (f32[8,16,128]{2,1,0:T(8,128)S(1)}, f32[8,16,128]{2,1,0:T(8,128)}, u32[]{:S(2)}) copy-start(f32[8,16,128]{2,1,0:T(8,128)} %k_ref.1) | copy-start | bytes 196612
  2.0 10.1 %collective-permute-start.1 = (f32[33,8,2,128]{3,2,1,0:T(2,128)S(1)}, f32[33,8,2,128]{3,2,1,0:T(2,128)S(1)}, u32[]{:S(2)}, u32[]{:S(2)}) collective-permute-start(f32[33,8,2,128]{3,2,1,0:T(2,128)S(1)} %get-tuple-element.9), channel_id=1, source_target_pairs={{16,0},{32,16},{48,32},{64,48},{80,64},{96,80},{112,96},{128,112},... | collective-permute-start | bytes 811016 | tf_op jit(solution)/shard_map/ppermute | solution.py:18
  4.3 11.8 %collective-permute-start = (f32[33,8,2,128]{3,2,1,0:T(2,128)S(1)}, f32[33,8,2,128]{3,2,1,0:T(2,128)S(1)}, u32[]{:S(2)}, u32[]{:S(2)}) collective-permute-start(f32[33,8,2,128]{3,2,1,0:T(2,128)S(1)} %get-tuple-element.10), channel_id=1, source_target_pairs={{0,16},{16,32},{32,48},{48,64},{64,80},{80,96},{96,112},{112,128},... | collective-permute-start | bytes 811016 | tf_op jit(solution)/shard_map/ppermute | solution.py:17
  16.2 0.7 copy-start.3
  29.1 7.1 %collective-permute-start.2 = (f32[33,8,20,2]{0,1,3,2:T(8,128)}, f32[33,8,20,2]{0,1,3,2:T(8,128)S(1)}, u32[]{:S(2)}, u32[]{:S(2)}) collective-permute-start(f32[33,8,20,2]{0,1,3,2:T(8,128)} %copy.11), channel_id=1, source_target_pairs={{0,1},{1,2},{2,3},{3,4},{4,5},{5,6},{6,7},{7,8},{8,9},{9,10},{10,1... | collective-permute-start | bytes 126728 | tf_op jit(solution)/shard_map/ppermute | solution.py:17
  30.4 7.9 %collective-permute-start.3 = (f32[33,8,20,2]{0,1,3,2:T(8,128)}, f32[33,8,20,2]{0,1,3,2:T(8,128)S(1)}, u32[]{:S(2)}, u32[]{:S(2)}) collective-permute-start(f32[33,8,20,2]{0,1,3,2:T(8,128)} %copy.13), channel_id=1, source_target_pairs={{1,0},{2,1},{3,2},{4,3},{5,4},{6,5},{7,6},{8,7},{9,8},{10,9},{11,1... | collective-permute-start | bytes 126728 | tf_op jit(solution)/shard_map/ppermute | solution.py:18
  76.8 75.4 %copy-start.1 = (f32[32,8,16,128]{3,2,1,0:T(8,128)S(1)}, f32[32,8,16,128]{3,2,1,0:T(8,128)}, u32[]{:S(2)}) copy-start(f32[32,8,16,128]{3,2,1,0:T(8,128)} %shard_map.28) | copy-start | bytes 6291460
  110.1 7.5 %collective-permute-start.4 = (f32[32,32]{0,1:T(8,128)S(1)}, f32[32,32]{0,1:T(8,128)S(1)}, u32[]{:S(2)}, u32[]{:S(2)}) collective-permute-start(f32[32,32]{0,1:T(8,128)S(1)} %copy.20), channel_id=1, source_target_pairs={{0,16},{16,0},{32,48},{48,32},{64,80},{80,64},{96,112},{112,96},{1... | collective-permute-start | bytes 12296 | tf_op jit(solution)/shard_map/ppermute | solution.py:95
  117.5 6.5 %collective-permute-start.5 = (f32[32,32]{0,1:T(8,128)S(1)}, f32[32,32]{0,1:T(8,128)S(1)}, u32[]{:S(2)}, u32[]{:S(2)}) collective-permute-start(f32[32,32]{0,1:T(8,128)S(1)} %add.38), channel_id=1, source_target_pairs={{0,32},{16,48},{32,0},{48,16},{64,96},{80,112},{96,64},{112,80},{1... | collective-permute-start | bytes 12296 | tf_op jit(solution)/shard_map/ppermute | solution.py:95
  124.0 8.6 %collective-permute-start.6 = (f32[32,32]{0,1:T(8,128)S(1)}, f32[32,32]{0,1:T(8,128)S(1)}, u32[]{:S(2)}, u32[]{:S(2)}) collective-permute-start(f32[32,32]{0,1:T(8,128)S(1)} %add.39), channel_id=1, source_target_pairs={{0,112},{16,96},{32,80},{48,64},{64,48},{80,32},{96,16},{112,0},{1... | collective-permute-start | bytes 12296 | tf_op jit(solution)/shard_map/ppermute | solution.py:95
  132.7 5.6 %collective-permute-start.7 = (f32[32,32]{0,1:T(8,128)S(1)}, f32[32,32]{0,1:T(8,128)S(1)}, u32[]{:S(2)}, u32[]{:S(2)}) collective-permute-start(f32[32,32]{0,1:T(8,128)S(1)} %add.40), channel_id=1, source_target_pairs={{0,128},{16,144},{32,160},{48,176},{64,192},{80,208},{96,224},{112... | collective-permute-start | bytes 12296 | tf_op jit(solution)/shard_map/ppermute | solution.py:95
  138.3 6.8 %collective-permute-start.8 = (f32[32,32]{0,1:T(8,128)S(1)}, f32[32,32]{0,1:T(8,128)S(1)}, u32[]{:S(2)}, u32[]{:S(2)}) collective-permute-start(f32[32,32]{0,1:T(8,128)S(1)} %add.41), channel_id=1, source_target_pairs={{0,384},{16,400},{32,416},{48,432},{64,448},{80,464},{96,480},{112... | collective-permute-start | bytes 12296 | tf_op jit(solution)/shard_map/ppermute | solution.py:95
  155.2 1.3 copy-start.2
  173.2 5.6 %collective-permute-start.9 = (f32[32,32]{0,1:T(8,128)S(1)}, f32[32,32]{0,1:T(8,128)S(1)}, u32[]{:S(2)}, u32[]{:S(2)}) collective-permute-start(f32[32,32]{0,1:T(8,128)S(1)} %copy.26), channel_id=1, source_target_pairs={{0,16},{16,0},{32,48},{48,32},{64,80},{80,64},{96,112},{112,96},{1... | collective-permute-start | bytes 12296 | tf_op jit(solution)/shard_map/ppermute | solution.py:95
  178.9 6.5 %collective-permute-start.10 = (f32[32,32]{0,1:T(8,128)S(1)}, f32[32,32]{0,1:T(8,128)S(1)}, u32[]{:S(2)}, u32[]{:S(2)}) collective-permute-start(f32[32,32]{0,1:T(8,128)S(1)} %add.43), channel_id=1, source_target_pairs={{0,32},{16,48},{32,0},{48,16},{64,96},{80,112},{96,64},{112,80},{1... | collective-permute-start | bytes 12296 | tf_op jit(solution)/shard_map/ppermute | solution.py:95
  185.4 8.6 %collective-permute-start.11 = (f32[32,32]{0,1:T(8,128)S(1)}, f32[32,32]{0,1:T(8,128)S(1)}, u32[]{:S(2)}, u32[]{:S(2)}) collective-permute-start(f32[32,32]{0,1:T(8,128)S(1)} %add.44), channel_id=1, source_target_pairs={{0,112},{16,96},{32,80},{48,64},{64,48},{80,32},{96,16},{112,0},{1... | collective-permute-start | bytes 12296 | tf_op jit(solution)/shard_map/ppermute | solution.py:95
  194.0 5.6 %collective-permute-start.12 = (f32[32,32]{0,1:T(8,128)S(1)}, f32[32,32]{0,1:T(8,128)S(1)}, u32[]{:S(2)}, u32[]{:S(2)}) collective-permute-start(f32[32,32]{0,1:T(8,128)S(1)} %add.45), channel_id=1, source_target_pairs={{0,128},{16,144},{32,160},{48,176},{64,192},{80,208},{96,224},{112... | collective-permute-start | bytes 12296 | tf_op jit(solution)/shard_map/ppermute | solution.py:95
  199.7 6.8 %collective-permute-start.13 = (f32[32,32]{0,1:T(8,128)S(1)}, f32[32,32]{0,1:T(8,128)S(1)}, u32[]{:S(2)}, u32[]{:S(2)}) collective-permute-start(f32[32,32]{0,1:T(8,128)S(1)} %add.46), channel_id=1, source_target_pairs={{0,384},{16,400},{32,416},{48,432},{64,448},{80,464},{96,480},{112... | collective-permute-start | bytes 12296 | tf_op jit(solution)/shard_map/ppermute | solution.py:95

commit v5 on v3

--- a/solution.py
+++ b/solution.py
@@ -44,7 +44,9 @@
 
 
 def butterfly_sum(value):
-    value = jnp.sum(lax.all_gather(value, "gy"), axis=0)
+    count = lax.axis_size("gy")
+    copies = jnp.broadcast_to(value[None], (count,) + value.shape)
+    value = jnp.sum(lax.all_to_all(copies, "gy", 0, 0, tiled=True), axis=0)
     for partner in gx_partners(lax.axis_size("gx")):
         value = value + lax.ppermute(value, "gx", [(i, partner(i)) for i in range(len(partner.table))])
     return value

time: 196 us -> 190 us (0.969)
  blocking collectives: 41.1 us -> 31.9 us
    all_gather x2 -> x0, blocking collectives: 41.1 us -> none  [butterfly_sum(): value = jnp.sum(lax.all_gather(value, 'gy'), axis=0)]
    all_to_all x0 -> x2, blocking collectives: none -> 31.9 us  [butterfly_sum(): value = jnp.sum(lax.all_to_all(copies, 'gy', 0, 0, tiled=True), axis=0)]
    unnamed x10 -> x14, local copies, waits for them, and re-layouts: 5.13 us -> 5.68 us
where the time goes in v5:
time: 190 us; the launch traced here: 189 us
  starting transfers between devices  48.5 us (26%)
  waiting for transfers between devices  36.4 us (19%)
  blocking collectives  31.9 us (17%)
  other arithmetic  31.4 us (17%)
  local copies, waits for them, and re-layouts  28.6 us (15%)
  matrix products  11.5 us (6%)
    ppermute x10, starting transfers between devices, butterfly_sum(): lax.ppermute(value, 'gx', [(i, partner(i)) for i in range(len(partner.tab...  36.9 us
    all_to_all x2, blocking collectives, butterfly_sum(): value = jnp.sum(lax.all_to_all(copies, 'gy', 0, 0, tiled=True), axis=0)  31.9 us
    ppermute x10, waiting for transfers between devices, butterfly_sum(): lax.ppermute(value, 'gx', [(i, partner(i)) for i in range(len(partner.tab...  31.5 us
    slice x3, local copies, waits for them, and re-layouts, extend(): left, right = shifted_in(block[..., -width:], block[..., :width], 'gy')  9.95 us
    another operation x6, other arithmetic, inverse_factor(): factor = jnp.linalg.cholesky(gram_matrix)  7.18 us
    select_n x1, other arithmetic, body(): once = jnp.where(inside_mask(x_cells, y_cells), once, 0.0)  7.04 us
    concatenate x1, other arithmetic, extend(): return jnp.concatenate([left, block, right], axis=3)  6.97 us
    ppermute x2, starting transfers between devices, shifted_in(): from_above = lax.ppermute(upper_part, axis, backward)  6.81 us
  transfers between devices with their start and end apart: 14, of which 13 were waited for; matrix products, arithmetic and copies ran while one was open for 4% of the time, Pallas kernels for 0%

profile of v5, /device:TPU:8, one launch (start us, length us, event | category | flops | bytes accessed | tf_op | source)
XLA Modules:
  0.0 188.8 jit_solution(15265124540348262658)
XLA Ops:
  0.0 2.5 %copy.30 = f32[32,8,16,128]{3,1,2,0:T(8,128)S(1)} copy(f32[32,8,16,128]{3,2,1,0:T(8,128)} %param.5) | data formatting | bytes 4194304 | tf_op args[0]
  2.6 3.5 %collective-permute-start = (f32[33,8,2,128]{3,1,2,0:T(8,128)S(1)}, f32[33,8,2,128]{3,1,2,0:T(8,128)S(1)}, u32[]{:S(2)}, u32[]{:S(2)}) collective-permute-start(f32[33,8,2,128]{3,1,2,0:T(8,128)S(1)} %get-tuple-element.9), channel_id=1, source_target_pairs={{0,16},{16,32},{32,48},{48,64},{64,80},{80,96},{96,112},{112,128},... | collective-permute-start | bytes 811016 | tf_op jit(solution)/shard_map/ppermute | solution.py:15
  6.1 5.5 %collective-permute-start.1 = (f32[33,8,2,128]{3,1,2,0:T(8,128)S(1)}, f32[33,8,2,128]{3,1,2,0:T(8,128)S(1)}, u32[]{:S(2)}, u32[]{:S(2)}) collective-permute-start(f32[33,8,2,128]{3,1,2,0:T(8,128)S(1)} %get-tuple-element.10), channel_id=1, source_target_pairs={{16,0},{32,16},{48,32},{64,48},{80,64},{96,80},{112,96},{128,112},... | collective-permute-start | bytes 811016 | tf_op jit(solution)/shard_map/ppermute | solution.py:16
  11.7 2.4 %collective-permute-done = f32[33,8,2,128]{3,1,2,0:T(8,128)S(1)} collective-permute-done((f32[33,8,2,128]{3,1,2,0:T(8,128)S(1)}, f32[33,8,2,128]{3,1,2,0:T(8,128)S(1)}, u32[]{:S(2)}, u32[]{:S(2)}) %collective-permute-start) | collective-permute-done | bytes 270368 | tf_op jit(solution)/shard_map/ppermute | solution.py:15
  14.1 1.8 collective-permute-done.1
  16.2 3.3 %fusion.31 = (f32[33,8,20,2]{3,1,2,0:T(8,128)}, f32[33,8,20,2]{3,1,2,0:T(8,128)}) fusion(f32[33,8,20,128]{3,1,2,0:T(8,128)S(1)} %pad_maximum_fusion.9), kind=kLoop, calls=%fused_computation.66 | loop fusion | bytes 168960 | tf_op jit(solution)/shard_map/slice | solution.py:23
  19.5 3.3 %copy.31 = f32[33,8,20,2]{0,1,3,2:T(8,128)S(1)} copy(f32[33,8,20,2]{3,1,2,0:T(8,128)} %get-tuple-element.6) | data formatting | bytes 84480 | tf_op jit(solution)/shard_map/slice | solution.py:23
  22.8 1.3 collective-permute-start.2
  24.1 3.3 %copy.32 = f32[33,8,20,2]{0,1,3,2:T(8,128)S(1)} copy(f32[33,8,20,2]{3,1,2,0:T(8,128)} %get-tuple-element.8) | data formatting | bytes 84480 | tf_op jit(solution)/shard_map/slice | solution.py:23
  27.4 1.3 collective-permute-start.3
  28.8 3.8 %copy.33 = f32[33,8,20,2]{3,1,2,0:T(8,128)} copy(f32[33,8,20,2]{0,1,3,2:T(8,128)S(1)} %collective-permute-done.2) | data formatting | bytes 84480 | tf_op jit(solution)/shard_map/ppermute | solution.py:15
  33.3 3.8 %copy.34 = f32[33,8,20,2]{3,1,2,0:T(8,128)} copy(f32[33,8,20,2]{0,1,3,2:T(8,128)S(1)} %collective-permute-done.3) | data formatting | bytes 84480 | tf_op jit(solution)/shard_map/ppermute | solution.py:16
  37.1 7.0 %pad_maximum_fusion = f32[33,8,20,132]{3,1,2,0:T(8,128)S(1)} fusion(f32[33,8,20,2]{3,1,2,0:T(8,128)} %copy.34, f32[33,8,2,128]{3,1,2,0:T(8,128)S(1)} %collective-permute-done.1, f32[1,8,16,128]{3,1,2,0:T(8,128)S(1)} %bitcast.44, f32[32,8,16,128]{3,1,2,0:T(8,128)S(1)} %copy.30, f32[33,8,2,128]{3,1,2,0:T(8,128)S(1)} %collective-permute-done, ...), kind=kLoop, calls=%fused_computation.2 | loop fusion | flops 3484800 | bytes 5575680 | tf_op jit(solution)/shard_map/concatenate | solution.py:24
  44.1 1.3 slice.97
  46.9 7.0 %fusion.3 = f32[32,8,18,130]{3,1,2,0:T(8,128)S(1)} fusion(f32[32,8,18,130]{3,1,2,0:T(8,128)S(1)} %slice.97, f32[33,8,20,2]{3,1,2,0:T(8,128)S(1)} %copy-done, f32[33,8,2,128]{3,1,2,0:T(8,128)S(1)} %collective-permute-done.1, f32[33,8,2,128]{3,1,2,0:T(8,128)S(1)} %collective-permute-done, f32[1,8,16,128]{3,1,2,0:T(8,128)S(1)} %bitcast.46, ...), kind=kLoop, calls=%fused_computation.8 | loop fusion | flops 9584640 | bytes 12449700 | tf_op jit(solution)/shard_map/jit(_where)/select_n | solution.py:99
  54.6 1.7 fusion.8
  56.3 1.3 copy-done.2
  57.6 2.8 %fusion.15 = f32[32,32]{1,0:T(8,128)S(1)} fusion(f32[32,8,16,128]{3,1,2,0:T(8,128)S(1)} %fusion.8), kind=kOutput, calls=%fused_computation.34 | convolution fusion | flops 201326592 | bytes 2101248 | tf_op jit(solution)/shard_map/czxy,dzxy->cd/dot_general | solution.py:84
  60.6 21.5 %all_to_all.10 = f32[16,1,1024]{2,1,0:T(1,128)S(1)} all-to-all(f32[16,1,1024]{2,1,0:T(1,128)S(1)} %reshape.26), channel_id=1, replica_groups=mesh['gx'=32,'gy'=16] {'gy'}, dimensions={0} | all-to-all | bytes 131072 | tf_op jit(solution)/shard_map/all_to_all | solution.py:49
  83.8 2.3 %collective-permute-start.4 = (f32[32,32]{0,1:T(8,128)S(1)}, f32[32,32]{0,1:T(8,128)S(1)}, u32[]{:S(2)}, u32[]{:S(2)}) collective-permute-start(f32[32,32]{0,1:T(8,128)S(1)} %copy.40), channel_id=1, source_target_pairs={{0,16},{16,0},{32,48},{48,32},{64,80},{80,64},{96,112},{112,96},{1... | collective-permute-start | bytes 12296 | tf_op jit(solution)/shard_map/ppermute | solution.py:51
  86.2 3.3 %collective-permute-done.4 = f32[32,32]{0,1:T(8,128)S(1)} collective-permute-done((f32[32,32]{0,1:T(8,128)S(1)}, f32[32,32]{0,1:T(8,128)S(1)}, u32[]{:S(2)}, u32[]{:S(2)}) %collective-permute-start.4) | collective-permute-done | bytes 4128 | tf_op jit(solution)/shard_map/ppermute | solution.py:51
  89.5 6.9 %collective-permute-start.5 = (f32[32,32]{0,1:T(8,128)S(1)}, f32[32,32]{0,1:T(8,128)S(1)}, u32[]{:S(2)}, u32[]{:S(2)}) collective-permute-start(f32[32,32]{0,1:T(8,128)S(1)} %add.99), channel_id=1, source_target_pairs={{0,32},{16,48},{32,0},{48,16},{64,96},{80,112},{96,64},{112,80},{1... | collective-permute-start | bytes 12296 | tf_op jit(solution)/shard_map/ppermute | solution.py:51
  96.3 1.7 collective-permute-done.5
  98.0 3.8 %collective-permute-start.6 = (f32[32,32]{0,1:T(8,128)S(1)}, f32[32,32]{0,1:T(8,128)S(1)}, u32[]{:S(2)}, u32[]{:S(2)}) collective-permute-start(f32[32,32]{0,1:T(8,128)S(1)} %add.100), channel_id=1, source_target_pairs={{0,112},{16,96},{32,80},{48,64},{64,48},{80,32},{96,16},{112,0},{1... | collective-permute-start | bytes 12296 | tf_op jit(solution)/shard_map/ppermute | solution.py:51
  101.9 4.8 %collective-permute-done.6 = f32[32,32]{0,1:T(8,128)S(1)} collective-permute-done((f32[32,32]{0,1:T(8,128)S(1)}, f32[32,32]{0,1:T(8,128)S(1)}, u32[]{:S(2)}, u32[]{:S(2)}) %collective-permute-start.6) | collective-permute-done | bytes 4128 | tf_op jit(solution)/shard_map/ppermute | solution.py:51
  106.7 3.4 %collective-permute-start.7 = (f32[32,32]{0,1:T(8,128)S(1)}, f32[32,32]{0,1:T(8,128)S(1)}, u32[]{:S(2)}, u32[]{:S(2)}) collective-permute-start(f32[32,32]{0,1:T(8,128)S(1)} %add.101), channel_id=1, source_target_pairs={{0,128},{16,144},{32,160},{48,176},{64,192},{80,208},{96,224},{112... | collective-permute-start | bytes 12296 | tf_op jit(solution)/shard_map/ppermute | solution.py:51
  110.1 2.2 %collective-permute-done.7 = f32[32,32]{0,1:T(8,128)S(1)} collective-permute-done((f32[32,32]{0,1:T(8,128)S(1)}, f32[32,32]{0,1:T(8,128)S(1)}, u32[]{:S(2)}, u32[]{:S(2)}) %collective-permute-start.7) | collective-permute-done | bytes 4128 | tf_op jit(solution)/shard_map/ppermute | solution.py:51
  112.3 4.9 %collective-permute-start.8 = (f32[32,32]{0,1:T(8,128)S(1)}, f32[32,32]{0,1:T(8,128)S(1)}, u32[]{:S(2)}, u32[]{:S(2)}) collective-permute-start(f32[32,32]{0,1:T(8,128)S(1)} %add.102), channel_id=1, source_target_pairs={{0,384},{16,400},{32,416},{48,432},{64,448},{80,464},{96,480},{112... | collective-permute-start | bytes 12296 | tf_op jit(solution)/shard_map/ppermute | solution.py:51
  117.2 1.9 %collective-permute-done.8 = f32[32,32]{0,1:T(8,128)S(1)} collective-permute-done((f32[32,32]{0,1:T(8,128)S(1)}, f32[32,32]{0,1:T(8,128)S(1)}, u32[]{:S(2)}, u32[]{:S(2)}) %collective-permute-start.8) | collective-permute-done | bytes 4128 | tf_op jit(solution)/shard_map/ppermute | solution.py:51
  119.2 2.9 %cholesky.44 = f32[32,32]{1,0:T(8,128)S(1)} custom-call(f32[32,32]{1,0:T(8,128)S(1)} %fusion.28), custom_call_target="Cholesky" | custom-call | tf_op jit(solution)/shard_map/jit(cholesky)/cholesky | solution.py:88
  123.4 2.4 %custom-call.6 = f32[1,32,32]{1,2,0:T(8,128)S(1)} custom-call(f32[1,32,32]{2,1,0:T(8,128)S(1)} %fusion.23), custom_call_target="InvertDiagBlocksLowerTriangular" | custom-call | tf_op jit(solution)/shard_map/triangular_solve/custom-call.0 | solution.py:90
  126.1 4.5 %fusion.11 = f32[32,8,16,128]{3,0,2,1:T(8,128)S(1)} fusion(f32[32,32,1,1]{1,0,3,2:T(8,128)S(1)} %convolution_bitcast_fusion.1, f32[32,8,16,128]{3,1,2,0:T(8,128)} %copy-done.2), kind=kOutput, calls=%fused_computation.29 | convolution fusion | flops 201326592 | bytes 4198400 | tf_op jit(solution)/shard_map/cd,dzxy->czxy/dot_general | solution.py:102
  130.6 1.8 fusion.18
  132.6 10.4 %all_to_all.11 = f32[16,1,1024]{2,1,0:T(1,128)S(1)} all-to-all(f32[16,1,1024]{2,1,0:T(1,128)S(1)} %reshape.28), channel_id=1, replica_groups=mesh['gx'=32,'gy'=16] {'gy'}, dimensions={0} | all-to-all | bytes 131072 | tf_op jit(solution)/shard_map/all_to_all | solution.py:49
  144.0 1.9 %collective-permute-start.9 = (f32[32,32]{0,1:T(8,128)S(1)}, f32[32,32]{0,1:T(8,128)S(1)}, u32[]{:S(2)}, u32[]{:S(2)}) collective-permute-start(f32[32,32]{0,1:T(8,128)S(1)} %copy.46), channel_id=1, source_target_pairs={{0,16},{16,0},{32,48},{48,32},{64,80},{80,64},{96,112},{112,96},{1... | collective-permute-start | bytes 12296 | tf_op jit(solution)/shard_map/ppermute | solution.py:51
  146.0 3.7 %collective-permute-done.9 = f32[32,32]{0,1:T(8,128)S(1)} collective-permute-done((f32[32,32]{0,1:T(8,128)S(1)}, f32[32,32]{0,1:T(8,128)S(1)}, u32[]{:S(2)}, u32[]{:S(2)}) %collective-permute-start.9) | collective-permute-done | bytes 4128 | tf_op jit(solution)/shard_map/ppermute | solution.py:51
  149.7 3.0 %collective-permute-start.10 = (f32[32,32]{0,1:T(8,128)S(1)}, f32[32,32]{0,1:T(8,128)S(1)}, u32[]{:S(2)}, u32[]{:S(2)}) collective-permute-start(f32[32,32]{0,1:T(8,128)S(1)} %add.104), channel_id=1, source_target_pairs={{0,32},{16,48},{32,0},{48,16},{64,96},{80,112},{96,64},{112,80},{1... | collective-permute-start | bytes 12296 | tf_op jit(solution)/shard_map/ppermute | solution.py:51
  152.7 3.5 %collective-permute-done.10 = f32[32,32]{0,1:T(8,128)S(1)} collective-permute-done((f32[32,32]{0,1:T(8,128)S(1)}, f32[32,32]{0,1:T(8,128)S(1)}, u32[]{:S(2)}, u32[]{:S(2)}) %collective-permute-start.10) | collective-permute-done | bytes 4128 | tf_op jit(solution)/shard_map/ppermute | solution.py:51
  156.2 3.8 %collective-permute-start.11 = (f32[32,32]{0,1:T(8,128)S(1)}, f32[32,32]{0,1:T(8,128)S(1)}, u32[]{:S(2)}, u32[]{:S(2)}) collective-permute-start(f32[32,32]{0,1:T(8,128)S(1)} %add.105), channel_id=1, source_target_pairs={{0,112},{16,96},{32,80},{48,64},{64,48},{80,32},{96,16},{112,0},{1... | collective-permute-start | bytes 12296 | tf_op jit(solution)/shard_map/ppermute | solution.py:51
  160.0 4.8 %collective-permute-done.11 = f32[32,32]{0,1:T(8,128)S(1)} collective-permute-done((f32[32,32]{0,1:T(8,128)S(1)}, f32[32,32]{0,1:T(8,128)S(1)}, u32[]{:S(2)}, u32[]{:S(2)}) %collective-permute-start.11) | collective-permute-done | bytes 4128 | tf_op jit(solution)/shard_map/ppermute | solution.py:51
  164.8 2.2 %collective-permute-start.12 = (f32[32,32]{0,1:T(8,128)S(1)}, f32[32,32]{0,1:T(8,128)S(1)}, u32[]{:S(2)}, u32[]{:S(2)}) collective-permute-start(f32[32,32]{0,1:T(8,128)S(1)} %add.106), channel_id=1, source_target_pairs={{0,128},{16,144},{32,160},{48,176},{64,192},{80,208},{96,224},{112... | collective-permute-start | bytes 12296 | tf_op jit(solution)/shard_map/ppermute | solution.py:51
  167.0 3.4 %collective-permute-done.12 = f32[32,32]{0,1:T(8,128)S(1)} collective-permute-done((f32[32,32]{0,1:T(8,128)S(1)}, f32[32,32]{0,1:T(8,128)S(1)}, u32[]{:S(2)}, u32[]{:S(2)}) %collective-permute-start.12) | collective-permute-done | bytes 4128 | tf_op jit(solution)/shard_map/ppermute | solution.py:51
  170.5 4.7 %collective-permute-start.13 = (f32[32,32]{0,1:T(8,128)S(1)}, f32[32,32]{0,1:T(8,128)S(1)}, u32[]{:S(2)}, u32[]{:S(2)}) collective-permute-start(f32[32,32]{0,1:T(8,128)S(1)} %add.107), channel_id=1, source_target_pairs={{0,384},{16,400},{32,416},{48,432},{64,448},{80,464},{96,480},{112... | collective-permute-start | bytes 12296 | tf_op jit(solution)/shard_map/ppermute | solution.py:51
  175.1 2.1 %collective-permute-done.13 = f32[32,32]{0,1:T(8,128)S(1)} collective-permute-done((f32[32,32]{0,1:T(8,128)S(1)}, f32[32,32]{0,1:T(8,128)S(1)}, u32[]{:S(2)}, u32[]{:S(2)}) %collective-permute-start.13) | collective-permute-done | bytes 4128 | tf_op jit(solution)/shard_map/ppermute | solution.py:51
  177.4 2.9 %cholesky.55 = f32[32,32]{1,0:T(8,128)S(1)} custom-call(f32[32,32]{1,0:T(8,128)S(1)} %fusion.26), custom_call_target="Cholesky" | custom-call | tf_op jit(solution)/shard_map/jit(cholesky)/cholesky | solution.py:88
  181.6 2.4 %custom-call.7 = f32[1,32,32]{1,2,0:T(8,128)S(1)} custom-call(f32[1,32,32]{2,1,0:T(8,128)S(1)} %fusion.24), custom_call_target="InvertDiagBlocksLowerTriangular" | custom-call | tf_op jit(solution)/shard_map/triangular_solve/custom-call.0 | solution.py:90
  184.3 1.9 %convolution_multiply_fusion = f32[32,8,16,128]{3,0,2,1:T(8,128)S(1)} fusion(f32[32,32,1,1]{1,0,3,2:T(8,128)S(1)} %convolution_bitcast_fusion, f32[32,8,16,128]{3,0,2,1:T(8,128)S(1)} %fusion.11), kind=kOutput, calls=%fused_computation.33 | convolution fusion | flops 201850880 | bytes 4198400 | tf_op jit(solution)/shard_map/cd,dzxy->czxy/dot_general | solution.py:105
  186.3 2.5 %copy.48 = f32[32,8,16,128]{3,2,1,0:T(8,128)} copy(f32[32,8,16,128]{3,0,2,1:T(8,128)S(1)} %convolution_multiply_fusion) | data formatting | bytes 4194304 | tf_op jit(solution)/shard_map/mul | solution.py:106
  (55 shorter events, 9.5 us)
Async XLA Ops:
  0.0 2.5 %copy-start.3 = (f32[8,16,128]{2,1,0:T(8,128)S(1)}, f32[8,16,128]{2,1,0:T(8,128)}, u32[]{:S(2)}) copy-start(f32[8,16,128]{2,1,0:T(8,128)} %param.6) | copy-start | bytes 196612
  2.6 11.5 %collective-permute-start = (f32[33,8,2,128]{3,1,2,0:T(8,128)S(1)}, f32[33,8,2,128]{3,1,2,0:T(8,128)S(1)}, u32[]{:S(2)}, u32[]{:S(2)}) collective-permute-start(f32[33,8,2,128]{3,1,2,0:T(8,128)S(1)} %get-tuple-element.9), channel_id=1, source_target_pairs={{0,16},{16,32},{32,48},{48,64},{64,80},{80,96},{96,112},{112,128},... | collective-permute-start | bytes 811016 | tf_op jit(solution)/shard_map/ppermute | solution.py:15
  6.1 9.8 %collective-permute-start.1 = (f32[33,8,2,128]{3,1,2,0:T(8,128)S(1)}, f32[33,8,2,128]{3,1,2,0:T(8,128)S(1)}, u32[]{:S(2)}, u32[]{:S(2)}) collective-permute-start(f32[33,8,2,128]{3,1,2,0:T(8,128)S(1)} %get-tuple-element.10), channel_id=1, source_target_pairs={{16,0},{32,16},{48,32},{64,48},{80,64},{96,80},{112,96},{128,112},... | collective-permute-start | bytes 811016 | tf_op jit(solution)/shard_map/ppermute | solution.py:16
  22.8 6.0 %collective-permute-start.2 = (f32[33,8,20,2]{0,1,3,2:T(8,128)S(1)}, f32[33,8,20,2]{0,1,3,2:T(8,128)S(1)}, u32[]{:S(2)}, u32[]{:S(2)}) collective-permute-start(f32[33,8,20,2]{0,1,3,2:T(8,128)S(1)} %copy.31), channel_id=1, source_target_pairs={{0,1},{1,2},{2,3},{3,4},{4,5},{5,6},{6,7},{7,8},{8,9},{9,10},{10,1... | collective-permute-start | bytes 126728 | tf_op jit(solution)/shard_map/ppermute | solution.py:15
  27.4 5.9 %collective-permute-start.3 = (f32[33,8,20,2]{0,1,3,2:T(8,128)S(1)}, f32[33,8,20,2]{0,1,3,2:T(8,128)S(1)}, u32[]{:S(2)}, u32[]{:S(2)}) collective-permute-start(f32[33,8,20,2]{0,1,3,2:T(8,128)S(1)} %copy.32), channel_id=1, source_target_pairs={{1,0},{2,1},{3,2},{4,3},{5,4},{6,5},{7,6},{8,7},{9,8},{10,9},{11,1... | collective-permute-start | bytes 126728 | tf_op jit(solution)/shard_map/ppermute | solution.py:16
  44.1 1.8 copy-start
  44.1 2.6 %copy-start.1 = (f32[33,8,20,2]{3,1,2,0:T(8,128)S(1)}, f32[33,8,20,2]{3,1,2,0:T(8,128)}, u32[]{:S(2)}) copy-start(f32[33,8,20,2]{3,1,2,0:T(8,128)} %copy.34) | copy-start | bytes 126724
  56.3 1.3 copy-start.2
  83.8 5.6 %collective-permute-start.4 = (f32[32,32]{0,1:T(8,128)S(1)}, f32[32,32]{0,1:T(8,128)S(1)}, u32[]{:S(2)}, u32[]{:S(2)}) collective-permute-start(f32[32,32]{0,1:T(8,128)S(1)} %copy.40), channel_id=1, source_target_pairs={{0,16},{16,0},{32,48},{48,32},{64,80},{80,64},{96,112},{112,96},{1... | collective-permute-start | bytes 12296 | tf_op jit(solution)/shard_map/ppermute | solution.py:51
  89.5 8.6 %collective-permute-start.5 = (f32[32,32]{0,1:T(8,128)S(1)}, f32[32,32]{0,1:T(8,128)S(1)}, u32[]{:S(2)}, u32[]{:S(2)}) collective-permute-start(f32[32,32]{0,1:T(8,128)S(1)} %add.99), channel_id=1, source_target_pairs={{0,32},{16,48},{32,0},{48,16},{64,96},{80,112},{96,64},{112,80},{1... | collective-permute-start | bytes 12296 | tf_op jit(solution)/shard_map/ppermute | solution.py:51
  98.0 8.6 %collective-permute-start.6 = (f32[32,32]{0,1:T(8,128)S(1)}, f32[32,32]{0,1:T(8,128)S(1)}, u32[]{:S(2)}, u32[]{:S(2)}) collective-permute-start(f32[32,32]{0,1:T(8,128)S(1)} %add.100), channel_id=1, source_target_pairs={{0,112},{16,96},{32,80},{48,64},{64,48},{80,32},{96,16},{112,0},{1... | collective-permute-start | bytes 12296 | tf_op jit(solution)/shard_map/ppermute | solution.py:51
  106.7 5.6 %collective-permute-start.7 = (f32[32,32]{0,1:T(8,128)S(1)}, f32[32,32]{0,1:T(8,128)S(1)}, u32[]{:S(2)}, u32[]{:S(2)}) collective-permute-start(f32[32,32]{0,1:T(8,128)S(1)} %add.101), channel_id=1, source_target_pairs={{0,128},{16,144},{32,160},{48,176},{64,192},{80,208},{96,224},{112... | collective-permute-start | bytes 12296 | tf_op jit(solution)/shard_map/ppermute | solution.py:51
  112.3 6.8 %collective-permute-start.8 = (f32[32,32]{0,1:T(8,128)S(1)}, f32[32,32]{0,1:T(8,128)S(1)}, u32[]{:S(2)}, u32[]{:S(2)}) collective-permute-start(f32[32,32]{0,1:T(8,128)S(1)} %add.102), channel_id=1, source_target_pairs={{0,384},{16,400},{32,416},{48,432},{64,448},{80,464},{96,480},{112... | collective-permute-start | bytes 12296 | tf_op jit(solution)/shard_map/ppermute | solution.py:51
  144.0 5.6 %collective-permute-start.9 = (f32[32,32]{0,1:T(8,128)S(1)}, f32[32,32]{0,1:T(8,128)S(1)}, u32[]{:S(2)}, u32[]{:S(2)}) collective-permute-start(f32[32,32]{0,1:T(8,128)S(1)} %copy.46), channel_id=1, source_target_pairs={{0,16},{16,0},{32,48},{48,32},{64,80},{80,64},{96,112},{112,96},{1... | collective-permute-start | bytes 12296 | tf_op jit(solution)/shard_map/ppermute | solution.py:51
  149.7 6.5 %collective-permute-start.10 = (f32[32,32]{0,1:T(8,128)S(1)}, f32[32,32]{0,1:T(8,128)S(1)}, u32[]{:S(2)}, u32[]{:S(2)}) collective-permute-start(f32[32,32]{0,1:T(8,128)S(1)} %add.104), channel_id=1, source_target_pairs={{0,32},{16,48},{32,0},{48,16},{64,96},{80,112},{96,64},{112,80},{1... | collective-permute-start | bytes 12296 | tf_op jit(solution)/shard_map/ppermute | solution.py:51
  156.2 8.6 %collective-permute-start.11 = (f32[32,32]{0,1:T(8,128)S(1)}, f32[32,32]{0,1:T(8,128)S(1)}, u32[]{:S(2)}, u32[]{:S(2)}) collective-permute-start(f32[32,32]{0,1:T(8,128)S(1)} %add.105), channel_id=1, source_target_pairs={{0,112},{16,96},{32,80},{48,64},{64,48},{80,32},{96,16},{112,0},{1... | collective-permute-start | bytes 12296 | tf_op jit(solution)/shard_map/ppermute | solution.py:51
  164.8 5.6 %collective-permute-start.12 = (f32[32,32]{0,1:T(8,128)S(1)}, f32[32,32]{0,1:T(8,128)S(1)}, u32[]{:S(2)}, u32[]{:S(2)}) collective-permute-start(f32[32,32]{0,1:T(8,128)S(1)} %add.106), channel_id=1, source_target_pairs={{0,128},{16,144},{32,160},{48,176},{64,192},{80,208},{96,224},{112... | collective-permute-start | bytes 12296 | tf_op jit(solution)/shard_map/ppermute | solution.py:51
  170.5 6.8 %collective-permute-start.13 = (f32[32,32]{0,1:T(8,128)S(1)}, f32[32,32]{0,1:T(8,128)S(1)}, u32[]{:S(2)}, u32[]{:S(2)}) collective-permute-start(f32[32,32]{0,1:T(8,128)S(1)} %add.107), channel_id=1, source_target_pairs={{0,384},{16,400},{32,416},{48,432},{64,448},{80,464},{96,480},{112... | collective-permute-start | bytes 12296 | tf_op jit(solution)/shard_map/ppermute | solution.py:51

commit v6 on v1

--- a/solution.py
+++ b/solution.py
@@ -46,11 +46,8 @@
 def butterfly_sum(value):
     for axis in ("gy", "gx"):
         count = lax.axis_size(axis)
-        step = 1
-        while step < count:
-            pairs = [(i, i ^ step) for i in range(count)]
-            value = value + lax.ppermute(value, axis, pairs)
-            step *= 2
+        copies = jnp.broadcast_to(value[None], (count,) + value.shape)
+        value = jnp.sum(lax.all_to_all(copies, axis, 0, 0, tiled=True), axis=0)
     return value
 
 

time: 215 us -> 158 us (0.73)
  the two profiles are of different devices: /device:TPU:24 before, /device:TPU:8 now
where the time goes in v6:
time: 158 us
  blocking collectives  66.7 us (42%)
  other arithmetic  33.4 us (21%)
  local copies, waits for them, and re-layouts  29.4 us (19%)
  starting transfers between devices  11.6 us (7%)
  matrix products  11.5 us (7%)
  waiting for transfers between devices  4.9 us (3%)
    all_to_all x4, blocking collectives, butterfly_sum(): value = jnp.sum(lax.all_to_all(copies, axis, 0, 0, tiled=True), axis=0)  66.7 us
    slice x3, local copies, waits for them, and re-layouts, extend(): left, right = shifted_in(block[..., -width:], block[..., :width], 'gy')  9.95 us
    another operation x6, other arithmetic, inverse_factor(): factor = jnp.linalg.cholesky(gram_matrix)  7.19 us
    select_n x1, other arithmetic, body(): once = jnp.where(inside_mask(x_cells, y_cells), once, 0.0)  7.04 us
    concatenate x1, other arithmetic, extend(): return jnp.concatenate([left, block, right], axis=3)  6.97 us
    ppermute x2, starting transfers between devices, shifted_in(): from_above = lax.ppermute(upper_part, axis, backward)  6.81 us
    unnamed x18, local copies, waits for them, and re-layouts  6.52 us
    another operation x4, other arithmetic, inverse_factor(): return lax.linalg.triangular_solve(factor, eye, left_side=True, lower=True)  6.08 us
  transfers between devices with their start and end apart: 4, of which 3 were waited for; matrix products, arithmetic and copies ran while one was open for 5% of the time, Pallas kernels for 0%

profile of v6, /device:TPU:8, one launch (start us, length us, event | category | flops | bytes accessed | tf_op | source)
XLA Modules:
  0.0 157.9 jit_solution(6300386635953308954)
XLA Ops:
  0.0 2.5 %copy.30 = f32[32,8,16,128]{3,1,2,0:T(8,128)S(1)} copy(f32[32,8,16,128]{3,2,1,0:T(8,128)} %param.5) | data formatting | bytes 4194304 | tf_op args[0]
  2.6 3.5 %collective-permute-start = (f32[33,8,2,128]{3,1,2,0:T(8,128)S(1)}, f32[33,8,2,128]{3,1,2,0:T(8,128)S(1)}, u32[]{:S(2)}, u32[]{:S(2)}) collective-permute-start(f32[33,8,2,128]{3,1,2,0:T(8,128)S(1)} %get-tuple-element.9), channel_id=1, source_target_pairs={{0,16},{16,32},{32,48},{48,64},{64,80},{80,96},{96,112},{112,128},... | collective-permute-start | bytes 811016 | tf_op jit(solution)/shard_map/ppermute | solution.py:15
  6.1 5.5 %collective-permute-start.1 = (f32[33,8,2,128]{3,1,2,0:T(8,128)S(1)}, f32[33,8,2,128]{3,1,2,0:T(8,128)S(1)}, u32[]{:S(2)}, u32[]{:S(2)}) collective-permute-start(f32[33,8,2,128]{3,1,2,0:T(8,128)S(1)} %get-tuple-element.10), channel_id=1, source_target_pairs={{16,0},{32,16},{48,32},{64,48},{80,64},{96,80},{112,96},{128,112},... | collective-permute-start | bytes 811016 | tf_op jit(solution)/shard_map/ppermute | solution.py:16
  11.7 2.4 %collective-permute-done = f32[33,8,2,128]{3,1,2,0:T(8,128)S(1)} collective-permute-done((f32[33,8,2,128]{3,1,2,0:T(8,128)S(1)}, f32[33,8,2,128]{3,1,2,0:T(8,128)S(1)}, u32[]{:S(2)}, u32[]{:S(2)}) %collective-permute-start) | collective-permute-done | bytes 270368 | tf_op jit(solution)/shard_map/ppermute | solution.py:15
  14.1 1.8 %collective-permute-done.1 = f32[33,8,2,128]{3,1,2,0:T(8,128)S(1)} collective-permute-done((f32[33,8,2,128]{3,1,2,0:T(8,128)S(1)}, f32[33,8,2,128]{3,1,2,0:T(8,128)S(1)}, u32[]{:S(2)}, u32[]{:S(2)}) %collective-permute-start.1) | collective-permute-done | bytes 270368 | tf_op jit(solution)/shard_map/ppermute | solution.py:16
  15.9 0.2 pad_maximum_fusion.9
  16.2 3.3 %fusion.31 = (f32[33,8,20,2]{3,1,2,0:T(8,128)}, f32[33,8,20,2]{3,1,2,0:T(8,128)}) fusion(f32[33,8,20,128]{3,1,2,0:T(8,128)S(1)} %pad_maximum_fusion.9), kind=kLoop, calls=%fused_computation.66 | loop fusion | bytes 168960 | tf_op jit(solution)/shard_map/slice | solution.py:23
  19.5 3.3 %copy.31 = f32[33,8,20,2]{0,1,3,2:T(8,128)S(1)} copy(f32[33,8,20,2]{3,1,2,0:T(8,128)} %get-tuple-element.6) | data formatting | bytes 84480 | tf_op jit(solution)/shard_map/slice | solution.py:23
  22.8 1.3 collective-permute-start.2
  24.1 3.3 %copy.32 = f32[33,8,20,2]{0,1,3,2:T(8,128)S(1)} copy(f32[33,8,20,2]{3,1,2,0:T(8,128)} %get-tuple-element.8) | data formatting | bytes 84480 | tf_op jit(solution)/shard_map/slice | solution.py:23
  27.4 1.3 collective-permute-start.3
  28.8 3.8 %copy.33 = f32[33,8,20,2]{3,1,2,0:T(8,128)} copy(f32[33,8,20,2]{0,1,3,2:T(8,128)S(1)} %collective-permute-done.2) | data formatting | bytes 84480 | tf_op jit(solution)/shard_map/ppermute | solution.py:15
  32.6 0.7 collective-permute-done.3
  33.3 3.8 %copy.34 = f32[33,8,20,2]{3,1,2,0:T(8,128)} copy(f32[33,8,20,2]{0,1,3,2:T(8,128)S(1)} %collective-permute-done.3) | data formatting | bytes 84480 | tf_op jit(solution)/shard_map/ppermute | solution.py:16
  37.1 7.0 %pad_maximum_fusion = f32[33,8,20,132]{3,1,2,0:T(8,128)S(1)} fusion(f32[33,8,20,2]{3,1,2,0:T(8,128)} %copy.34, f32[33,8,2,128]{3,1,2,0:T(8,128)S(1)} %collective-permute-done.1, f32[1,8,16,128]{3,1,2,0:T(8,128)S(1)} %bitcast.44, f32[32,8,16,128]{3,1,2,0:T(8,128)S(1)} %copy.30, f32[33,8,2,128]{3,1,2,0:T(8,128)S(1)} %collective-permute-done, ...), kind=kLoop, calls=%fused_computation.2 | loop fusion | flops 3484800 | bytes 5575680 | tf_op jit(solution)/shard_map/concatenate | solution.py:24
  44.1 1.3 slice.97
  45.4 0.5 copy-done
  45.9 0.8 copy-done.1
  46.9 7.0 %fusion.3 = f32[32,8,18,130]{3,1,2,0:T(8,128)S(1)} fusion(f32[32,8,18,130]{3,1,2,0:T(8,128)S(1)} %slice.97, f32[33,8,20,2]{3,1,2,0:T(8,128)S(1)} %copy-done, f32[33,8,2,128]{3,1,2,0:T(8,128)S(1)} %collective-permute-done.1, f32[33,8,2,128]{3,1,2,0:T(8,128)S(1)} %collective-permute-done, f32[1,8,16,128]{3,1,2,0:T(8,128)S(1)} %bitcast.46, ...), kind=kLoop, calls=%fused_computation.8 | loop fusion | flops 9584640 | bytes 12449700 | tf_op jit(solution)/shard_map/jit(_where)/select_n | solution.py:70
  54.0 0.6 slice.100
  54.6 1.7 %fusion.8 = f32[32,8,16,128]{3,1,2,0:T(8,128)S(1)} fusion(f32[32,8,16,128]{3,1,2,0:T(8,128)S(1)} %slice.100, f32[32,8,18,130]{3,1,2,0:T(8,128)S(1)} %fusion.3, f32[8,16,128]{2,0,1:T(8,128)S(1)} %copy.28), kind=kLoop, calls=%fused_computation.23 | loop fusion | flops 3670016 | bytes 12648448 | tf_op jit(solution)/shard_map/sub | solution.py:33
  56.3 1.3 copy-done.2
  57.6 2.8 %fusion.15 = f32[32,32]{1,0:T(8,128)S(1)} fusion(f32[32,8,16,128]{3,1,2,0:T(8,128)S(1)} %fusion.8), kind=kOutput, calls=%fused_computation.34 | convolution fusion | flops 201326592 | bytes 2101248 | tf_op jit(solution)/shard_map/czxy,dzxy->cd/dot_general | solution.py:55
  60.6 21.5 %all_to_all.20 = f32[16,1,1024]{2,1,0:T(1,128)S(1)} all-to-all(f32[16,1,1024]{2,1,0:T(1,128)S(1)} %reshape.28), channel_id=1, replica_groups=mesh['gx'=32,'gy'=16] {'gy'}, dimensions={0} | all-to-all | bytes 131072 | tf_op jit(solution)/shard_map/all_to_all | solution.py:50
  82.2 0.6 broadcast.73
  82.8 0.8 reduce.4
  83.8 0.3 reshape.30
  84.1 20.4 %all_to_all.21 = f32[32,1,1024]{2,1,0:T(1,128)S(1)} all-to-all(f32[32,1,1024]{2,1,0:T(1,128)S(1)} %reshape.30), channel_id=1, replica_groups=mesh['gx'=32,'gy'=16] {'gx'}, dimensions={0} | all-to-all | bytes 262144 | tf_op jit(solution)/shard_map/all_to_all | solution.py:50
  104.5 1.0 reduce.5
  105.8 2.9 %cholesky.44 = f32[32,32]{1,0:T(8,128)S(1)} custom-call(f32[32,32]{1,0:T(8,128)S(1)} %fusion.28), custom_call_target="Cholesky" | custom-call | tf_op jit(solution)/shard_map/jit(cholesky)/cholesky | solution.py:59
  108.8 0.6 compare_reduce_fusion.1
  109.4 0.6 fusion.23
  110.0 2.4 %custom-call.6 = f32[1,32,32]{1,2,0:T(8,128)S(1)} custom-call(f32[1,32,32]{2,1,0:T(8,128)S(1)} %fusion.23), custom_call_target="InvertDiagBlocksLowerTriangular" | custom-call | tf_op jit(solution)/shard_map/triangular_solve/custom-call.0 | solution.py:61
  112.4 0.2 convolution_bitcast_fusion.1
  112.6 4.5 %fusion.11 = f32[32,8,16,128]{3,0,2,1:T(8,128)S(1)} fusion(f32[32,32,1,1]{1,0,3,2:T(8,128)S(1)} %convolution_bitcast_fusion.1, f32[32,8,16,128]{3,1,2,0:T(8,128)} %copy-done.2), kind=kOutput, calls=%fused_computation.29 | convolution fusion | flops 201326592 | bytes 4198400 | tf_op jit(solution)/shard_map/cd,dzxy->czxy/dot_general | solution.py:73
  117.2 1.8 %fusion.18 = f32[32,32]{1,0:T(8,128)S(1)} fusion(f32[32,8,16,128]{3,0,2,1:T(8,128)S(1)} %fusion.11), kind=kOutput, calls=%fused_computation.35 | convolution fusion | flops 201326592 | bytes 2101248 | tf_op jit(solution)/shard_map/czxy,dzxy->cd/dot_general | solution.py:55
  119.2 10.4 %all_to_all.22 = f32[16,1,1024]{2,1,0:T(1,128)S(1)} all-to-all(f32[16,1,1024]{2,1,0:T(1,128)S(1)} %reshape.32), channel_id=1, replica_groups=mesh['gx'=32,'gy'=16] {'gy'}, dimensions={0} | all-to-all | bytes 131072 | tf_op jit(solution)/shard_map/all_to_all | solution.py:50
  129.5 0.8 reduce.6
  130.6 0.3 reshape.34
  130.9 14.3 %all_to_all.23 = f32[32,1,1024]{2,1,0:T(1,128)S(1)} all-to-all(f32[32,1,1024]{2,1,0:T(1,128)S(1)} %reshape.34), channel_id=1, replica_groups=mesh['gx'=32,'gy'=16] {'gx'}, dimensions={0} | all-to-all | bytes 262144 | tf_op jit(solution)/shard_map/all_to_all | solution.py:50
  145.2 1.0 reduce.7
  146.5 2.9 %cholesky.55 = f32[32,32]{1,0:T(8,128)S(1)} custom-call(f32[32,32]{1,0:T(8,128)S(1)} %fusion.26), custom_call_target="Cholesky" | custom-call | tf_op jit(solution)/shard_map/jit(cholesky)/cholesky | solution.py:59
  149.5 0.6 compare_reduce_fusion
  150.1 0.7 fusion.24
  150.8 2.4 %custom-call.7 = f32[1,32,32]{1,2,0:T(8,128)S(1)} custom-call(f32[1,32,32]{2,1,0:T(8,128)S(1)} %fusion.24), custom_call_target="InvertDiagBlocksLowerTriangular" | custom-call | tf_op jit(solution)/shard_map/triangular_solve/custom-call.0 | solution.py:61
  153.2 0.2 convolution_bitcast_fusion
  153.4 1.9 %convolution_multiply_fusion = f32[32,8,16,128]{3,0,2,1:T(8,128)S(1)} fusion(f32[32,32,1,1]{1,0,3,2:T(8,128)S(1)} %convolution_bitcast_fusion, f32[32,8,16,128]{3,0,2,1:T(8,128)S(1)} %fusion.11), kind=kOutput, calls=%fused_computation.33 | convolution fusion | flops 201850880 | bytes 4198400 | tf_op jit(solution)/shard_map/cd,dzxy->czxy/dot_general | solution.py:76
  155.4 2.5 %copy.44 = f32[32,8,16,128]{3,2,1,0:T(8,128)} copy(f32[32,8,16,128]{3,0,2,1:T(8,128)S(1)} %convolution_multiply_fusion) | data formatting | bytes 4194304 | tf_op jit(solution)/shard_map/mul | solution.py:77
  (35 shorter events, 1.8 us)
Async XLA Ops:
  0.0 2.5 %copy-start.3 = (f32[8,16,128]{2,1,0:T(8,128)S(1)}, f32[8,16,128]{2,1,0:T(8,128)}, u32[]{:S(2)}) copy-start(f32[8,16,128]{2,1,0:T(8,128)} %param.6) | copy-start | bytes 196612
  2.6 11.5 %collective-permute-start = (f32[33,8,2,128]{3,1,2,0:T(8,128)S(1)}, f32[33,8,2,128]{3,1,2,0:T(8,128)S(1)}, u32[]{:S(2)}, u32[]{:S(2)}) collective-permute-start(f32[33,8,2,128]{3,1,2,0:T(8,128)S(1)} %get-tuple-element.9), channel_id=1, source_target_pairs={{0,16},{16,32},{32,48},{48,64},{64,80},{80,96},{96,112},{112,128},... | collective-permute-start | bytes 811016 | tf_op jit(solution)/shard_map/ppermute | solution.py:15
  6.1 9.8 %collective-permute-start.1 = (f32[33,8,2,128]{3,1,2,0:T(8,128)S(1)}, f32[33,8,2,128]{3,1,2,0:T(8,128)S(1)}, u32[]{:S(2)}, u32[]{:S(2)}) collective-permute-start(f32[33,8,2,128]{3,1,2,0:T(8,128)S(1)} %get-tuple-element.10), channel_id=1, source_target_pairs={{16,0},{32,16},{48,32},{64,48},{80,64},{96,80},{112,96},{128,112},... | collective-permute-start | bytes 811016 | tf_op jit(solution)/shard_map/ppermute | solution.py:16
  22.8 6.0 %collective-permute-start.2 = (f32[33,8,20,2]{0,1,3,2:T(8,128)S(1)}, f32[33,8,20,2]{0,1,3,2:T(8,128)S(1)}, u32[]{:S(2)}, u32[]{:S(2)}) collective-permute-start(f32[33,8,20,2]{0,1,3,2:T(8,128)S(1)} %copy.31), channel_id=1, source_target_pairs={{0,1},{1,2},{2,3},{3,4},{4,5},{5,6},{6,7},{7,8},{8,9},{9,10},{10,1... | collective-permute-start | bytes 126728 | tf_op jit(solution)/shard_map/ppermute | solution.py:15
  27.4 5.9 %collective-permute-start.3 = (f32[33,8,20,2]{0,1,3,2:T(8,128)S(1)}, f32[33,8,20,2]{0,1,3,2:T(8,128)S(1)}, u32[]{:S(2)}, u32[]{:S(2)}) collective-permute-start(f32[33,8,20,2]{0,1,3,2:T(8,128)S(1)} %copy.32), channel_id=1, source_target_pairs={{1,0},{2,1},{3,2},{4,3},{5,4},{6,5},{7,6},{8,7},{9,8},{10,9},{11,1... | collective-permute-start | bytes 126728 | tf_op jit(solution)/shard_map/ppermute | solution.py:16
  44.1 1.8 %copy-start = (f32[33,8,20,2]{3,1,2,0:T(8,128)S(1)}, f32[33,8,20,2]{3,1,2,0:T(8,128)}, u32[]{:S(2)}) copy-start(f32[33,8,20,2]{3,1,2,0:T(8,128)} %copy.33) | copy-start | bytes 126724
  44.1 2.6 %copy-start.1 = (f32[33,8,20,2]{3,1,2,0:T(8,128)S(1)}, f32[33,8,20,2]{3,1,2,0:T(8,128)}, u32[]{:S(2)}) copy-start(f32[33,8,20,2]{3,1,2,0:T(8,128)} %copy.34) | copy-start | bytes 126724
  56.3 1.3 copy-start.2
